TPU v7x, 256 devices: a whole 4x4x8 slice. The times are simulated.
256 devices in a mesh: seq: 16 (over x, y), tp: 16 (over z, core).
Axes of the slice: x: 4, y: 4, z: 8, core: 2. Of those that a mesh axis runs over, the one named last changes fastest.
Arguments:
- query: bfloat16 [16384, 8192], P('seq', 'tp'), may hold values from -6 to 6
- key_in: bfloat16 [16384, 8192], P('seq', 'tp'), may hold values from -6 to 6
- value: bfloat16 [16384, 8192], P('seq', 'tp'), may hold values from -6 to 6
- gate: bfloat16 [16384, 8192], P('seq', 'tp'), may hold values from -8 to 8
- kv_start: float32 [64, 128, 128], P('tp'), may hold values from -240 to 240
- norm_gain: float32 [8192], P('tp'), may hold values from 0.5 to 2
- w_out: bfloat16 [8192, 6144], P('tp'), may hold values from -0.0625 to 0.0625
Outputs:
- mixed: bfloat16 [16384, 6144], P(('seq', 'tp'))
All inputs are finite; a program needn't handle non-finite values.
Results may differ from a plain program's by a relative error of at most 0.019.
Values may be sent and summed in bfloat16 or wider, within the bound.
No kernel may reach another device: no remote copies, remote signals or barrier semaphores. Data moves between devices by JAX's collectives and lax.ppermute only.
A program may use at most 128 MiB of HBM per device.

v0:
```python
import jax
import jax.numpy as jnp
from jax import lax
from jax.sharding import PartitionSpec as P

HD = 128


def per_device(query, key_in, value, gate, kv_start, norm_gain, w_out):
    rows = query.shape[0]
    heads = query.shape[1] // HD
    block = min(512, rows)
    count = rows // block
    highest = lax.Precision.HIGHEST
    qa = (
        jax.nn.silu(query.astype(jnp.float32)).astype(jnp.bfloat16).reshape(count, block, heads, HD)
    )
    ka = (
        jax.nn.silu(key_in.astype(jnp.float32))
        .astype(jnp.bfloat16)
        .reshape(count, block, heads, HD)
    )
    va = value.reshape(count, block, heads, HD)
    block_states = jnp.einsum("nthd,nthe->nhde", ka, va, preferred_element_type=jnp.float32)
    own_total = jnp.sum(block_states, axis=0)
    local_before = jnp.cumsum(block_states, axis=0) - block_states
    gathered = lax.all_gather(
        own_total[None].astype(jnp.bfloat16), "seq", axis=0, tiled=True
    ).astype(jnp.float32)
    position = lax.axis_index("seq")
    below = (jnp.arange(gathered.shape[0]) < position).astype(jnp.float32)
    prior = jnp.sum(gathered * below[:, None, None, None], axis=0)
    states = local_before + (kv_start + prior)[None]
    q_float = qa.astype(jnp.float32)
    inter = jnp.einsum("nthd,nhde->nthe", q_float, states, precision=highest)
    scores = jnp.einsum("nthd,nshd->nhts", qa, ka, preferred_element_type=jnp.float32)
    causal = jnp.arange(block)[:, None] >= jnp.arange(block)[None, :]
    scores = jnp.where(causal[None, None], scores, jnp.float32(0.0))
    intra = jnp.einsum("nhts,nshe->nthe", scores, va.astype(jnp.float32), precision=highest)
    heads_out = (inter + intra).reshape(rows, heads, HD)
    scale = lax.rsqrt(jnp.mean(heads_out * heads_out, axis=-1, keepdims=True) + 1e-05)
    normed = (heads_out * scale).reshape(rows, heads * HD)
    attn = (normed * norm_gain[None, :] * jax.nn.sigmoid(gate.astype(jnp.float32))).astype(
        jnp.bfloat16
    )
    return lax.psum_scatter(
        jnp.dot(attn, w_out, preferred_element_type=jnp.float32).astype(jnp.bfloat16),
        "tp",
        scatter_dimension=0,
        tiled=True,
    )


def solution(mesh):
    in_specs = (
        P("seq", "tp"),
        P("seq", "tp"),
        P("seq", "tp"),
        P("seq", "tp"),
        P("tp", None, None),
        P("tp"),
        P("tp", None),
    )
    out_specs = P(("seq", "tp"), None)
    return jax.shard_map(
        per_device, mesh=mesh, in_specs=in_specs, out_specs=out_specs, check_vma=False
    )
```

profile of v0, /device:TPU:2, one launch (start us, length us, event | category | flops | bytes accessed | tf_op | source)
XLA Modules:
  0.0 170.8 jit_solution(4474242960137433406)
XLA Ops:
  6.5 0.0 all-gather.3.cloned.1.call-start
  6.5 1.8 %fusion.8 = bf16[1024,512]{1,0:T(8,128)(2,1)S(1)} fusion(bf16[1024,512]{1,0:T(8,128)(2,1)} %param.8), kind=kLoop, calls=%fused_computation.14 | loop fusion | flops 3145728 | bytes 2097152 | tf_op jit(solution)/shard_map/convert_element_type | solution.py:20
  8.4 0.3 reshape.60
  8.7 1.3 reshape.61
  10.0 0.7 copy.33
  10.7 0.0 copy-start.3
  10.7 2.0 %fusion.28 = (bf16[4,128,128]{2,1,0:T(8,128)(2,1)}, f32[2,4,128,128]{3,2,1,0:T(8,128)}) fusion(bf16[2,512,4,128]{1,3,2,0:T(8,128)(2,1)S(1)} %copy.33, bf16[2,512,4,128]{3,2,1,0:T(4,128)(2,1)S(1)} %reshape.60), kind=kOutput, calls=%fused_computation.40 | convolution fusion | flops 134283264 | bytes 2752512 | tf_op jit(solution)/shard_map/nthd,nthe->nhde/dot_general | solution.py:24
  12.7 0.0 all-gather.3.cloned.1.call-update
  12.7 0.0 reduce-scatter.2.cloned.1.call-start
  12.7 0.0 copy-done.3
  12.7 1.6 fusion.12
  14.3 1.3 reshape.62
  15.7 0.1 iota_compare_fusion
  15.8 1.3 fusion.22
  17.0 6.7 %fusion = f32[2,4,512,128]{2,3,1,0:T(8,128)} fusion(bf16[2,512,4,128]{1,3,2,0:T(8,128)(2,1)S(1)} %copy.33, f32[2,4,512,512]{3,2,1,0:T(8,128)S(1)} %fusion.22, pred[512,512]{1,0:T(8,128)(4,1)S(1)} %iota_compare_fusion), kind=kOutput, calls=%fused_computation.1 | convolution fusion | flops 3223322624 | bytes 11796480 | tf_op jit(solution)/shard_map/nhts,nshe->nthe/dot_general | solution.py:39
  23.7 0.0 copy-start.4
  23.7 0.0 copy-start.1
  23.7 41.7 %all-gather.3.cloned.1.call-done = bf16[64,128,128]{2,1,0:T(8,128)(2,1)} async-done(((bf16[4,128,128]{2,1,0:T(8,128)(2,1)}), bf16[64,128,128]{2,1,0:T(8,128)(2,1)}) %all-gather.3.cloned.1.call-update) | async-done | bytes 2097168 | tf_op jit(solution)/shard_map/all_gather | solution.py:27
  65.4 2.2 %fusion.2 = f32[4,128,128]{2,1,0:T(8,128)S(1)} fusion(bf16[16,4,128,128]{3,2,1,0:T(8,128)(2,1)} %bitcast.27, f32[16]{0:T(128)S(1)} %compare_convert_fusion), kind=kLoop, calls=%fused_computation.4 | loop fusion | flops 3080192 | bytes 2359360 | tf_op jit(solution)/shard_map/reduce_sum | solution.py:32
  67.6 0.0 copy-done.4
  67.7 0.0 copy-done.1
  67.7 0.1 fusion.16
  67.9 0.0 copy-done
  67.9 1.3 multiply_reduce_fusion
  69.2 0.2 copy.35
  69.4 1.9 %copy.34 = f32[2,512,4,128]{3,2,1,0:T(4,128)} copy(f32[2,512,4,128]{1,3,2,0:T(8,128)S(1)} %get-tuple-element.8) | data formatting | bytes 4194304 | tf_op jit(solution)/shard_map/add | solution.py:40
  71.3 1.2 mul.46
  72.5 0.4 copy-done.2
  72.8 0.0 copy-done.5
  72.8 11.9 %convolution_convert_fusion = bf16[1024,6144]{1,0:T(8,128)(2,1)} fusion(bf16[512,6144]{1,0:T(8,128)(2,1)} %param.13, f32[128,8,4,128]{3,2,1,0:T(4,128)S(1)} %bitcast.28, f32[128,8,4,128]{3,2,1,0:T(4,128)S(1)} %bitcast.29, bf16[1024,512]{1,0:T(8,128)(2,1)} %param.10, f32[512]{0:T(512)S(1)} %copy-done.5), kind=kOutput, calls=%fused_computation | convolution fusion | flops 6452936704 | bytes 24119296 | tf_op jit(solution)/shard_map/dot_general | solution.py:47
  84.7 0.0 reduce-scatter.2.cloned.1.call-update
  84.8 79.2 %reduce-scatter.2.cloned.1.call-done = bf16[64,6144]{1,0:T(8,128)(2,1)} async-done(((bf16[1024,6144]{1,0:T(8,128)(2,1)}), bf16[64,6144]{1,0:T(8,128)(2,1)}) %reduce-scatter.2.cloned.1.call-update) | async-done | bytes 786448 | tf_op jit(solution)/shard_map/reduce_scatter | solution.py:46
  (6 shorter events, 0.1 us)
Async XLA Ops:
  6.5 58.8 %all-gather.3.cloned.1.call-start = ((), (), s32[]{:S(2)}) async-start(), calls=%async_computation.2 | async-start | bytes 2228224 | tf_op jit(solution)/shard_map/all_gather | solution.py:27
  10.7 2.1 %copy-start.3 = (bf16[1024,512]{1,0:T(8,128)(2,1)S(1)}, bf16[1024,512]{1,0:T(8,128)(2,1)}, u32[]{:S(2)}) copy-start(bf16[1024,512]{1,0:T(8,128)(2,1)} %param.7) | copy-start | bytes 3145732
  12.7 151.3 %reduce-scatter.2.cloned.1.call-start = ((), (), s32[]{:S(2)}) async-start(), calls=%async_computation.1 | async-start | bytes 13369344 | tf_op jit(solution)/shard_map/reduce_scatter | solution.py:46
  23.7 43.9 %copy-start.4 = (f32[4,128,128]{2,1,0:T(8,128)S(1)}, f32[4,128,128]{2,1,0:T(8,128)}, u32[]{:S(2)}) copy-start(f32[4,128,128]{2,1,0:T(8,128)} %param.11) | copy-start | bytes 786436
  23.7 44.0 %copy-start.1 = (f32[2,4,128,128]{3,2,1,0:T(8,128)S(1)}, f32[2,4,128,128]{3,2,1,0:T(8,128)}, u32[]{:S(2)}) copy-start(f32[2,4,128,128]{3,2,1,0:T(8,128)} %get-tuple-element.6) | copy-start | bytes 1572868
  65.4 2.5 %copy-start = (f32[2,4,512,128]{2,3,1,0:T(8,128)S(1)}, f32[2,4,512,128]{2,3,1,0:T(8,128)}, u32[]{:S(2)}) copy-start(f32[2,4,512,128]{2,3,1,0:T(8,128)} %fusion) | copy-start | bytes 6291460
  71.3 1.6 copy-start.2
  71.3 1.6 copy-start.5
Sparse Core Ops, SparseCore 0:
  12.8 52.5 all-gather.2
  84.9 79.0 reduce-scatter.1
where the time goes:
time: 171 us
  waiting for transfers between devices  121 us (71%)
  matrix products  23 us (13%)
  between operations  13.6 us (8%)
  local copies, waits for them, and re-layouts  7.34 us (4%)
  other arithmetic  5.92 us (3%)
    reduce_scatter x1, waiting for transfers between devices, per_device(): lax.psum_scatter(jnp.dot(attn, w_out, preferred_element_type=jnp.float32)...  79.2 us
    all_gather x1, waiting for transfers between devices, per_device(): lax.all_gather(own_total[None].astype(jnp.bfloat16), 'seq', axis=0, tiled...  41.7 us
    dot_general x1, matrix products, per_device(): jnp.dot(attn, w_out, preferred_element_type=jnp.float32)  11.9 us
    dot_general x1, matrix products, per_device(): jnp.einsum('nhts,nshe->nthe', scores, va.astype(jnp.float32), precision=h...  6.66 us
  transfers between devices with their start and end apart: 2, of which 2 were waited for; matrix products, arithmetic and copies ran while one was open for 6% of the time, Pallas kernels for 0%

commit v1 on v0

--- a/solution.py
+++ b/solution.py
@@ -4,6 +4,34 @@
 from jax.sharding import PartitionSpec as P
 
 HD = 128
+
+
+def row_length(n):
+    best = 1
+    for r in range(1, n + 1):
+        if n % r == 0 and r * r <= n:
+            best = r
+    return best
+
+
+def exclusive_prefix(total):
+    n = lax.axis_size("seq")
+    r = row_length(n)
+    rows = n // r
+    index = lax.axis_index("seq")
+    along = index % r
+    sent = total.astype(jnp.bfloat16)
+    row_total = sent.astype(jnp.float32)
+    before = jnp.zeros_like(row_total)
+    for k in range(1, r):
+        perm = [(a * r + b, a * r + (b + k) % r) for a in range(rows) for b in range(r)]
+        got = lax.ppermute(sent, "seq", perm).astype(jnp.float32)
+        row_total = row_total + got
+        before = before + jnp.where(k <= along, got, jnp.float32(0.0))
+    for k in range(1, rows):
+        perm = [(a * r + b, (a + k) * r + b) for a in range(rows - k) for b in range(r)]
+        before = before + lax.ppermute(row_total, "seq", perm)
+    return before
 
 
 def per_device(query, key_in, value, gate, kv_start, norm_gain, w_out):
@@ -24,12 +52,7 @@
     block_states = jnp.einsum("nthd,nthe->nhde", ka, va, preferred_element_type=jnp.float32)
     own_total = jnp.sum(block_states, axis=0)
     local_before = jnp.cumsum(block_states, axis=0) - block_states
-    gathered = lax.all_gather(
-        own_total[None].astype(jnp.bfloat16), "seq", axis=0, tiled=True
-    ).astype(jnp.float32)
-    position = lax.axis_index("seq")
-    below = (jnp.arange(gathered.shape[0]) < position).astype(jnp.float32)
-    prior = jnp.sum(gathered * below[:, None, None, None], axis=0)
+    prior = exclusive_prefix(own_total)
     states = local_before + (kv_start + prior)[None]
     q_float = qa.astype(jnp.float32)
     inter = jnp.einsum("nthd,nhde->nthe", q_float, states, precision=highest)

time: 171 us -> 150 us (0.88)
  waiting for transfers between devices: 121 us -> 87.4 us
  starting transfers between devices: 0.04 us -> 12.9 us
    all_gather x1 -> x0, waiting for transfers between devices: 41.7 us -> none  [per_device(): lax.all_gather(own_total[None].astype(jnp.bfloat16), 'seq', axis=0, tiled...]
    ppermute x0 -> x6, starting transfers between devices: none -> 12.9 us  [the longest x3 8.25 us: exclusive_prefix(): before = before + lax.ppermute(row_total, 'seq', perm)]
    ppermute x0 -> x6, waiting for transfers between devices: none -> 7.61 us  [the longest x3 3.99 us: exclusive_prefix(): before = before + lax.ppermute(row_total, 'seq', perm)]
    reduce_sum x1 -> x0, other arithmetic: 2.24 us -> none  [per_device(): prior = jnp.sum(gathered * below[:, None, None, None], axis=0)]
  transfers between devices with their start and end apart: 2 -> 7, of which waited for: 2 -> 4; matrix products, arithmetic and copies ran while one was open for 6% -> 7% of each run, Pallas kernels for 0% -> 0%
where the time goes in v1:
time: 150 us
  waiting for transfers between devices  87.4 us (58%)
  matrix products  23.1 us (15%)
  between operations  13.5 us (9%)
  starting transfers between devices  12.9 us (9%)
  local copies, waits for them, and re-layouts  7.31 us (5%)
  other arithmetic  5.96 us (4%)
    reduce_scatter x1, waiting for transfers between devices, per_device(): lax.psum_scatter(jnp.dot(attn, w_out, preferred_element_type=jnp.float32)...  79.7 us
    dot_general x1, matrix products, per_device(): jnp.dot(attn, w_out, preferred_element_type=jnp.float32)  11.9 us
    ppermute x3, starting transfers between devices, exclusive_prefix(): before = before + lax.ppermute(row_total, 'seq', perm)  8.25 us
    dot_general x1, matrix products, per_device(): jnp.einsum('nhts,nshe->nthe', scores, va.astype(jnp.float32), precision=h...  6.7 us
    ppermute x3, starting transfers between devices, exclusive_prefix(): got = lax.ppermute(sent, 'seq', perm).astype(jnp.float32)  4.61 us
    ppermute x3, waiting for transfers between devices, exclusive_prefix(): before = before + lax.ppermute(row_total, 'seq', perm)  3.99 us
    ppermute x3, waiting for transfers between devices, exclusive_prefix(): got = lax.ppermute(sent, 'seq', perm).astype(jnp.float32)  3.62 us
  transfers between devices with their start and end apart: 7, of which 4 were waited for; matrix products, arithmetic and copies ran while one was open for 7% of the time, Pallas kernels for 0%

profile of v1, /device:TPU:2, one launch (start us, length us, event | category | flops | bytes accessed | tf_op | source)
XLA Modules:
  0.0 150.2 jit_solution(3759585568765902919)
XLA Ops:
  6.5 1.8 %fusion.7 = bf16[1024,512]{1,0:T(8,128)(2,1)S(1)} fusion(bf16[1024,512]{1,0:T(8,128)(2,1)} %param.8), kind=kLoop, calls=%fused_computation.12 | loop fusion | flops 3145728 | bytes 2097152 | tf_op jit(solution)/shard_map/convert_element_type | solution.py:48
  8.4 0.3 reshape.46
  8.7 1.3 reshape.47
  10.0 0.7 copy.33
  10.7 2.0 %fusion.34 = (bf16[4,128,128]{2,1,0:T(8,128)(2,1)}, f32[2,4,128,128]{3,2,1,0:T(8,128)}) fusion(bf16[2,512,4,128]{1,3,2,0:T(8,128)(2,1)S(1)} %copy.33, bf16[2,512,4,128]{3,2,1,0:T(4,128)(2,1)S(1)} %reshape.46), kind=kOutput, calls=%fused_computation.50 | convolution fusion | flops 134283264 | bytes 2752512 | tf_op jit(solution)/shard_map/nthd,nthe->nhde/dot_general | solution.py:52
  12.7 3.0 %collective-permute-start.2 = (bf16[4,128,128]{2,1,0:T(8,128)(2,1)}, bf16[4,128,128]{2,1,0:T(8,128)(2,1)S(1)}, u32[]{:S(2)}, u32[]{:S(2)}) collective-permute-start(bf16[4,128,128]{2,1,0:T(8,128)(2,1)} %get-tuple-element.5), channel_id=1, source_target_pairs={{0,48},{16,0},{32,16},{48,32},{64,112},{80,64},{96,80},{112,96},{1... | collective-permute-start | bytes 393224 | tf_op jit(solution)/shard_map/ppermute | solution.py:28
  15.7 0.6 collective-permute-start.1
  16.3 1.0 collective-permute-start
  17.3 1.6 %fusion.11 = bf16[1024,512]{1,0:T(8,128)(2,1)} fusion(bf16[1024,512]{1,0:T(8,128)(2,1)S(1)} %copy-done.3), kind=kLoop, calls=%fused_computation.16 | loop fusion | flops 3145728 | bytes 2097152 | tf_op jit(solution)/shard_map/convert_element_type | solution.py:44
  18.9 1.3 reshape.48
  20.2 1.3 fusion.20
  21.5 0.1 iota_compare_fusion
  21.5 0.0 collective-permute-done.2
  21.6 2.2 %collective-permute-done.1 = bf16[4,128,128]{2,1,0:T(8,128)(2,1)S(1)} collective-permute-done((bf16[4,128,128]{2,1,0:T(8,128)(2,1)}, bf16[4,128,128]{2,1,0:T(8,128)(2,1)S(1)}, u32[]{:S(2)}, u32[]{:S(2)}) %collective-permute-start.1) | collective-permute-done | bytes 131104 | tf_op jit(solution)/shard_map/ppermute | solution.py:28
  23.8 1.4 collective-permute-done
  25.2 1.0 convert_add_fusion
  26.1 0.0 copy-start.1
  26.1 1.5 %collective-permute-start.5 = (f32[4,128,128]{2,1,0:T(8,128)S(1)}, f32[4,128,128]{2,1,0:T(8,128)}, u32[]{:S(2)}, u32[]{:S(2)}) collective-permute-start(f32[4,128,128]{2,1,0:T(8,128)S(1)} %convert_add_fusion), channel_id=1, source_target_pairs={{0,192},{16,208},{32,224},{48,240},{1,193},{17,209},{33,225},{49,2... | collective-permute-start | bytes 786440 | tf_op jit(solution)/shard_map/ppermute | solution.py:33
  27.7 4.7 %collective-permute-start.4 = (f32[4,128,128]{2,1,0:T(8,128)S(1)}, f32[4,128,128]{2,1,0:T(8,128)}, u32[]{:S(2)}, u32[]{:S(2)}) collective-permute-start(f32[4,128,128]{2,1,0:T(8,128)S(1)} %convert_add_fusion), channel_id=1, source_target_pairs={{0,128},{16,144},{32,160},{48,176},{64,192},{80,208},{96,224},{112... | collective-permute-start | bytes 786440 | tf_op jit(solution)/shard_map/ppermute | solution.py:33
  32.3 2.1 %collective-permute-start.3 = (f32[4,128,128]{2,1,0:T(8,128)S(1)}, f32[4,128,128]{2,1,0:T(8,128)}, u32[]{:S(2)}, u32[]{:S(2)}) collective-permute-start(f32[4,128,128]{2,1,0:T(8,128)S(1)} %convert_add_fusion), channel_id=1, source_target_pairs={{0,64},{16,80},{32,96},{48,112},{64,128},{80,144},{96,160},{112,17... | collective-permute-start | bytes 786440 | tf_op jit(solution)/shard_map/ppermute | solution.py:33
  34.4 6.7 %fusion = f32[2,4,512,128]{2,3,1,0:T(8,128)} fusion(bf16[2,512,4,128]{1,3,2,0:T(8,128)(2,1)S(1)} %copy.33, f32[2,4,512,512]{3,2,1,0:T(8,128)S(1)} %fusion.20, pred[512,512]{1,0:T(8,128)(4,1)S(1)} %iota_compare_fusion), kind=kOutput, calls=%fused_computation.1 | convolution fusion | flops 3223322624 | bytes 11796480 | tf_op jit(solution)/shard_map/nhts,nshe->nthe/dot_general | solution.py:62
  41.1 0.2 reduce-window_subtract_fusion
  41.4 4.0 %collective-permute-done.3 = f32[4,128,128]{2,1,0:T(8,128)} collective-permute-done((f32[4,128,128]{2,1,0:T(8,128)S(1)}, f32[4,128,128]{2,1,0:T(8,128)}, u32[]{:S(2)}, u32[]{:S(2)}) %collective-permute-start.3) | collective-permute-done | bytes 262176 | tf_op jit(solution)/shard_map/ppermute | solution.py:33
  45.3 1.3 fusion.30
  46.7 1.3 multiply_reduce_fusion
  47.9 0.2 copy.35
  48.2 1.8 %copy.34 = f32[2,512,4,128]{3,2,1,0:T(4,128)} copy(f32[2,512,4,128]{1,3,2,0:T(8,128)S(1)} %get-tuple-element.8) | data formatting | bytes 4194304 | tf_op jit(solution)/shard_map/add | solution.py:63
  50.0 1.2 mul.36
  51.3 0.4 copy-done.2
  51.6 11.9 %convolution_convert_fusion = bf16[1024,6144]{1,0:T(8,128)(2,1)} fusion(bf16[512,6144]{1,0:T(8,128)(2,1)} %param.13, f32[128,8,4,128]{3,2,1,0:T(4,128)S(1)} %bitcast.24, f32[128,8,4,128]{3,2,1,0:T(4,128)S(1)} %bitcast.25, bf16[1024,512]{1,0:T(8,128)(2,1)} %param.10, f32[512]{0:T(512)S(1)} %copy-done.4), kind=kOutput, calls=%fused_computation | convolution fusion | flops 6452936704 | bytes 24119296 | tf_op jit(solution)/shard_map/dot_general | solution.py:70
  63.6 0.0 reduce-scatter.2.cloned.1.call-update
  63.6 79.7 %reduce-scatter.2.cloned.1.call-done = bf16[64,6144]{1,0:T(8,128)(2,1)} async-done(((bf16[1024,6144]{1,0:T(8,128)(2,1)}), bf16[64,6144]{1,0:T(8,128)(2,1)}) %reduce-scatter.2.cloned.1.call-update) | async-done | bytes 786448 | tf_op jit(solution)/shard_map/reduce_scatter | solution.py:69
  (12 shorter events, 0.0 us)
Async XLA Ops:
  6.5 136.8 %reduce-scatter.2.cloned.1.call-start = ((), (), s32[]{:S(2)}) async-start(), calls=%async_computation.1 | async-start | bytes 13369344 | tf_op jit(solution)/shard_map/reduce_scatter | solution.py:69
  10.7 6.6 %copy-start.3 = (bf16[1024,512]{1,0:T(8,128)(2,1)S(1)}, bf16[1024,512]{1,0:T(8,128)(2,1)}, u32[]{:S(2)}) copy-start(bf16[1024,512]{1,0:T(8,128)(2,1)} %param.7) | copy-start | bytes 3145732
  12.7 8.9 %collective-permute-start.2 = (bf16[4,128,128]{2,1,0:T(8,128)(2,1)}, bf16[4,128,128]{2,1,0:T(8,128)(2,1)S(1)}, u32[]{:S(2)}, u32[]{:S(2)}) collective-permute-start(bf16[4,128,128]{2,1,0:T(8,128)(2,1)} %get-tuple-element.5), channel_id=1, source_target_pairs={{0,48},{16,0},{32,16},{48,32},{64,112},{80,64},{96,80},{112,96},{1... | collective-permute-start | bytes 393224 | tf_op jit(solution)/shard_map/ppermute | solution.py:28
  15.7 8.1 %collective-permute-start.1 = (bf16[4,128,128]{2,1,0:T(8,128)(2,1)}, bf16[4,128,128]{2,1,0:T(8,128)(2,1)S(1)}, u32[]{:S(2)}, u32[]{:S(2)}) collective-permute-start(bf16[4,128,128]{2,1,0:T(8,128)(2,1)} %get-tuple-element.5), channel_id=1, source_target_pairs={{0,32},{16,48},{32,0},{48,16},{64,96},{80,112},{96,64},{112,80},{1... | collective-permute-start | bytes 393224 | tf_op jit(solution)/shard_map/ppermute | solution.py:28
  16.3 8.8 %collective-permute-start = (bf16[4,128,128]{2,1,0:T(8,128)(2,1)}, bf16[4,128,128]{2,1,0:T(8,128)(2,1)S(1)}, u32[]{:S(2)}, u32[]{:S(2)}) collective-permute-start(bf16[4,128,128]{2,1,0:T(8,128)(2,1)} %get-tuple-element.5), channel_id=1, source_target_pairs={{0,16},{16,32},{32,48},{48,0},{64,80},{80,96},{96,112},{112,64},{1... | collective-permute-start | bytes 393224 | tf_op jit(solution)/shard_map/ppermute | solution.py:28
  26.1 15.0 %copy-start.1 = (f32[2,4,128,128]{3,2,1,0:T(8,128)S(1)}, f32[2,4,128,128]{3,2,1,0:T(8,128)}, u32[]{:S(2)}) copy-start(f32[2,4,128,128]{3,2,1,0:T(8,128)} %get-tuple-element.6) | copy-start | bytes 1572868
  26.1 15.2 %collective-permute-start.5 = (f32[4,128,128]{2,1,0:T(8,128)S(1)}, f32[4,128,128]{2,1,0:T(8,128)}, u32[]{:S(2)}, u32[]{:S(2)}) collective-permute-start(f32[4,128,128]{2,1,0:T(8,128)S(1)} %convert_add_fusion), channel_id=1, source_target_pairs={{0,192},{16,208},{32,224},{48,240},{1,193},{17,209},{33,225},{49,2... | collective-permute-start | bytes 786440 | tf_op jit(solution)/shard_map/ppermute | solution.py:33
  27.7 13.7 %collective-permute-start.4 = (f32[4,128,128]{2,1,0:T(8,128)S(1)}, f32[4,128,128]{2,1,0:T(8,128)}, u32[]{:S(2)}, u32[]{:S(2)}) collective-permute-start(f32[4,128,128]{2,1,0:T(8,128)S(1)} %convert_add_fusion), channel_id=1, source_target_pairs={{0,128},{16,144},{32,160},{48,176},{64,192},{80,208},{96,224},{112... | collective-permute-start | bytes 786440 | tf_op jit(solution)/shard_map/ppermute | solution.py:33
  32.3 13.0 %collective-permute-start.3 = (f32[4,128,128]{2,1,0:T(8,128)S(1)}, f32[4,128,128]{2,1,0:T(8,128)}, u32[]{:S(2)}, u32[]{:S(2)}) collective-permute-start(f32[4,128,128]{2,1,0:T(8,128)S(1)} %convert_add_fusion), channel_id=1, source_target_pairs={{0,64},{16,80},{32,96},{48,112},{64,128},{80,144},{96,160},{112,17... | collective-permute-start | bytes 786440 | tf_op jit(solution)/shard_map/ppermute | solution.py:33
  41.1 5.5 %copy-start = (f32[2,4,512,128]{2,3,1,0:T(8,128)S(1)}, f32[2,4,512,128]{2,3,1,0:T(8,128)}, u32[]{:S(2)}) copy-start(f32[2,4,512,128]{2,3,1,0:T(8,128)} %fusion) | copy-start | bytes 6291460
  50.0 1.6 %copy-start.2 = (f32[2,512,4,128]{3,2,1,0:T(4,128)S(1)}, f32[2,512,4,128]{3,2,1,0:T(4,128)}, u32[]{:S(2)}) copy-start(f32[2,512,4,128]{3,2,1,0:T(4,128)} %copy.34) | copy-start | bytes 6291460
  50.0 1.6 %copy-start.4 = (f32[512]{0:T(512)S(1)}, f32[512]{0:T(512)}, u32[]{:S(2)}) copy-start(f32[512]{0:T(512)} %param.12) | copy-start | bytes 6148
Sparse Core Ops, SparseCore 0:
  63.7 79.5 reduce-scatter.1

commit v2 on v1

--- a/solution.py
+++ b/solution.py
@@ -4,6 +4,7 @@
 from jax.sharding import PartitionSpec as P
 
 HD = 128
+CHUNKS = 4
 
 
 def row_length(n):
@@ -61,17 +62,23 @@
     scores = jnp.where(causal[None, None], scores, jnp.float32(0.0))
     intra = jnp.einsum("nhts,nshe->nthe", scores, va.astype(jnp.float32), precision=highest)
     heads_out = (inter + intra).reshape(rows, heads, HD)
-    scale = lax.rsqrt(jnp.mean(heads_out * heads_out, axis=-1, keepdims=True) + 1e-05)
-    normed = (heads_out * scale).reshape(rows, heads * HD)
-    attn = (normed * norm_gain[None, :] * jax.nn.sigmoid(gate.astype(jnp.float32))).astype(
-        jnp.bfloat16
-    )
-    return lax.psum_scatter(
-        jnp.dot(attn, w_out, preferred_element_type=jnp.float32).astype(jnp.bfloat16),
-        "tp",
-        scatter_dimension=0,
-        tiled=True,
-    )
+    n_tp = lax.axis_size("tp")
+    chunks = CHUNKS
+    per = rows // n_tp // chunks
+    split_heads = heads_out.reshape(n_tp, chunks, per, heads, HD)
+    split_gate = gate.reshape(n_tp, chunks, per, heads * HD)
+    pieces = []
+    for c in range(chunks):
+        part_out = split_heads[:, c].reshape(n_tp * per, heads, HD)
+        scale = lax.rsqrt(jnp.mean(part_out * part_out, axis=-1, keepdims=True) + 1e-05)
+        normed = (part_out * scale).reshape(n_tp * per, heads * HD)
+        gate_c = split_gate[:, c].reshape(n_tp * per, heads * HD)
+        attn = (normed * norm_gain[None, :] * jax.nn.sigmoid(gate_c.astype(jnp.float32))).astype(
+            jnp.bfloat16
+        )
+        partial = jnp.dot(attn, w_out, preferred_element_type=jnp.float32).astype(jnp.bfloat16)
+        pieces.append(lax.psum_scatter(partial, "tp", scatter_dimension=0, tiled=True))
+    return jnp.concatenate(pieces, axis=0)
 
 
 def solution(mesh):

time: 150 us -> 326 us (2.17)
  waiting for transfers between devices: 87.4 us -> 240 us
  matrix products: 23.1 us -> 37.8 us
  other arithmetic: 5.96 us -> 12.8 us
    reduce_scatter x1 -> x4, waiting for transfers between devices: 79.7 us -> 238 us  [per_device(): lax.psum_scatter(partial, 'tp', scatter_dimension=0, tiled=True)]
    dot_general x1 -> x4, matrix products: 11.9 us -> 25.1 us  [per_device(): jnp.dot(attn, w_out, preferred_element_type=jnp.float32)]
    ppermute x3, waiting for transfers between devices: 3.62 us -> 0.01 us  [exclusive_prefix(): got = lax.ppermute(sent, 'seq', perm).astype(jnp.float32)]
  transfers between devices with their start and end apart: 7 -> 10, of which waited for: 4 -> 5; matrix products, arithmetic and copies ran while one was open for 7% -> 10% of each run, Pallas kernels for 0% -> 0%
where the time goes in v2:
time: 326 us; the launch traced here: 325 us
  waiting for transfers between devices  240 us (74%)
  matrix products  37.8 us (12%)
  between operations  13.4 us (4%)
  other arithmetic  12.8 us (4%)
  starting transfers between devices  12.2 us (4%)
  local copies, waits for them, and re-layouts  8.34 us (3%)
    reduce_scatter x4, waiting for transfers between devices, per_device(): lax.psum_scatter(partial, 'tp', scatter_dimension=0, tiled=True)  238 us
    dot_general x4, matrix products, per_device(): jnp.dot(attn, w_out, preferred_element_type=jnp.float32)  25.1 us
    dot_general x1, matrix products, per_device(): jnp.einsum('nhts,nshe->nthe', scores, va.astype(jnp.float32), precision=h...  6.78 us
  transfers between devices with their start and end apart: 10, of which 5 were waited for; matrix products, arithmetic and copies ran while one was open for 10% of the time, Pallas kernels for 0%

profile of v2, /device:TPU:2, one launch (start us, length us, event | category | flops | bytes accessed | tf_op | source)
XLA Modules:
  0.0 324.9 jit_solution(9999708821236229770)
XLA Ops:
  6.5 1.8 fusion.7
  8.7 1.4 reshape.135
  10.1 2.0 fusion.41
  12.1 1.6 collective-permute-start
  13.7 2.9 collective-permute-start.1
  16.6 1.3 collective-permute-start.2
  18.0 1.6 fusion.11
  19.6 1.3 reshape.136
  20.9 1.3 fusion.14
  22.2 6.8 %fusion = f32[2,4,512,128]{2,3,1,0:T(8,128)} fusion(f32[2,4,512,512]{3,2,1,0:T(8,128)S(1)} %fusion.14, pred[512,512]{1,0:T(8,128)(4,1)S(1)} %iota_compare_fusion, bf16[2,512,4,128]{3,2,1,0:T(4,128)(2,1)S(1)} %reshape.135), kind=kOutput, calls=%fused_computation | convolution fusion | flops 3223322624 | bytes 11796480 | tf_op jit(solution)/shard_map/nhts,nshe->nthe/dot_general | solution.py:63
  29.0 1.2 convert_add_fusion
  30.2 3.4 %collective-permute-start.3 = (f32[4,128,128]{2,1,0:T(8,128)S(1)}, f32[4,128,128]{2,1,0:T(8,128)S(1)}, u32[]{:S(2)}, u32[]{:S(2)}) collective-permute-start(f32[4,128,128]{2,1,0:T(8,128)S(1)} %convert_add_fusion), channel_id=1, source_target_pairs={{0,64},{16,80},{32,96},{48,112},{64,128},{80,144},{96,160},{112,17... | collective-permute-start | bytes 786440 | tf_op jit(solution)/shard_map/ppermute | solution.py:34
  33.6 1.9 collective-permute-start.4
  35.5 0.9 collective-permute-start.5
  36.4 1.7 add_divide_fusion.3
  38.4 2.2 collective-permute-done.3
  40.5 1.1 fusion.38
  41.6 2.7 bitcast_add_fusion
  44.3 1.9 copy.46
  46.1 2.2 multiply_reduce_fusion.3
  49.4 0.3 copy.50
  49.8 0.3 copy.53
  51.9 0.8 fusion.31
  52.7 6.3 %convolution_convert_fusion = bf16[256,6144]{1,0:T(8,128)(2,1)} fusion(bf16[256,512]{1,0:T(8,128)(2,1)S(1)} %get-tuple-element.20, bf16[512,6144]{1,0:T(8,128)(2,1)} %param.13), kind=kOutput, calls=%fused_computation.2 | convolution fusion | flops 1612185600 | bytes 9699328 | tf_op jit(solution)/shard_map/dot_general | solution.py:79
  59.1 6.3 %convolution_convert_fusion.3 = bf16[256,6144]{1,0:T(8,128)(2,1)} fusion(bf16[256,512]{1,0:T(8,128)(2,1)S(1)} %get-tuple-element.17, bf16[512,6144]{1,0:T(8,128)(2,1)} %param.13), kind=kOutput, calls=%fused_computation.5 | convolution fusion | flops 1612185600 | bytes 9699328 | tf_op jit(solution)/shard_map/dot_general | solution.py:79
  65.4 6.3 %convolution_convert_fusion.2 = bf16[256,6144]{1,0:T(8,128)(2,1)} fusion(bf16[256,512]{1,0:T(8,128)(2,1)S(1)} %get-tuple-element.18, bf16[512,6144]{1,0:T(8,128)(2,1)} %param.13), kind=kOutput, calls=%fused_computation.4 | convolution fusion | flops 1612185600 | bytes 9699328 | tf_op jit(solution)/shard_map/dot_general | solution.py:79
  71.8 6.2 %convolution_convert_fusion.1 = bf16[256,6144]{1,0:T(8,128)(2,1)} fusion(bf16[256,512]{1,0:T(8,128)(2,1)S(1)} %get-tuple-element.19, bf16[512,6144]{1,0:T(8,128)(2,1)} %param.13), kind=kOutput, calls=%fused_computation.3 | convolution fusion | flops 1612185600 | bytes 9699328 | tf_op jit(solution)/shard_map/dot_general | solution.py:79
  78.0 50.1 %reduce-scatter.11.cloned.1.call-done = bf16[16,6144]{1,0:T(8,128)(2,1)} async-done(((bf16[256,6144]{1,0:T(8,128)(2,1)}), bf16[16,6144]{1,0:T(8,128)(2,1)}) %reduce-scatter.11.cloned.1.call-update) | async-done | bytes 196624 | tf_op jit(solution)/shard_map/reduce_scatter | solution.py:80
  128.2 62.7 %reduce-scatter.5.cloned.1.call-done = bf16[16,6144]{1,0:T(8,128)(2,1)} async-done(((bf16[256,6144]{1,0:T(8,128)(2,1)}), bf16[16,6144]{1,0:T(8,128)(2,1)}) %reduce-scatter.5.cloned.1.call-update) | async-done | bytes 196624 | tf_op jit(solution)/shard_map/reduce_scatter | solution.py:80
  190.9 62.7 %reduce-scatter.7.cloned.1.call-done = bf16[16,6144]{1,0:T(8,128)(2,1)} async-done(((bf16[256,6144]{1,0:T(8,128)(2,1)}), bf16[16,6144]{1,0:T(8,128)(2,1)}) %reduce-scatter.7.cloned.1.call-update) | async-done | bytes 196624 | tf_op jit(solution)/shard_map/reduce_scatter | solution.py:80
  253.6 62.6 %reduce-scatter.9.cloned.1.call-done = bf16[16,6144]{1,0:T(8,128)(2,1)} async-done(((bf16[256,6144]{1,0:T(8,128)(2,1)}), bf16[16,6144]{1,0:T(8,128)(2,1)}) %reduce-scatter.9.cloned.1.call-update) | async-done | bytes 196624 | tf_op jit(solution)/shard_map/reduce_scatter | solution.py:80
  316.2 2.1 pad_maximum_fusion
  (46 shorter events, 3.6 us)
Async XLA Ops:
  6.5 121.6 %reduce-scatter.11.cloned.1.call-start = ((), (), s32[]{:S(2)}) async-start(), calls=%async_computation.7 | async-start | bytes 3342336 | tf_op jit(solution)/shard_map/reduce_scatter | solution.py:80
  8.7 9.4 %copy-start.6 = (bf16[1024,512]{1,0:T(8,128)(2,1)S(1)}, bf16[1024,512]{1,0:T(8,128)(2,1)}, u32[]{:S(2)}) copy-start(bf16[1024,512]{1,0:T(8,128)(2,1)} %param.7) | copy-start | bytes 3145732
  12.1 16.9 %collective-permute-start = (bf16[4,128,128]{2,1,0:T(8,128)(2,1)}, bf16[4,128,128]{2,1,0:T(8,128)(2,1)S(1)}, u32[]{:S(2)}, u32[]{:S(2)}) collective-permute-start(bf16[4,128,128]{2,1,0:T(8,128)(2,1)} %get-tuple-element.21), channel_id=1, source_target_pairs={{0,16},{16,32},{32,48},{48,0},{64,80},{80,96},{96,112},{112,64},{1... | collective-permute-start | bytes 393224 | tf_op jit(solution)/shard_map/ppermute | solution.py:29
  13.7 15.3 %collective-permute-start.1 = (bf16[4,128,128]{2,1,0:T(8,128)(2,1)}, bf16[4,128,128]{2,1,0:T(8,128)(2,1)}, u32[]{:S(2)}, u32[]{:S(2)}) collective-permute-start(bf16[4,128,128]{2,1,0:T(8,128)(2,1)} %get-tuple-element.21), channel_id=1, source_target_pairs={{0,32},{16,48},{32,0},{48,16},{64,96},{80,112},{96,64},{112,80},{1... | collective-permute-start | bytes 393224 | tf_op jit(solution)/shard_map/ppermute | solution.py:29
  16.6 12.4 %collective-permute-start.2 = (bf16[4,128,128]{2,1,0:T(8,128)(2,1)}, bf16[4,128,128]{2,1,0:T(8,128)(2,1)}, u32[]{:S(2)}, u32[]{:S(2)}) collective-permute-start(bf16[4,128,128]{2,1,0:T(8,128)(2,1)} %get-tuple-element.21), channel_id=1, source_target_pairs={{0,48},{16,0},{32,16},{48,32},{64,112},{80,64},{96,80},{112,96},{1... | collective-permute-start | bytes 393224 | tf_op jit(solution)/shard_map/ppermute | solution.py:29
  22.2 14.2 %copy-start.5 = (bf16[1024,512]{1,0:T(8,128)(2,1)S(1)}, bf16[1024,512]{1,0:T(8,128)(2,1)}, u32[]{:S(2)}) copy-start(bf16[1024,512]{1,0:T(8,128)(2,1)} %param.10) | copy-start | bytes 3145732
  29.0 9.1 %copy-start = (f32[2,4,128,128]{3,2,1,0:T(8,128)S(1)}, f32[2,4,128,128]{3,2,1,0:T(8,128)}, u32[]{:S(2)}) copy-start(f32[2,4,128,128]{3,2,1,0:T(8,128)} %get-tuple-element.22) | copy-start | bytes 1572868
  29.0 11.5 %copy-start.7 = (f32[4,128,128]{2,1,0:T(8,128)S(1)}, f32[4,128,128]{2,1,0:T(8,128)}, u32[]{:S(2)}) copy-start(f32[4,128,128]{2,1,0:T(8,128)} %param.11) | copy-start | bytes 786436
  30.2 10.3 %collective-permute-start.3 = (f32[4,128,128]{2,1,0:T(8,128)S(1)}, f32[4,128,128]{2,1,0:T(8,128)S(1)}, u32[]{:S(2)}, u32[]{:S(2)}) collective-permute-start(f32[4,128,128]{2,1,0:T(8,128)S(1)} %convert_add_fusion), channel_id=1, source_target_pairs={{0,64},{16,80},{32,96},{48,112},{64,128},{80,144},{96,160},{112,17... | collective-permute-start | bytes 786440 | tf_op jit(solution)/shard_map/ppermute | solution.py:34
  33.6 6.9 %collective-permute-start.4 = (f32[4,128,128]{2,1,0:T(8,128)S(1)}, f32[4,128,128]{2,1,0:T(8,128)S(1)}, u32[]{:S(2)}, u32[]{:S(2)}) collective-permute-start(f32[4,128,128]{2,1,0:T(8,128)S(1)} %convert_add_fusion), channel_id=1, source_target_pairs={{0,128},{16,144},{32,160},{48,176},{64,192},{80,208},{96,224},{112... | collective-permute-start | bytes 786440 | tf_op jit(solution)/shard_map/ppermute | solution.py:34
  35.5 5.0 %collective-permute-start.5 = (f32[4,128,128]{2,1,0:T(8,128)S(1)}, f32[4,128,128]{2,1,0:T(8,128)S(1)}, u32[]{:S(2)}, u32[]{:S(2)}) collective-permute-start(f32[4,128,128]{2,1,0:T(8,128)S(1)} %convert_add_fusion), channel_id=1, source_target_pairs={{0,192},{16,208},{32,224},{48,240},{1,193},{17,209},{33,225},{49,2... | collective-permute-start | bytes 786440 | tf_op jit(solution)/shard_map/ppermute | solution.py:34
  49.4 2.4 copy-start.1
  49.4 2.4 copy-start.2
  49.4 2.4 copy-start.3
  49.4 2.4 copy-start.4
  49.4 2.4 copy-start.8
  59.1 131.8 %reduce-scatter.5.cloned.1.call-start = ((), (), s32[]{:S(2)}) async-start(), calls=%async_computation.4 | async-start | bytes 3342336 | tf_op jit(solution)/shard_map/reduce_scatter | solution.py:80
  65.4 188.2 %reduce-scatter.7.cloned.1.call-start = ((), (), s32[]{:S(2)}) async-start(), calls=%async_computation.5 | async-start | bytes 3342336 | tf_op jit(solution)/shard_map/reduce_scatter | solution.py:80
  71.7 244.5 %reduce-scatter.9.cloned.1.call-start = ((), (), s32[]{:S(2)}) async-start(), calls=%async_computation.6 | async-start | bytes 3342336 | tf_op jit(solution)/shard_map/reduce_scatter | solution.py:80
Sparse Core Ops, SparseCore 0:
  59.2 68.9 reduce-scatter.10
  130.7 60.1 reduce-scatter.4
  193.4 60.1 reduce-scatter.6
  256.0 60.1 reduce-scatter.8

commit v3 on v1

--- a/solution.py
+++ b/solution.py
@@ -66,25 +66,40 @@
     attn = (normed * norm_gain[None, :] * jax.nn.sigmoid(gate.astype(jnp.float32))).astype(
         jnp.bfloat16
     )
-    return lax.psum_scatter(
-        jnp.dot(attn, w_out, preferred_element_type=jnp.float32).astype(jnp.bfloat16),
-        "tp",
-        scatter_dimension=0,
-        tiled=True,
-    )
+    core = lax.axis_index("core")
+    swap = [(0, 1), (1, 0)]
+    width = w_out.shape[1] // 2
+    other_w = lax.ppermute(lax.dynamic_slice_in_dim(w_out, (1 - core) * width, width, 1), "core", swap)
+    own_w = lax.dynamic_slice_in_dim(w_out, core * width, width, 1)
+    other_attn = lax.ppermute(attn, "core", swap)
+    partial = jnp.dot(
+        jnp.concatenate([attn, other_attn], axis=1),
+        jnp.concatenate([own_w, other_w], axis=0),
+        preferred_element_type=jnp.float32,
+    ).astype(jnp.bfloat16)
+    summed = lax.psum_scatter(partial, "z", scatter_dimension=0, tiled=True)
+    half = summed.shape[0] // 2
+    keep = lax.dynamic_slice_in_dim(summed, core * half, half, 0)
+    give = lax.dynamic_slice_in_dim(summed, (1 - core) * half, half, 0)
+    got = lax.ppermute(give, "core", swap)
+    return jnp.where(core == 0, jnp.concatenate([keep, got], axis=1), jnp.concatenate([got, keep], axis=1))
 
 
 def solution(mesh):
+    n_tp = mesh.shape["tp"]
+    devices = mesh.devices.reshape(mesh.shape["seq"], n_tp // 2, 2)
+    inner = jax.sharding.Mesh(devices, ("seq", "z", "core"))
+    tp = ("z", "core")
     in_specs = (
-        P("seq", "tp"),
-        P("seq", "tp"),
-        P("seq", "tp"),
-        P("seq", "tp"),
-        P("tp", None, None),
-        P("tp"),
-        P("tp", None),
+        P("seq", tp),
+        P("seq", tp),
+        P("seq", tp),
+        P("seq", tp),
+        P(tp, None, None),
+        P(tp),
+        P(tp, None),
     )
-    out_specs = P(("seq", "tp"), None)
+    out_specs = P(("seq", "z", "core"), None)
     return jax.shard_map(
-        per_device, mesh=mesh, in_specs=in_specs, out_specs=out_specs, check_vma=False
+        per_device, mesh=inner, in_specs=in_specs, out_specs=out_specs, check_vma=False
     )

time: 150 us -> 158 us (1.053)
  local copies, waits for them, and re-layouts: 7.31 us -> 14.7 us
  waiting for transfers between devices: 87.4 us -> 84.1 us
  other arithmetic: 5.96 us -> 9.22 us
    dynamic_slice x0 -> x2, local copies, waits for them, and re-layouts: none -> 7.19 us  [the longest x1 6.03 us: per_device(): own_w = lax.dynamic_slice_in_dim(w_out, core * width, width, 1)]
    ppermute x0 -> x3, waiting for transfers between devices: none -> 4.14 us  [the longest x1 2.44 us: per_device(): other_attn = lax.ppermute(attn, 'core', swap)]
    ppermute x3, waiting for transfers between devices: 3.99 us -> 0.01 us  [exclusive_prefix(): before = before + lax.ppermute(row_total, 'seq', perm)]
    ppermute x3, waiting for transfers between devices: 3.62 us -> 0.01 us  [exclusive_prefix(): got = lax.ppermute(sent, 'seq', perm).astype(jnp.float32)]
    convert_element_type x0 -> x1, other arithmetic: none -> 2.08 us  [per_device(): (normed * norm_gain[None, :] * jax.nn.sigmoid(gate.astype(jnp.float32)))....]
  transfers between devices with their start and end apart: 7 -> 10, of which waited for: 4 -> 3; matrix products, arithmetic and copies ran while one was open for 7% -> 17% of each run, Pallas kernels for 0% -> 0%
where the time goes in v3:
time: 158 us; the launch traced here: 157 us
  waiting for transfers between devices  84.1 us (53%)
  matrix products  21.6 us (14%)
  local copies, waits for them, and re-layouts  14.7 us (9%)
  starting transfers between devices  13.8 us (9%)
  between operations  13.6 us (9%)
  other arithmetic  9.22 us (6%)
    reduce_scatter x1, waiting for transfers between devices, per_device(): summed = lax.psum_scatter(partial, 'z', scatter_dimension=0, tiled=True)  79.9 us
    dot_general x1, matrix products, per_device(): jnp.dot(jnp.concatenate([attn, other_attn], axis=1), jnp.concatenate([own...  10.5 us
    ppermute x3, starting transfers between devices, exclusive_prefix(): before = before + lax.ppermute(row_total, 'seq', perm)  7.52 us
    dot_general x1, matrix products, per_device(): jnp.einsum('nhts,nshe->nthe', scores, va.astype(jnp.float32), precision=h...  6.67 us
    dynamic_slice x1, local copies, waits for them, and re-layouts, per_device(): own_w = lax.dynamic_slice_in_dim(w_out, core * width, width, 1)  6.03 us
    ppermute x3, starting transfers between devices, exclusive_prefix(): got = lax.ppermute(sent, 'seq', perm).astype(jnp.float32)  5.82 us
  transfers between devices with their start and end apart: 10, of which 3 were waited for; matrix products, arithmetic and copies ran while one was open for 17% of the time, Pallas kernels for 0%

profile of v3, /device:TPU:2, one launch (start us, length us, event | category | flops | bytes accessed | tf_op | source)
XLA Modules:
  0.0 157.0 jit_solution(16939915369702993948)
XLA Ops:
  6.5 1.3 reshape.47
  7.9 0.7 copy.33
  8.6 1.8 %fusion.14 = bf16[1024,512]{1,0:T(8,128)(2,1)S(1)} fusion(bf16[1024,512]{1,0:T(8,128)(2,1)} %param.8), kind=kLoop, calls=%fused_computation.16 | loop fusion | flops 3145728 | bytes 2097152 | tf_op jit(solution)/shard_map/convert_element_type | solution.py:48
  10.4 0.3 reshape.46
  10.7 2.0 %fusion.41 = (bf16[4,128,128]{2,1,0:T(8,128)(2,1)}, f32[2,4,128,128]{3,2,1,0:T(8,128)}) fusion(bf16[2,512,4,128]{1,3,2,0:T(8,128)(2,1)S(1)} %copy.33, bf16[2,512,4,128]{3,2,1,0:T(4,128)(2,1)S(1)} %reshape.46), kind=kOutput, calls=%fused_computation.60 | convolution fusion | flops 134283264 | bytes 2752512 | tf_op jit(solution)/shard_map/nthd,nthe->nhde/dot_general | solution.py:52
  12.7 1.6 %collective-permute-start = (bf16[4,128,128]{2,1,0:T(8,128)(2,1)}, bf16[4,128,128]{2,1,0:T(8,128)(2,1)S(1)}, u32[]{:S(2)}, u32[]{:S(2)}) collective-permute-start(bf16[4,128,128]{2,1,0:T(8,128)(2,1)} %get-tuple-element.9), channel_id=1, source_target_pairs={{0,16},{16,32},{32,48},{48,0},{64,80},{80,96},{96,112},{112,64},{1... | collective-permute-start | bytes 393224 | tf_op jit(solution)/shard_map/ppermute | solution.py:28
  14.2 2.9 %collective-permute-start.1 = (bf16[4,128,128]{2,1,0:T(8,128)(2,1)}, bf16[4,128,128]{2,1,0:T(8,128)(2,1)S(1)}, u32[]{:S(2)}, u32[]{:S(2)}) collective-permute-start(bf16[4,128,128]{2,1,0:T(8,128)(2,1)} %get-tuple-element.9), channel_id=1, source_target_pairs={{0,32},{16,48},{32,0},{48,16},{64,96},{80,112},{96,64},{112,80},{1... | collective-permute-start | bytes 393224 | tf_op jit(solution)/shard_map/ppermute | solution.py:28
  17.1 1.3 collective-permute-start.2
  18.5 6.0 %constant_dynamic-slice_fusion.3 = (bf16[512,3072]{1,0:T(8,128)(2,1)}, bf16[512,3072]{1,0:T(8,128)(2,1)}) fusion(bf16[512,6144]{1,0:T(8,128)(2,1)} %param.13, s32[]{:T(128)S(6)} %select_n.60, s32[]{:T(128)S(6)} %select_n.61), kind=kLoop, calls=%fused_computation.57 | loop fusion | bytes 12582920 | tf_op jit(solution)/shard_map/dynamic_slice | solution.py:73
  24.5 1.5 fusion.18
  26.1 1.3 reshape.48
  27.4 1.3 fusion.27
  28.8 1.0 convert_add_fusion
  29.8 3.5 %collective-permute-start.3 = (f32[4,128,128]{2,1,0:T(8,128)S(1)}, f32[4,128,128]{2,1,0:T(8,128)}, u32[]{:S(2)}, u32[]{:S(2)}) collective-permute-start(f32[4,128,128]{2,1,0:T(8,128)S(1)} %convert_add_fusion), channel_id=1, source_target_pairs={{0,64},{16,80},{32,96},{48,112},{64,128},{80,144},{96,160},{112,17... | collective-permute-start | bytes 786440 | tf_op jit(solution)/shard_map/ppermute | solution.py:33
  33.3 2.6 %collective-permute-start.4 = (f32[4,128,128]{2,1,0:T(8,128)S(1)}, f32[4,128,128]{2,1,0:T(8,128)}, u32[]{:S(2)}, u32[]{:S(2)}) collective-permute-start(f32[4,128,128]{2,1,0:T(8,128)S(1)} %convert_add_fusion), channel_id=1, source_target_pairs={{0,128},{16,144},{32,160},{48,176},{64,192},{80,208},{96,224},{112... | collective-permute-start | bytes 786440 | tf_op jit(solution)/shard_map/ppermute | solution.py:33
  36.0 1.4 collective-permute-start.5
  37.3 6.7 %fusion = f32[2,4,512,128]{2,3,1,0:T(8,128)} fusion(bf16[2,512,4,128]{1,3,2,0:T(8,128)(2,1)S(1)} %copy.33, f32[2,4,512,512]{3,2,1,0:T(8,128)S(1)} %fusion.27, pred[512,512]{1,0:T(8,128)(4,1)S(1)} %iota_compare_fusion), kind=kOutput, calls=%fused_computation | convolution fusion | flops 3223322624 | bytes 11796480 | tf_op jit(solution)/shard_map/nhts,nshe->nthe/dot_general | solution.py:62
  44.0 0.2 reduce-window_subtract_fusion
  44.3 1.4 fusion.37
  45.9 1.3 multiply_reduce_fusion
  47.2 0.2 copy.35
  47.4 1.8 %copy.34 = f32[2,512,4,128]{3,2,1,0:T(4,128)} copy(f32[2,512,4,128]{1,3,2,0:T(8,128)S(1)} %get-tuple-element.12) | data formatting | bytes 4194304 | tf_op jit(solution)/shard_map/add | solution.py:63
  49.3 1.2 mul.48
  50.5 0.4 copy-done.1
  50.8 2.1 %fusion.21 = bf16[1024,512]{1,0:T(8,128)(2,1)S(1)} fusion(f32[128,8,4,128]{3,2,1,0:T(4,128)S(1)} %bitcast.21, f32[128,8,4,128]{3,2,1,0:T(4,128)S(1)} %bitcast.22, bf16[1024,512]{1,0:T(8,128)(2,1)} %param.10, f32[512]{0:T(512)S(1)} %copy-done.5), kind=kLoop, calls=%fused_computation.24 | loop fusion | flops 4194304 | bytes 6293504 | tf_op jit(solution)/shard_map/convert_element_type | solution.py:66
  52.9 0.3 collective-permute-start.6
  53.2 2.4 %collective-permute-done.6 = bf16[1024,512]{1,0:T(8,128)(2,1)S(1)} collective-permute-done((bf16[1024,512]{1,0:T(8,128)(2,1)S(1)}, bf16[1024,512]{1,0:T(8,128)(2,1)S(1)}, u32[]{:S(2)}, u32[]{:S(2)}) %collective-permute-start.6) | collective-permute-done | bytes 1048608 | tf_op jit(solution)/shard_map/ppermute | solution.py:74
  55.7 10.5 %fusion.6 = bf16[1024,3072]{1,0:T(8,128)(2,1)} fusion(bf16[512,3072]{1,0:T(8,128)(2,1)} %collective-permute-done.7, bf16[512,3072]{1,0:T(8,128)(2,1)S(1)} %copy-done.3, bf16[1024,512]{1,0:T(8,128)(2,1)S(1)} %collective-permute-done.6, bf16[1024,512]{1,0:T(8,128)(2,1)S(1)} %fusion.21), kind=kOutput, calls=%fused_computation.6 | convolution fusion | flops 6462373888 | bytes 14680064 | tf_op jit(solution)/shard_map/dot_general | solution.py:75
  66.2 79.9 %reduce-scatter.2.cloned.1.call-done = bf16[128,3072]{1,0:T(8,128)(2,1)} async-done(((bf16[1024,3072]{1,0:T(8,128)(2,1)}), bf16[128,3072]{1,0:T(8,128)(2,1)}) %reduce-scatter.2.cloned.1.call-update) | async-done | bytes 786448 | tf_op jit(solution)/shard_map/reduce_scatter | solution.py:80
  146.1 1.2 constant_dynamic-slice_fusion.1
  147.4 1.7 %collective-permute-done.8 = bf16[64,3072]{1,0:T(8,128)(2,1)S(1)} collective-permute-done((bf16[64,3072]{1,0:T(8,128)(2,1)S(1)}, bf16[64,3072]{1,0:T(8,128)(2,1)S(1)}, u32[]{:S(2)}, u32[]{:S(2)}) %collective-permute-start.8) | collective-permute-done | bytes 393248 | tf_op jit(solution)/shard_map/ppermute | solution.py:84
  149.1 1.1 maximum_select_fusion
  (24 shorter events, 0.5 us)
Async XLA Ops:
  6.5 139.6 %reduce-scatter.2.cloned.1.call-start = ((), (), s32[]{:S(2)}) async-start(), calls=%async_computation.1 | async-start | bytes 7077888 | tf_op jit(solution)/shard_map/reduce_scatter | solution.py:80
  12.7 16.1 %collective-permute-start = (bf16[4,128,128]{2,1,0:T(8,128)(2,1)}, bf16[4,128,128]{2,1,0:T(8,128)(2,1)S(1)}, u32[]{:S(2)}, u32[]{:S(2)}) collective-permute-start(bf16[4,128,128]{2,1,0:T(8,128)(2,1)} %get-tuple-element.9), channel_id=1, source_target_pairs={{0,16},{16,32},{32,48},{48,0},{64,80},{80,96},{96,112},{112,64},{1... | collective-permute-start | bytes 393224 | tf_op jit(solution)/shard_map/ppermute | solution.py:28
  14.2 14.5 %collective-permute-start.1 = (bf16[4,128,128]{2,1,0:T(8,128)(2,1)}, bf16[4,128,128]{2,1,0:T(8,128)(2,1)S(1)}, u32[]{:S(2)}, u32[]{:S(2)}) collective-permute-start(bf16[4,128,128]{2,1,0:T(8,128)(2,1)} %get-tuple-element.9), channel_id=1, source_target_pairs={{0,32},{16,48},{32,0},{48,16},{64,96},{80,112},{96,64},{112,80},{1... | collective-permute-start | bytes 393224 | tf_op jit(solution)/shard_map/ppermute | solution.py:28
  17.1 11.7 %collective-permute-start.2 = (bf16[4,128,128]{2,1,0:T(8,128)(2,1)}, bf16[4,128,128]{2,1,0:T(8,128)(2,1)S(1)}, u32[]{:S(2)}, u32[]{:S(2)}) collective-permute-start(bf16[4,128,128]{2,1,0:T(8,128)(2,1)} %get-tuple-element.9), channel_id=1, source_target_pairs={{0,48},{16,0},{32,16},{48,32},{64,112},{80,64},{96,80},{112,96},{1... | collective-permute-start | bytes 393224 | tf_op jit(solution)/shard_map/ppermute | solution.py:28
  18.5 6.0 %copy-start.4 = (bf16[1024,512]{1,0:T(8,128)(2,1)S(1)}, bf16[1024,512]{1,0:T(8,128)(2,1)}, u32[]{:S(2)}) copy-start(bf16[1024,512]{1,0:T(8,128)(2,1)} %param.7) | copy-start | bytes 3145732
  24.5 31.2 %collective-permute-start.7 = (bf16[512,3072]{1,0:T(8,128)(2,1)}, bf16[512,3072]{1,0:T(8,128)(2,1)}, u32[]{:S(2)}, u32[]{:S(2)}) collective-permute-start(bf16[512,3072]{1,0:T(8,128)(2,1)} %get-tuple-element.6), channel_id=1, source_target_pairs={{0,1},{1,0},{2,3},{3,2},{4,5},{5,4},{6,7},{7,6},{8,9},{9,8},{10,11... | collective-permute-start | bytes 9437192 | tf_op jit(solution)/shard_map/ppermute | solution.py:72
  29.8 14.2 %copy-start.2 = (f32[2,4,128,128]{3,2,1,0:T(8,128)S(1)}, f32[2,4,128,128]{3,2,1,0:T(8,128)}, u32[]{:S(2)}) copy-start(f32[2,4,128,128]{3,2,1,0:T(8,128)} %get-tuple-element.10) | copy-start | bytes 1572868
  29.8 14.4 %collective-permute-start.3 = (f32[4,128,128]{2,1,0:T(8,128)S(1)}, f32[4,128,128]{2,1,0:T(8,128)}, u32[]{:S(2)}, u32[]{:S(2)}) collective-permute-start(f32[4,128,128]{2,1,0:T(8,128)S(1)} %convert_add_fusion), channel_id=1, source_target_pairs={{0,64},{16,80},{32,96},{48,112},{64,128},{80,144},{96,160},{112,17... | collective-permute-start | bytes 786440 | tf_op jit(solution)/shard_map/ppermute | solution.py:33
  33.3 10.9 %collective-permute-start.4 = (f32[4,128,128]{2,1,0:T(8,128)S(1)}, f32[4,128,128]{2,1,0:T(8,128)}, u32[]{:S(2)}, u32[]{:S(2)}) collective-permute-start(f32[4,128,128]{2,1,0:T(8,128)S(1)} %convert_add_fusion), channel_id=1, source_target_pairs={{0,128},{16,144},{32,160},{48,176},{64,192},{80,208},{96,224},{112... | collective-permute-start | bytes 786440 | tf_op jit(solution)/shard_map/ppermute | solution.py:33
  36.0 8.3 %collective-permute-start.5 = (f32[4,128,128]{2,1,0:T(8,128)S(1)}, f32[4,128,128]{2,1,0:T(8,128)}, u32[]{:S(2)}, u32[]{:S(2)}) collective-permute-start(f32[4,128,128]{2,1,0:T(8,128)S(1)} %convert_add_fusion), channel_id=1, source_target_pairs={{0,192},{16,208},{32,224},{48,240},{1,193},{17,209},{33,225},{49,2... | collective-permute-start | bytes 786440 | tf_op jit(solution)/shard_map/ppermute | solution.py:33
  44.0 1.9 %copy-start = (f32[2,4,512,128]{2,3,1,0:T(8,128)S(1)}, f32[2,4,512,128]{2,3,1,0:T(8,128)}, u32[]{:S(2)}) copy-start(f32[2,4,512,128]{2,3,1,0:T(8,128)} %fusion) | copy-start | bytes 6291460
  49.3 1.6 %copy-start.1 = (f32[2,512,4,128]{3,2,1,0:T(4,128)S(1)}, f32[2,512,4,128]{3,2,1,0:T(4,128)}, u32[]{:S(2)}) copy-start(f32[2,512,4,128]{3,2,1,0:T(4,128)} %copy.34) | copy-start | bytes 6291460
  49.3 1.6 %copy-start.5 = (f32[512]{0:T(512)S(1)}, f32[512]{0:T(512)}, u32[]{:S(2)}) copy-start(f32[512]{0:T(512)} %param.12) | copy-start | bytes 6148
  50.8 4.8 %copy-start.3 = (bf16[512,3072]{1,0:T(8,128)(2,1)S(1)}, bf16[512,3072]{1,0:T(8,128)(2,1)}, u32[]{:S(2)}) copy-start(bf16[512,3072]{1,0:T(8,128)(2,1)} %get-tuple-element.5) | copy-start | bytes 9437188
  52.9 2.7 %collective-permute-start.6 = (bf16[1024,512]{1,0:T(8,128)(2,1)S(1)}, bf16[1024,512]{1,0:T(8,128)(2,1)S(1)}, u32[]{:S(2)}, u32[]{:S(2)}) collective-permute-start(bf16[1024,512]{1,0:T(8,128)(2,1)S(1)} %fusion.21), channel_id=1, source_target_pairs={{0,1},{1,0},{2,3},{3,2},{4,5},{5,4},{6,7},{7,6},{8,9},{9,8},{10,11... | collective-permute-start | bytes 3145736 | tf_op jit(solution)/shard_map/ppermute | solution.py:74
  147.3 1.8 %collective-permute-start.8 = (bf16[64,3072]{1,0:T(8,128)(2,1)S(1)}, bf16[64,3072]{1,0:T(8,128)(2,1)S(1)}, u32[]{:S(2)}, u32[]{:S(2)}) collective-permute-start(bf16[64,3072]{1,0:T(8,128)(2,1)S(1)} %get-tuple-element.8), channel_id=1, source_target_pairs={{0,1},{1,0},{2,3},{3,2},{4,5},{5,4},{6,7},{7,6},{8,9},{9,8},{10,11... | collective-permute-start | bytes 1179656 | tf_op jit(solution)/shard_map/ppermute | solution.py:84
Sparse Core Ops, SparseCore 0:
  66.3 79.7 reduce-scatter.1

commit v4 on v1

--- a/solution.py
+++ b/solution.py
@@ -30,7 +30,7 @@
         before = before + jnp.where(k <= along, got, jnp.float32(0.0))
     for k in range(1, rows):
         perm = [(a * r + b, (a + k) * r + b) for a in range(rows - k) for b in range(r)]
-        before = before + lax.ppermute(row_total, "seq", perm)
+        before = before + lax.ppermute(row_total.astype(jnp.bfloat16), "seq", perm).astype(jnp.float32)
     return before
 
 
@@ -52,6 +52,7 @@
     block_states = jnp.einsum("nthd,nthe->nhde", ka, va, preferred_element_type=jnp.float32)
     own_total = jnp.sum(block_states, axis=0)
     local_before = jnp.cumsum(block_states, axis=0) - block_states
+    gated = norm_gain[None, :] * jax.nn.sigmoid(gate.astype(jnp.float32))
     prior = exclusive_prefix(own_total)
     states = local_before + (kv_start + prior)[None]
     q_float = qa.astype(jnp.float32)
@@ -63,9 +64,8 @@
     heads_out = (inter + intra).reshape(rows, heads, HD)
     scale = lax.rsqrt(jnp.mean(heads_out * heads_out, axis=-1, keepdims=True) + 1e-05)
     normed = (heads_out * scale).reshape(rows, heads * HD)
-    attn = (normed * norm_gain[None, :] * jax.nn.sigmoid(gate.astype(jnp.float32))).astype(
-        jnp.bfloat16
-    )
+    attn = (normed * gated).astype(jnp.bfloat16)
+    attn = lax.optimization_barrier(attn)
     return lax.psum_scatter(
         jnp.dot(attn, w_out, preferred_element_type=jnp.float32).astype(jnp.bfloat16),
         "tp",

time: 150 us -> 150 us (level)
  other arithmetic: 5.96 us -> 8.1 us
  waiting for transfers between devices: 87.4 us -> 85.5 us
    ppermute x3, waiting for transfers between devices: 3.62 us -> 0.01 us  [exclusive_prefix(): got = lax.ppermute(sent, 'seq', perm).astype(jnp.float32)]
    convert_element_type x0 -> x2, other arithmetic: none -> 3.18 us  [the longest x1 1.93 us: per_device(): attn = (normed * gated).astype(jnp.bfloat16)]
  transfers between devices with their start and end apart: 7 -> 7, of which waited for: 4 -> 3; matrix products, arithmetic and copies ran while one was open for 7% -> 8% of each run, Pallas kernels for 0% -> 0%
where the time goes in v4:
time: 150 us; the launch traced here: 149 us
  waiting for transfers between devices  85.5 us (57%)
  matrix products  23.7 us (16%)
  between operations  13.6 us (9%)
  starting transfers between devices  12 us (8%)
  other arithmetic  8.1 us (5%)
  local copies, waits for them, and re-layouts  6.29 us (4%)
    reduce_scatter x1, waiting for transfers between devices, per_device(): lax.psum_scatter(jnp.dot(attn, w_out, preferred_element_type=jnp.float32)...  80.9 us
    dot_general x1, matrix products, per_device(): jnp.dot(attn, w_out, preferred_element_type=jnp.float32)  12.5 us
    ppermute x3, starting transfers between devices, exclusive_prefix(): lax.ppermute(row_total.astype(jnp.bfloat16), 'seq', perm)  7.43 us
    dot_general x1, matrix products, per_device(): jnp.einsum('nhts,nshe->nthe', scores, va.astype(jnp.float32), precision=h...  6.72 us
    ppermute x3, starting transfers between devices, exclusive_prefix(): got = lax.ppermute(sent, 'seq', perm).astype(jnp.float32)  4.61 us
    ppermute x3, waiting for transfers between devices, exclusive_prefix(): lax.ppermute(row_total.astype(jnp.bfloat16), 'seq', perm)  4.52 us
  transfers between devices with their start and end apart: 7, of which 3 were waited for; matrix products, arithmetic and copies ran while one was open for 8% of the time, Pallas kernels for 0%

profile of v4, /device:TPU:2, one launch (start us, length us, event | category | flops | bytes accessed | tf_op | source)
XLA Modules:
  0.0 149.2 jit_solution(17889593695211334752)
XLA Ops:
  6.5 1.9 %fusion.7 = bf16[1024,512]{1,0:T(8,128)(2,1)S(1)} fusion(bf16[1024,512]{1,0:T(8,128)(2,1)} %param.8), kind=kLoop, calls=%fused_computation.12 | loop fusion | flops 3145728 | bytes 2097152 | tf_op jit(solution)/shard_map/convert_element_type | solution.py:48
  8.4 0.3 reshape.46
  8.8 0.3 reshape.47
  9.1 0.7 copy.33
  9.7 0.0 copy-start.4
  9.7 2.0 %fusion.30 = (bf16[4,128,128]{2,1,0:T(8,128)(2,1)}, f32[2,4,128,128]{3,2,1,0:T(8,128)}) fusion(bf16[2,512,4,128]{1,3,2,0:T(8,128)(2,1)S(1)} %copy.33, bf16[2,512,4,128]{3,2,1,0:T(4,128)(2,1)S(1)} %reshape.46), kind=kOutput, calls=%fused_computation.47 | convolution fusion | flops 134283264 | bytes 2752512 | tf_op jit(solution)/shard_map/nthd,nthe->nhde/dot_general | solution.py:52
  11.7 3.0 %collective-permute-start.2 = (bf16[4,128,128]{2,1,0:T(8,128)(2,1)}, bf16[4,128,128]{2,1,0:T(8,128)(2,1)S(1)}, u32[]{:S(2)}, u32[]{:S(2)}) collective-permute-start(bf16[4,128,128]{2,1,0:T(8,128)(2,1)} %get-tuple-element.5), channel_id=1, source_target_pairs={{0,48},{16,0},{32,16},{48,32},{64,112},{80,64},{96,80},{112,96},{1... | collective-permute-start | bytes 393224 | tf_op jit(solution)/shard_map/ppermute | solution.py:28
  14.7 0.6 collective-permute-start.1
  15.4 1.0 collective-permute-start
  16.3 0.1 iota_compare_fusion
  16.4 1.6 %fusion.11 = bf16[1024,512]{1,0:T(8,128)(2,1)} fusion(bf16[1024,512]{1,0:T(8,128)(2,1)S(1)} %copy-done.4), kind=kLoop, calls=%fused_computation.16 | loop fusion | flops 3145728 | bytes 2097152 | tf_op jit(solution)/shard_map/convert_element_type | solution.py:44
  18.0 1.3 reshape.48
  19.3 1.3 fusion.16
  20.6 0.0 copy-start.2
  20.6 6.7 %fusion = f32[2,4,512,128]{2,3,1,0:T(8,128)} fusion(bf16[2,512,4,128]{1,3,2,0:T(8,128)(2,1)S(1)} %copy.33, f32[2,4,512,512]{3,2,1,0:T(8,128)S(1)} %fusion.16, pred[512,512]{1,0:T(8,128)(4,1)S(1)} %iota_compare_fusion), kind=kOutput, calls=%fused_computation.1 | convolution fusion | flops 3223322624 | bytes 11796480 | tf_op jit(solution)/shard_map/nhts,nshe->nthe/dot_general | solution.py:63
  27.4 1.3 fusion.27
  28.6 0.7 collective-permute-start.5
  29.3 4.7 %collective-permute-start.4 = (bf16[4,128,128]{2,1,0:T(8,128)(2,1)S(1)}, bf16[4,128,128]{2,1,0:T(8,128)(2,1)S(1)}, u32[]{:S(2)}, u32[]{:S(2)}) collective-permute-start(bf16[4,128,128]{2,1,0:T(8,128)(2,1)S(1)} %fusion.27), channel_id=1, source_target_pairs={{0,128},{16,144},{32,160},{48,176},{64,192},{80,208},{96,224},{112... | collective-permute-start | bytes 393224 | tf_op jit(solution)/shard_map/ppermute | solution.py:33
  34.0 2.1 %collective-permute-start.3 = (bf16[4,128,128]{2,1,0:T(8,128)(2,1)S(1)}, bf16[4,128,128]{2,1,0:T(8,128)(2,1)S(1)}, u32[]{:S(2)}, u32[]{:S(2)}) collective-permute-start(bf16[4,128,128]{2,1,0:T(8,128)(2,1)S(1)} %fusion.27), channel_id=1, source_target_pairs={{0,64},{16,80},{32,96},{48,112},{64,128},{80,144},{96,160},{112,17... | collective-permute-start | bytes 393224 | tf_op jit(solution)/shard_map/ppermute | solution.py:33
  36.1 0.2 reduce-window_subtract_fusion
  36.3 0.1 collective-permute-done.4
  36.5 4.4 %collective-permute-done.3 = bf16[4,128,128]{2,1,0:T(8,128)(2,1)S(1)} collective-permute-done((bf16[4,128,128]{2,1,0:T(8,128)(2,1)S(1)}, bf16[4,128,128]{2,1,0:T(8,128)(2,1)S(1)}, u32[]{:S(2)}, u32[]{:S(2)}) %collective-permute-start.3) | collective-permute-done | bytes 131104 | tf_op jit(solution)/shard_map/ppermute | solution.py:33
  40.9 1.1 fusion.26
  42.0 1.3 multiply_reduce_fusion
  43.3 0.2 copy.35
  43.5 1.9 %copy.34 = f32[2,512,4,128]{3,2,1,0:T(4,128)} copy(f32[2,512,4,128]{1,3,2,0:T(8,128)S(1)} %get-tuple-element.8) | data formatting | bytes 4194304 | tf_op jit(solution)/shard_map/add | solution.py:64
  45.4 1.2 mul.36
  46.6 0.4 copy-done.1
  47.0 1.9 %fusion.13 = bf16[1024,512]{1,0:T(8,128)(2,1)S(1)} fusion(f32[128,8,4,128]{3,2,1,0:T(4,128)S(1)} %bitcast.21, f32[128,8,4,128]{3,2,1,0:T(4,128)S(1)} %bitcast.22, bf16[1024,512]{1,0:T(8,128)(2,1)} %param.10, f32[512]{0:T(512)S(1)} %copy-done.6), kind=kLoop, calls=%fused_computation.19 | loop fusion | flops 4194304 | bytes 6293504 | tf_op jit(solution)/shard_map/convert_element_type | solution.py:67
  48.9 12.5 %convolution_convert_fusion = bf16[1024,6144]{1,0:T(8,128)(2,1)} fusion(bf16[1024,512]{1,0:T(8,128)(2,1)S(1)} %fusion.13, bf16[512,6144]{1,0:T(8,128)(2,1)} %param.13), kind=kOutput, calls=%fused_computation | convolution fusion | flops 6448742400 | bytes 19922944 | tf_op jit(solution)/shard_map/dot_general | solution.py:70
  61.4 0.0 reduce-scatter.2.cloned.1.call-update
  61.4 80.9 %reduce-scatter.2.cloned.1.call-done = bf16[64,6144]{1,0:T(8,128)(2,1)} async-done(((bf16[1024,6144]{1,0:T(8,128)(2,1)}), bf16[64,6144]{1,0:T(8,128)(2,1)}) %reduce-scatter.2.cloned.1.call-update) | async-done | bytes 786448 | tf_op jit(solution)/shard_map/reduce_scatter | solution.py:69
  (17 shorter events, 0.0 us)
Async XLA Ops:
  6.5 2.2 %copy-start.3 = (bf16[1024,512]{1,0:T(8,128)(2,1)S(1)}, bf16[1024,512]{1,0:T(8,128)(2,1)}, u32[]{:S(2)}) copy-start(bf16[1024,512]{1,0:T(8,128)(2,1)} %param.9) | copy-start | bytes 3145732
  6.5 135.8 %reduce-scatter.2.cloned.1.call-start = ((), (), s32[]{:S(2)}) async-start(), calls=%async_computation.1 | async-start | bytes 13369344 | tf_op jit(solution)/shard_map/reduce_scatter | solution.py:69
  9.7 6.7 %copy-start.4 = (bf16[1024,512]{1,0:T(8,128)(2,1)S(1)}, bf16[1024,512]{1,0:T(8,128)(2,1)}, u32[]{:S(2)}) copy-start(bf16[1024,512]{1,0:T(8,128)(2,1)} %param.7) | copy-start | bytes 3145732
  11.7 15.6 %collective-permute-start.2 = (bf16[4,128,128]{2,1,0:T(8,128)(2,1)}, bf16[4,128,128]{2,1,0:T(8,128)(2,1)S(1)}, u32[]{:S(2)}, u32[]{:S(2)}) collective-permute-start(bf16[4,128,128]{2,1,0:T(8,128)(2,1)} %get-tuple-element.5), channel_id=1, source_target_pairs={{0,48},{16,0},{32,16},{48,32},{64,112},{80,64},{96,80},{112,96},{1... | collective-permute-start | bytes 393224 | tf_op jit(solution)/shard_map/ppermute | solution.py:28
  14.7 12.6 %collective-permute-start.1 = (bf16[4,128,128]{2,1,0:T(8,128)(2,1)}, bf16[4,128,128]{2,1,0:T(8,128)(2,1)}, u32[]{:S(2)}, u32[]{:S(2)}) collective-permute-start(bf16[4,128,128]{2,1,0:T(8,128)(2,1)} %get-tuple-element.5), channel_id=1, source_target_pairs={{0,32},{16,48},{32,0},{48,16},{64,96},{80,112},{96,64},{112,80},{1... | collective-permute-start | bytes 393224 | tf_op jit(solution)/shard_map/ppermute | solution.py:28
  15.4 12.0 %collective-permute-start = (bf16[4,128,128]{2,1,0:T(8,128)(2,1)}, bf16[4,128,128]{2,1,0:T(8,128)(2,1)}, u32[]{:S(2)}, u32[]{:S(2)}) collective-permute-start(bf16[4,128,128]{2,1,0:T(8,128)(2,1)} %get-tuple-element.5), channel_id=1, source_target_pairs={{0,16},{16,32},{32,48},{48,0},{64,80},{80,96},{96,112},{112,64},{1... | collective-permute-start | bytes 393224 | tf_op jit(solution)/shard_map/ppermute | solution.py:28
  20.6 15.5 %copy-start.2 = (f32[2,4,128,128]{3,2,1,0:T(8,128)S(1)}, f32[2,4,128,128]{3,2,1,0:T(8,128)}, u32[]{:S(2)}) copy-start(f32[2,4,128,128]{3,2,1,0:T(8,128)} %get-tuple-element.6) | copy-start | bytes 1572868
  27.3 13.5 %copy-start.5 = (f32[4,128,128]{2,1,0:T(8,128)S(1)}, f32[4,128,128]{2,1,0:T(8,128)}, u32[]{:S(2)}) copy-start(f32[4,128,128]{2,1,0:T(8,128)} %param.11) | copy-start | bytes 786436
  27.3 14.6 %copy-start = (f32[2,4,512,128]{2,3,1,0:T(8,128)S(1)}, f32[2,4,512,128]{2,3,1,0:T(8,128)}, u32[]{:S(2)}) copy-start(f32[2,4,512,128]{2,3,1,0:T(8,128)} %fusion) | copy-start | bytes 6291460
  28.6 7.7 %collective-permute-start.5 = (bf16[4,128,128]{2,1,0:T(8,128)(2,1)S(1)}, bf16[4,128,128]{2,1,0:T(8,128)(2,1)S(1)}, u32[]{:S(2)}, u32[]{:S(2)}) collective-permute-start(bf16[4,128,128]{2,1,0:T(8,128)(2,1)S(1)} %fusion.27), channel_id=1, source_target_pairs={{0,192},{16,208},{32,224},{48,240},{1,193},{17,209},{33,225},{49,2... | collective-permute-start | bytes 393224 | tf_op jit(solution)/shard_map/ppermute | solution.py:33
  29.3 7.2 %collective-permute-start.4 = (bf16[4,128,128]{2,1,0:T(8,128)(2,1)S(1)}, bf16[4,128,128]{2,1,0:T(8,128)(2,1)S(1)}, u32[]{:S(2)}, u32[]{:S(2)}) collective-permute-start(bf16[4,128,128]{2,1,0:T(8,128)(2,1)S(1)} %fusion.27), channel_id=1, source_target_pairs={{0,128},{16,144},{32,160},{48,176},{64,192},{80,208},{96,224},{112... | collective-permute-start | bytes 393224 | tf_op jit(solution)/shard_map/ppermute | solution.py:33
  34.0 6.9 %collective-permute-start.3 = (bf16[4,128,128]{2,1,0:T(8,128)(2,1)S(1)}, bf16[4,128,128]{2,1,0:T(8,128)(2,1)S(1)}, u32[]{:S(2)}, u32[]{:S(2)}) collective-permute-start(bf16[4,128,128]{2,1,0:T(8,128)(2,1)S(1)} %fusion.27), channel_id=1, source_target_pairs={{0,64},{16,80},{32,96},{48,112},{64,128},{80,144},{96,160},{112,17... | collective-permute-start | bytes 393224 | tf_op jit(solution)/shard_map/ppermute | solution.py:33
  45.4 1.6 %copy-start.1 = (f32[2,512,4,128]{3,2,1,0:T(4,128)S(1)}, f32[2,512,4,128]{3,2,1,0:T(4,128)}, u32[]{:S(2)}) copy-start(f32[2,512,4,128]{3,2,1,0:T(4,128)} %copy.34) | copy-start | bytes 6291460
  45.4 1.6 %copy-start.6 = (f32[512]{0:T(512)S(1)}, f32[512]{0:T(512)}, u32[]{:S(2)}) copy-start(f32[512]{0:T(512)} %param.12) | copy-start | bytes 6148
Sparse Core Ops, SparseCore 0:
  61.5 80.7 reduce-scatter.1

commit v5 on v4

--- a/solution.py
+++ b/solution.py
@@ -39,7 +39,7 @@
     heads = query.shape[1] // HD
     block = min(512, rows)
     count = rows // block
-    highest = lax.Precision.HIGHEST
+    highest = lax.Precision.HIGH
     qa = (
         jax.nn.silu(query.astype(jnp.float32)).astype(jnp.bfloat16).reshape(count, block, heads, HD)
     )

time: 150 us -> 147 us (0.980)
  matrix products: 23.7 us -> 21.3 us
    dot_general x1, matrix products: 6.72 us -> 4.55 us  [per_device(): jnp.einsum('nhts,nshe->nthe', scores, va.astype(jnp.float32), precision=h...]
  transfers between devices with their start and end apart: 7 -> 7, of which waited for: 3 -> 3; matrix products, arithmetic and copies ran while one was open for 8% -> 6% of each run, Pallas kernels for 0% -> 0%
where the time goes in v5:
time: 147 us
  waiting for transfers between devices  85.5 us (58%)
  matrix products  21.3 us (14%)
  between operations  13.6 us (9%)
  starting transfers between devices  12 us (8%)
  other arithmetic  8.1 us (6%)
  local copies, waits for them, and re-layouts  6.29 us (4%)
    reduce_scatter x1, waiting for transfers between devices, per_device(): lax.psum_scatter(jnp.dot(attn, w_out, preferred_element_type=jnp.float32)...  80.9 us
    dot_general x1, matrix products, per_device(): jnp.dot(attn, w_out, preferred_element_type=jnp.float32)  12.5 us
    ppermute x3, starting transfers between devices, exclusive_prefix(): lax.ppermute(row_total.astype(jnp.bfloat16), 'seq', perm)  7.42 us
    ppermute x3, starting transfers between devices, exclusive_prefix(): got = lax.ppermute(sent, 'seq', perm).astype(jnp.float32)  4.61 us
    dot_general x1, matrix products, per_device(): jnp.einsum('nhts,nshe->nthe', scores, va.astype(jnp.float32), precision=h...  4.55 us
    ppermute x3, waiting for transfers between devices, exclusive_prefix(): lax.ppermute(row_total.astype(jnp.bfloat16), 'seq', perm)  4.52 us
  transfers between devices with their start and end apart: 7, of which 3 were waited for; matrix products, arithmetic and copies ran while one was open for 6% of the time, Pallas kernels for 0%

profile of v5, /device:TPU:2, one launch (start us, length us, event | category | flops | bytes accessed | tf_op | source)
XLA Modules:
  0.0 146.7 jit_solution(15896756357884836816)
XLA Ops:
  6.5 1.9 %fusion.7 = bf16[1024,512]{1,0:T(8,128)(2,1)S(1)} fusion(bf16[1024,512]{1,0:T(8,128)(2,1)} %param.8), kind=kLoop, calls=%fused_computation.12 | loop fusion | flops 3145728 | bytes 2097152 | tf_op jit(solution)/shard_map/convert_element_type | solution.py:48
  8.4 0.3 reshape.46
  8.8 0.3 reshape.47
  9.1 0.7 copy.33
  9.7 0.0 copy-start.4
  9.7 2.0 %fusion.30 = (bf16[4,128,128]{2,1,0:T(8,128)(2,1)}, f32[2,4,128,128]{3,2,1,0:T(8,128)}) fusion(bf16[2,512,4,128]{1,3,2,0:T(8,128)(2,1)S(1)} %copy.33, bf16[2,512,4,128]{3,2,1,0:T(4,128)(2,1)S(1)} %reshape.46), kind=kOutput, calls=%fused_computation.47 | convolution fusion | flops 134283264 | bytes 2752512 | tf_op jit(solution)/shard_map/nthd,nthe->nhde/dot_general | solution.py:52
  11.7 3.0 %collective-permute-start.2 = (bf16[4,128,128]{2,1,0:T(8,128)(2,1)}, bf16[4,128,128]{2,1,0:T(8,128)(2,1)S(1)}, u32[]{:S(2)}, u32[]{:S(2)}) collective-permute-start(bf16[4,128,128]{2,1,0:T(8,128)(2,1)} %get-tuple-element.5), channel_id=1, source_target_pairs={{0,48},{16,0},{32,16},{48,32},{64,112},{80,64},{96,80},{112,96},{1... | collective-permute-start | bytes 393224 | tf_op jit(solution)/shard_map/ppermute | solution.py:28
  14.7 0.6 collective-permute-start.1
  15.4 1.0 collective-permute-start
  16.3 0.1 iota_compare_fusion
  16.4 1.6 %fusion.11 = bf16[1024,512]{1,0:T(8,128)(2,1)} fusion(bf16[1024,512]{1,0:T(8,128)(2,1)S(1)} %copy-done.4), kind=kLoop, calls=%fused_computation.16 | loop fusion | flops 3145728 | bytes 2097152 | tf_op jit(solution)/shard_map/convert_element_type | solution.py:44
  18.0 1.3 reshape.48
  19.3 1.3 fusion.16
  20.6 0.0 copy-start.2
  20.6 4.6 %fusion = f32[2,4,512,128]{2,3,1,0:T(8,128)} fusion(bf16[2,512,4,128]{1,3,2,0:T(8,128)(2,1)S(1)} %copy.33, f32[2,4,512,512]{3,2,1,0:T(8,128)S(1)} %fusion.16, pred[512,512]{1,0:T(8,128)(4,1)S(1)} %iota_compare_fusion), kind=kOutput, calls=%fused_computation.1 | convolution fusion | flops 1612709888 | bytes 11796480 | tf_op jit(solution)/shard_map/nhts,nshe->nthe/dot_general | solution.py:63
  25.2 1.3 fusion.27
  26.4 0.7 collective-permute-start.5
  27.1 4.7 %collective-permute-start.4 = (bf16[4,128,128]{2,1,0:T(8,128)(2,1)S(1)}, bf16[4,128,128]{2,1,0:T(8,128)(2,1)S(1)}, u32[]{:S(2)}, u32[]{:S(2)}) collective-permute-start(bf16[4,128,128]{2,1,0:T(8,128)(2,1)S(1)} %fusion.27), channel_id=1, source_target_pairs={{0,128},{16,144},{32,160},{48,176},{64,192},{80,208},{96,224},{112... | collective-permute-start | bytes 393224 | tf_op jit(solution)/shard_map/ppermute | solution.py:33
  31.8 2.1 %collective-permute-start.3 = (bf16[4,128,128]{2,1,0:T(8,128)(2,1)S(1)}, bf16[4,128,128]{2,1,0:T(8,128)(2,1)S(1)}, u32[]{:S(2)}, u32[]{:S(2)}) collective-permute-start(bf16[4,128,128]{2,1,0:T(8,128)(2,1)S(1)} %fusion.27), channel_id=1, source_target_pairs={{0,64},{16,80},{32,96},{48,112},{64,128},{80,144},{96,160},{112,17... | collective-permute-start | bytes 393224 | tf_op jit(solution)/shard_map/ppermute | solution.py:33
  33.9 0.2 reduce-window_subtract_fusion
  34.2 0.1 collective-permute-done.4
  34.3 4.4 %collective-permute-done.3 = bf16[4,128,128]{2,1,0:T(8,128)(2,1)S(1)} collective-permute-done((bf16[4,128,128]{2,1,0:T(8,128)(2,1)S(1)}, bf16[4,128,128]{2,1,0:T(8,128)(2,1)S(1)}, u32[]{:S(2)}, u32[]{:S(2)}) %collective-permute-start.3) | collective-permute-done | bytes 131104 | tf_op jit(solution)/shard_map/ppermute | solution.py:33
  38.7 1.1 fusion.26
  39.8 1.0 multiply_reduce_fusion
  40.8 0.2 copy.35
  41.1 1.9 %copy.34 = f32[2,512,4,128]{3,2,1,0:T(4,128)} copy(f32[2,512,4,128]{1,3,2,0:T(8,128)S(1)} %get-tuple-element.8) | data formatting | bytes 4194304 | tf_op jit(solution)/shard_map/add | solution.py:64
  42.9 1.2 mul.36
  44.2 0.4 copy-done.1
  44.5 1.9 %fusion.13 = bf16[1024,512]{1,0:T(8,128)(2,1)S(1)} fusion(f32[128,8,4,128]{3,2,1,0:T(4,128)S(1)} %bitcast.21, f32[128,8,4,128]{3,2,1,0:T(4,128)S(1)} %bitcast.22, bf16[1024,512]{1,0:T(8,128)(2,1)} %param.10, f32[512]{0:T(512)S(1)} %copy-done.6), kind=kLoop, calls=%fused_computation.19 | loop fusion | flops 4194304 | bytes 6293504 | tf_op jit(solution)/shard_map/convert_element_type | solution.py:67
  46.5 12.5 %convolution_convert_fusion = bf16[1024,6144]{1,0:T(8,128)(2,1)} fusion(bf16[1024,512]{1,0:T(8,128)(2,1)S(1)} %fusion.13, bf16[512,6144]{1,0:T(8,128)(2,1)} %param.13), kind=kOutput, calls=%fused_computation | convolution fusion | flops 6448742400 | bytes 19922944 | tf_op jit(solution)/shard_map/dot_general | solution.py:70
  59.0 0.0 reduce-scatter.2.cloned.1.call-update
  59.0 80.9 %reduce-scatter.2.cloned.1.call-done = bf16[64,6144]{1,0:T(8,128)(2,1)} async-done(((bf16[1024,6144]{1,0:T(8,128)(2,1)}), bf16[64,6144]{1,0:T(8,128)(2,1)}) %reduce-scatter.2.cloned.1.call-update) | async-done | bytes 786448 | tf_op jit(solution)/shard_map/reduce_scatter | solution.py:69
  (17 shorter events, 0.0 us)
Async XLA Ops:
  6.5 2.2 %copy-start.3 = (bf16[1024,512]{1,0:T(8,128)(2,1)S(1)}, bf16[1024,512]{1,0:T(8,128)(2,1)}, u32[]{:S(2)}) copy-start(bf16[1024,512]{1,0:T(8,128)(2,1)} %param.9) | copy-start | bytes 3145732
  6.5 133.4 %reduce-scatter.2.cloned.1.call-start = ((), (), s32[]{:S(2)}) async-start(), calls=%async_computation.1 | async-start | bytes 13369344 | tf_op jit(solution)/shard_map/reduce_scatter | solution.py:69
  9.7 6.7 %copy-start.4 = (bf16[1024,512]{1,0:T(8,128)(2,1)S(1)}, bf16[1024,512]{1,0:T(8,128)(2,1)}, u32[]{:S(2)}) copy-start(bf16[1024,512]{1,0:T(8,128)(2,1)} %param.7) | copy-start | bytes 3145732
  11.7 13.5 %collective-permute-start.2 = (bf16[4,128,128]{2,1,0:T(8,128)(2,1)}, bf16[4,128,128]{2,1,0:T(8,128)(2,1)S(1)}, u32[]{:S(2)}, u32[]{:S(2)}) collective-permute-start(bf16[4,128,128]{2,1,0:T(8,128)(2,1)} %get-tuple-element.5), channel_id=1, source_target_pairs={{0,48},{16,0},{32,16},{48,32},{64,112},{80,64},{96,80},{112,96},{1... | collective-permute-start | bytes 393224 | tf_op jit(solution)/shard_map/ppermute | solution.py:28
  14.7 10.4 %collective-permute-start.1 = (bf16[4,128,128]{2,1,0:T(8,128)(2,1)}, bf16[4,128,128]{2,1,0:T(8,128)(2,1)}, u32[]{:S(2)}, u32[]{:S(2)}) collective-permute-start(bf16[4,128,128]{2,1,0:T(8,128)(2,1)} %get-tuple-element.5), channel_id=1, source_target_pairs={{0,32},{16,48},{32,0},{48,16},{64,96},{80,112},{96,64},{112,80},{1... | collective-permute-start | bytes 393224 | tf_op jit(solution)/shard_map/ppermute | solution.py:28
  15.4 9.8 %collective-permute-start = (bf16[4,128,128]{2,1,0:T(8,128)(2,1)}, bf16[4,128,128]{2,1,0:T(8,128)(2,1)}, u32[]{:S(2)}, u32[]{:S(2)}) collective-permute-start(bf16[4,128,128]{2,1,0:T(8,128)(2,1)} %get-tuple-element.5), channel_id=1, source_target_pairs={{0,16},{16,32},{32,48},{48,0},{64,80},{80,96},{96,112},{112,64},{1... | collective-permute-start | bytes 393224 | tf_op jit(solution)/shard_map/ppermute | solution.py:28
  20.6 13.3 %copy-start.2 = (f32[2,4,128,128]{3,2,1,0:T(8,128)S(1)}, f32[2,4,128,128]{3,2,1,0:T(8,128)}, u32[]{:S(2)}) copy-start(f32[2,4,128,128]{3,2,1,0:T(8,128)} %get-tuple-element.6) | copy-start | bytes 1572868
  25.2 13.5 %copy-start.5 = (f32[4,128,128]{2,1,0:T(8,128)S(1)}, f32[4,128,128]{2,1,0:T(8,128)}, u32[]{:S(2)}) copy-start(f32[4,128,128]{2,1,0:T(8,128)} %param.11) | copy-start | bytes 786436
  25.2 14.6 %copy-start = (f32[2,4,512,128]{2,3,1,0:T(8,128)S(1)}, f32[2,4,512,128]{2,3,1,0:T(8,128)}, u32[]{:S(2)}) copy-start(f32[2,4,512,128]{2,3,1,0:T(8,128)} %fusion) | copy-start | bytes 6291460
  26.4 7.7 %collective-permute-start.5 = (bf16[4,128,128]{2,1,0:T(8,128)(2,1)S(1)}, bf16[4,128,128]{2,1,0:T(8,128)(2,1)S(1)}, u32[]{:S(2)}, u32[]{:S(2)}) collective-permute-start(bf16[4,128,128]{2,1,0:T(8,128)(2,1)S(1)} %fusion.27), channel_id=1, source_target_pairs={{0,192},{16,208},{32,224},{48,240},{1,193},{17,209},{33,225},{49,2... | collective-permute-start | bytes 393224 | tf_op jit(solution)/shard_map/ppermute | solution.py:33
  27.1 7.2 %collective-permute-start.4 = (bf16[4,128,128]{2,1,0:T(8,128)(2,1)S(1)}, bf16[4,128,128]{2,1,0:T(8,128)(2,1)S(1)}, u32[]{:S(2)}, u32[]{:S(2)}) collective-permute-start(bf16[4,128,128]{2,1,0:T(8,128)(2,1)S(1)} %fusion.27), channel_id=1, source_target_pairs={{0,128},{16,144},{32,160},{48,176},{64,192},{80,208},{96,224},{112... | collective-permute-start | bytes 393224 | tf_op jit(solution)/shard_map/ppermute | solution.py:33
  31.8 6.9 %collective-permute-start.3 = (bf16[4,128,128]{2,1,0:T(8,128)(2,1)S(1)}, bf16[4,128,128]{2,1,0:T(8,128)(2,1)S(1)}, u32[]{:S(2)}, u32[]{:S(2)}) collective-permute-start(bf16[4,128,128]{2,1,0:T(8,128)(2,1)S(1)} %fusion.27), channel_id=1, source_target_pairs={{0,64},{16,80},{32,96},{48,112},{64,128},{80,144},{96,160},{112,17... | collective-permute-start | bytes 393224 | tf_op jit(solution)/shard_map/ppermute | solution.py:33
  42.9 1.6 %copy-start.1 = (f32[2,512,4,128]{3,2,1,0:T(4,128)S(1)}, f32[2,512,4,128]{3,2,1,0:T(4,128)}, u32[]{:S(2)}) copy-start(f32[2,512,4,128]{3,2,1,0:T(4,128)} %copy.34) | copy-start | bytes 6291460
  42.9 1.6 %copy-start.6 = (f32[512]{0:T(512)S(1)}, f32[512]{0:T(512)}, u32[]{:S(2)}) copy-start(f32[512]{0:T(512)} %param.12) | copy-start | bytes 6148
Sparse Core Ops, SparseCore 0:
  59.1 80.7 reduce-scatter.1

commit v6 on v5

--- a/solution.py
+++ b/solution.py
@@ -39,32 +39,35 @@
     heads = query.shape[1] // HD
     block = min(512, rows)
     count = rows // block
-    highest = lax.Precision.HIGH
-    qa = (
-        jax.nn.silu(query.astype(jnp.float32)).astype(jnp.bfloat16).reshape(count, block, heads, HD)
-    )
-    ka = (
-        jax.nn.silu(key_in.astype(jnp.float32))
-        .astype(jnp.bfloat16)
-        .reshape(count, block, heads, HD)
-    )
-    va = value.reshape(count, block, heads, HD)
-    block_states = jnp.einsum("nthd,nthe->nhde", ka, va, preferred_element_type=jnp.float32)
-    own_total = jnp.sum(block_states, axis=0)
-    local_before = jnp.cumsum(block_states, axis=0) - block_states
+    high = lax.Precision.HIGH
+    qa = jax.nn.silu(query.astype(jnp.float32)).astype(jnp.bfloat16)
+    ka = jax.nn.silu(key_in.astype(jnp.float32)).astype(jnp.bfloat16)
+
+    def head(x, h):
+        return x[:, h * HD:(h + 1) * HD].reshape(count, block, HD)
+
+    block_states = [
+        jnp.einsum("ntd,nte->nde", head(ka, h), head(value, h), preferred_element_type=jnp.float32)
+        for h in range(heads)
+    ]
+    own_total = jnp.stack([jnp.sum(b, axis=0) for b in block_states])
     gated = norm_gain[None, :] * jax.nn.sigmoid(gate.astype(jnp.float32))
     prior = exclusive_prefix(own_total)
-    states = local_before + (kv_start + prior)[None]
-    q_float = qa.astype(jnp.float32)
-    inter = jnp.einsum("nthd,nhde->nthe", q_float, states, precision=highest)
-    scores = jnp.einsum("nthd,nshd->nhts", qa, ka, preferred_element_type=jnp.float32)
     causal = jnp.arange(block)[:, None] >= jnp.arange(block)[None, :]
-    scores = jnp.where(causal[None, None], scores, jnp.float32(0.0))
-    intra = jnp.einsum("nhts,nshe->nthe", scores, va.astype(jnp.float32), precision=highest)
-    heads_out = (inter + intra).reshape(rows, heads, HD)
-    scale = lax.rsqrt(jnp.mean(heads_out * heads_out, axis=-1, keepdims=True) + 1e-05)
-    normed = (heads_out * scale).reshape(rows, heads * HD)
-    attn = (normed * gated).astype(jnp.bfloat16)
+    normed = []
+    for h in range(heads):
+        q_h = head(qa, h)
+        k_h = head(ka, h)
+        v_h = head(value, h)
+        states = jnp.cumsum(block_states[h], axis=0) - block_states[h] + (kv_start[h] + prior[h])[None]
+        inter = jnp.einsum("ntd,nde->nte", q_h.astype(jnp.float32), states, precision=high)
+        scores = jnp.einsum("ntd,nsd->nts", q_h, k_h, preferred_element_type=jnp.float32)
+        scores = jnp.where(causal[None], scores, jnp.float32(0.0))
+        intra = jnp.einsum("nts,nse->nte", scores, v_h.astype(jnp.float32), precision=high)
+        out_h = (inter + intra).reshape(rows, HD)
+        scale = lax.rsqrt(jnp.mean(out_h * out_h, axis=-1, keepdims=True) + 1e-05)
+        normed.append(out_h * scale)
+    attn = (jnp.concatenate(normed, axis=1) * gated).astype(jnp.bfloat16)
     attn = lax.optimization_barrier(attn)
     return lax.psum_scatter(
         jnp.dot(attn, w_out, preferred_element_type=jnp.float32).astype(jnp.bfloat16),

time: 147 us -> 147 us (level)
  local copies, waits for them, and re-layouts: 6.29 us -> 3.9 us
  matrix products: 21.3 us -> 22.8 us
    dot_general x4 -> x16, matrix products: 8.78 us -> 13.2 us  [the longest x4 5.7 us: per_device(): jnp.einsum('ntd,nsd->nts', q_h, k_h, preferred_element_type=jnp.float32)]
    unnamed x14 -> x44, local copies, waits for them, and re-layouts: 0.39 us -> 3.35 us
    dot_general x1, matrix products: 12.5 us -> 9.59 us  [per_device(): jnp.dot(attn, w_out, preferred_element_type=jnp.float32)]
    ppermute x3, waiting for transfers between devices: 0.01 us -> 2.83 us  [exclusive_prefix(): got = lax.ppermute(sent, 'seq', perm).astype(jnp.float32)]
    reshape x4 -> x0, local copies, waits for them, and re-layouts: 2.59 us -> none  [the longest x1 1.34 us: per_device(): jax.nn.silu(query.astype(jnp.float32)).astype(jnp.bfloat16)]
    convert_element_type x3, other arithmetic: 5.41 us -> 3.07 us  [the longest x1 1.9 us: per_device(): ka = jax.nn.silu(key_in.astype(jnp.float32)).astype(jnp.bfloat16)]
    add x1 -> x0, local copies, waits for them, and re-layouts: 1.88 us -> none  [per_device(): heads_out = (inter + intra).reshape(rows, heads, HD)]
  transfers between devices with their start and end apart: 7 -> 7, of which waited for: 3 -> 4; matrix products, arithmetic and copies ran while one was open for 6% -> 4% of each run, Pallas kernels for 0% -> 0%
where the time goes in v6:
time: 147 us; the launch traced here: 146 us
  waiting for transfers between devices  86.1 us (59%)
  matrix products  22.8 us (16%)
  between operations  13.8 us (9%)
  starting transfers between devices  12.8 us (9%)
  other arithmetic  6.99 us (5%)
  local copies, waits for them, and re-layouts  3.9 us (3%)
    reduce_scatter x1, waiting for transfers between devices, per_device(): lax.psum_scatter(jnp.dot(attn, w_out, preferred_element_type=jnp.float32)...  79.8 us
    dot_general x1, matrix products, per_device(): jnp.dot(attn, w_out, preferred_element_type=jnp.float32)  9.59 us
    ppermute x3, starting transfers between devices, exclusive_prefix(): lax.ppermute(row_total.astype(jnp.bfloat16), 'seq', perm)  8.08 us
    dot_general x4, matrix products, per_device(): jnp.einsum('ntd,nsd->nts', q_h, k_h, preferred_element_type=jnp.float32)  5.7 us
    ppermute x3, starting transfers between devices, exclusive_prefix(): got = lax.ppermute(sent, 'seq', perm).astype(jnp.float32)  4.76 us
    ppermute x3, waiting for transfers between devices, exclusive_prefix(): lax.ppermute(row_total.astype(jnp.bfloat16), 'seq', perm)  3.53 us
    unnamed x44, local copies, waits for them, and re-layouts  3.35 us
    dot_general x4, matrix products, per_device(): jnp.einsum('nts,nse->nte', scores, v_h.astype(jnp.float32), precision=high)  3.29 us
  transfers between devices with their start and end apart: 7, of which 4 were waited for; matrix products, arithmetic and copies ran while one was open for 4% of the time, Pallas kernels for 0%

profile of v6, /device:TPU:2, one launch (start us, length us, event | category | flops | bytes accessed | tf_op | source)
XLA Modules:
  0.0 146.5 jit_solution(9118933839238246063)
XLA Ops:
  6.5 1.9 %fusion.7 = bf16[1024,512]{1,0:T(8,128)(2,1)S(1)} fusion(bf16[1024,512]{1,0:T(8,128)(2,1)} %param.8), kind=kLoop, calls=%fused_computation.12 | loop fusion | flops 3145728 | bytes 2097152 | tf_op jit(solution)/shard_map/convert_element_type | solution.py:44
  9.2 0.9 fusion.61
  10.1 0.9 fusion.58
  11.0 0.9 fusion.59
  12.0 3.1 %collective-permute-start.2 = (bf16[4,128,128]{2,1,0:T(8,128)(2,1)S(1)}, bf16[4,128,128]{2,1,0:T(8,128)(2,1)S(1)}, u32[]{:S(2)}, u32[]{:S(2)}) collective-permute-start(bf16[4,128,128]{2,1,0:T(8,128)(2,1)S(1)} %pad_maximum_fusion), channel_id=1, source_target_pairs={{0,48},{16,0},{32,16},{48,32},{64,112},{80,64},{96,80},{112,96},{1... | collective-permute-start | bytes 393224 | tf_op jit(solution)/shard_map/ppermute | solution.py:28
  15.1 0.6 collective-permute-start.1
  15.7 1.0 collective-permute-start
  16.8 0.6 fusion.3
  17.6 1.7 %fusion.65 = f32[2,512,512]{2,1,0:T(8,128)} fusion(bf16[2,512,128]{2,1,0:T(8,128)(2,1)S(1)} %bitcast.86, bf16[2,512,128]{2,1,0:T(8,128)(2,1)S(1)} %bitcast.109), kind=kOutput, calls=%fused_computation.95 | convolution fusion | flops 134217728 | bytes 2621440 | tf_op jit(solution)/shard_map/ntd,nsd->nts/dot_general | solution.py:64
  19.3 1.8 %fusion.67 = f32[2,512,512]{2,1,0:T(8,128)} fusion(bf16[2,512,128]{2,1,0:T(8,128)(2,1)S(1)} %bitcast.88, bf16[2,512,128]{2,1,0:T(8,128)(2,1)S(1)} %bitcast.107), kind=kOutput, calls=%fused_computation.97 | convolution fusion | flops 134217728 | bytes 2621440 | tf_op jit(solution)/shard_map/ntd,nsd->nts/dot_general | solution.py:64
  21.1 0.4 fusion.63
  21.5 1.4 collective-permute-done.1
  22.9 1.4 collective-permute-done
  24.3 0.7 fusion.46
  25.1 1.3 collective-permute-start.5
  26.4 4.7 %collective-permute-start.4 = (bf16[4,128,128]{2,1,0:T(8,128)(2,1)}, bf16[4,128,128]{2,1,0:T(8,128)(2,1)}, u32[]{:S(2)}, u32[]{:S(2)}) collective-permute-start(bf16[4,128,128]{2,1,0:T(8,128)(2,1)} %fusion.46), channel_id=1, source_target_pairs={{0,128},{16,144},{32,160},{48,176},{64,192},{80,208},{96,224},{112... | collective-permute-start | bytes 393224 | tf_op jit(solution)/shard_map/ppermute | solution.py:33
  31.1 2.1 %collective-permute-start.3 = (bf16[4,128,128]{2,1,0:T(8,128)(2,1)}, bf16[4,128,128]{2,1,0:T(8,128)(2,1)}, u32[]{:S(2)}, u32[]{:S(2)}) collective-permute-start(bf16[4,128,128]{2,1,0:T(8,128)(2,1)} %fusion.46), channel_id=1, source_target_pairs={{0,64},{16,80},{32,96},{48,112},{64,128},{80,144},{96,160},{112,17... | collective-permute-start | bytes 393224 | tf_op jit(solution)/shard_map/ppermute | solution.py:33
  33.2 1.8 %fusion.69 = f32[2,512,512]{2,1,0:T(8,128)} fusion(bf16[2,512,128]{2,1,0:T(8,128)(2,1)S(1)} %bitcast.92, bf16[2,512,128]{2,1,0:T(8,128)(2,1)S(1)} %bitcast.103), kind=kOutput, calls=%fused_computation.99 | convolution fusion | flops 134217728 | bytes 2621440 | tf_op jit(solution)/shard_map/ntd,nsd->nts/dot_general | solution.py:64
  35.1 3.5 %collective-permute-done.3 = bf16[4,128,128]{2,1,0:T(8,128)(2,1)} collective-permute-done((bf16[4,128,128]{2,1,0:T(8,128)(2,1)}, bf16[4,128,128]{2,1,0:T(8,128)(2,1)}, u32[]{:S(2)}, u32[]{:S(2)}) %collective-permute-start.3) | collective-permute-done | bytes 131104 | tf_op jit(solution)/shard_map/ppermute | solution.py:33
  38.6 1.3 fusion.45
  39.9 1.0 fusion.50
  42.3 0.6 copy-done.1
  42.8 0.8 multiply_reduce_fusion.2
  43.7 0.8 multiply_reduce_fusion.1
  44.6 0.8 multiply_reduce_fusion.3
  45.5 0.7 copy-done.2
  46.2 0.8 multiply_reduce_fusion
  47.7 0.5 copy-done.14
  48.2 0.6 fusion.8
  48.8 1.4 copy-done.19
  50.2 9.6 %convolution_convert_fusion = bf16[1024,6144]{1,0:T(8,128)(2,1)} fusion(bf16[1024,512]{1,0:T(8,128)(2,1)S(1)} %fusion.8, bf16[512,6144]{1,0:T(8,128)(2,1)S(1)} %copy-done.19), kind=kOutput, calls=%fused_computation | convolution fusion | flops 6448742400 | bytes 19922944 | tf_op jit(solution)/shard_map/dot_general | solution.py:73
  59.8 79.8 %reduce-scatter.2.cloned.1.call-done = bf16[64,6144]{1,0:T(8,128)(2,1)} async-done(((bf16[1024,6144]{1,0:T(8,128)(2,1)}), bf16[64,6144]{1,0:T(8,128)(2,1)}) %reduce-scatter.2.cloned.1.call-update) | async-done | bytes 786448 | tf_op jit(solution)/shard_map/reduce_scatter | solution.py:72
  (65 shorter events, 3.1 us)
Async XLA Ops:
  6.5 2.1 %copy-start.12 = (bf16[1024,512]{1,0:T(8,128)(2,1)S(1)}, bf16[1024,512]{1,0:T(8,128)(2,1)}, u32[]{:S(2)}) copy-start(bf16[1024,512]{1,0:T(8,128)(2,1)} %param.9) | copy-start | bytes 3145732
  6.5 133.1 %reduce-scatter.2.cloned.1.call-start = ((), (), s32[]{:S(2)}) async-start(), calls=%async_computation.1 | async-start | bytes 13369344 | tf_op jit(solution)/shard_map/reduce_scatter | solution.py:72
  8.6 8.1 %copy-start.13 = (bf16[1024,512]{1,0:T(8,128)(2,1)S(1)}, bf16[1024,512]{1,0:T(8,128)(2,1)}, u32[]{:S(2)}) copy-start(bf16[1024,512]{1,0:T(8,128)(2,1)} %param.7) | copy-start | bytes 3145732
  8.8 6.9 %copy-start.3 = (bf16[1024,128]{1,0:T(8,128)(2,1)}, bf16[1024,128]{1,0:T(8,128)(2,1)S(1)}, u32[]{:S(2)}) copy-start(bf16[1024,128]{1,0:T(8,128)(2,1)S(1)} %get-tuple-element.9) | copy-start | bytes 786436
  8.9 6.9 %copy-start.5 = (bf16[1024,128]{1,0:T(8,128)(2,1)}, bf16[1024,128]{1,0:T(8,128)(2,1)S(1)}, u32[]{:S(2)}) copy-start(bf16[1024,128]{1,0:T(8,128)(2,1)S(1)} %get-tuple-element.12) | copy-start | bytes 786436
  8.9 6.8 %copy-start.7 = (bf16[1024,128]{1,0:T(8,128)(2,1)}, bf16[1024,128]{1,0:T(8,128)(2,1)S(1)}, u32[]{:S(2)}) copy-start(bf16[1024,128]{1,0:T(8,128)(2,1)S(1)} %get-tuple-element.10) | copy-start | bytes 786436
  12.0 9.5 %collective-permute-start.2 = (bf16[4,128,128]{2,1,0:T(8,128)(2,1)S(1)}, bf16[4,128,128]{2,1,0:T(8,128)(2,1)S(1)}, u32[]{:S(2)}, u32[]{:S(2)}) collective-permute-start(bf16[4,128,128]{2,1,0:T(8,128)(2,1)S(1)} %pad_maximum_fusion), channel_id=1, source_target_pairs={{0,48},{16,0},{32,16},{48,32},{64,112},{80,64},{96,80},{112,96},{1... | collective-permute-start | bytes 393224 | tf_op jit(solution)/shard_map/ppermute | solution.py:28
  15.1 7.9 %collective-permute-start.1 = (bf16[4,128,128]{2,1,0:T(8,128)(2,1)S(1)}, bf16[4,128,128]{2,1,0:T(8,128)(2,1)S(1)}, u32[]{:S(2)}, u32[]{:S(2)}) collective-permute-start(bf16[4,128,128]{2,1,0:T(8,128)(2,1)S(1)} %pad_maximum_fusion), channel_id=1, source_target_pairs={{0,32},{16,48},{32,0},{48,16},{64,96},{80,112},{96,64},{112,80},{1... | collective-permute-start | bytes 393224 | tf_op jit(solution)/shard_map/ppermute | solution.py:28
  15.7 8.6 %collective-permute-start = (bf16[4,128,128]{2,1,0:T(8,128)(2,1)S(1)}, bf16[4,128,128]{2,1,0:T(8,128)(2,1)S(1)}, u32[]{:S(2)}, u32[]{:S(2)}) collective-permute-start(bf16[4,128,128]{2,1,0:T(8,128)(2,1)S(1)} %pad_maximum_fusion), channel_id=1, source_target_pairs={{0,16},{16,32},{32,48},{48,0},{64,80},{80,96},{96,112},{112,64},{1... | collective-permute-start | bytes 393224 | tf_op jit(solution)/shard_map/ppermute | solution.py:28
  21.5 13.4 %copy-start.15 = (bf16[4,128,128]{2,1,0:T(8,128)(2,1)}, bf16[4,128,128]{2,1,0:T(8,128)(2,1)S(1)}, u32[]{:S(2)}) copy-start(bf16[4,128,128]{2,1,0:T(8,128)(2,1)S(1)} %collective-permute-done.2) | copy-start | bytes 393220
  22.9 12.0 %copy-start.16 = (bf16[4,128,128]{2,1,0:T(8,128)(2,1)}, bf16[4,128,128]{2,1,0:T(8,128)(2,1)S(1)}, u32[]{:S(2)}) copy-start(bf16[4,128,128]{2,1,0:T(8,128)(2,1)S(1)} %collective-permute-done.1) | copy-start | bytes 393220
  24.3 10.6 %copy-start.17 = (bf16[4,128,128]{2,1,0:T(8,128)(2,1)}, bf16[4,128,128]{2,1,0:T(8,128)(2,1)S(1)}, u32[]{:S(2)}) copy-start(bf16[4,128,128]{2,1,0:T(8,128)(2,1)S(1)} %collective-permute-done) | copy-start | bytes 393220
  25.1 10.0 %collective-permute-start.5 = (bf16[4,128,128]{2,1,0:T(8,128)(2,1)}, bf16[4,128,128]{2,1,0:T(8,128)(2,1)}, u32[]{:S(2)}, u32[]{:S(2)}) collective-permute-start(bf16[4,128,128]{2,1,0:T(8,128)(2,1)} %fusion.46), channel_id=1, source_target_pairs={{0,192},{16,208},{32,224},{48,240},{1,193},{17,209},{33,225},{49,2... | collective-permute-start | bytes 393224 | tf_op jit(solution)/shard_map/ppermute | solution.py:33
  26.4 8.7 %collective-permute-start.4 = (bf16[4,128,128]{2,1,0:T(8,128)(2,1)}, bf16[4,128,128]{2,1,0:T(8,128)(2,1)}, u32[]{:S(2)}, u32[]{:S(2)}) collective-permute-start(bf16[4,128,128]{2,1,0:T(8,128)(2,1)} %fusion.46), channel_id=1, source_target_pairs={{0,128},{16,144},{32,160},{48,176},{64,192},{80,208},{96,224},{112... | collective-permute-start | bytes 393224 | tf_op jit(solution)/shard_map/ppermute | solution.py:33
  31.1 7.5 %collective-permute-start.3 = (bf16[4,128,128]{2,1,0:T(8,128)(2,1)}, bf16[4,128,128]{2,1,0:T(8,128)(2,1)}, u32[]{:S(2)}, u32[]{:S(2)}) collective-permute-start(bf16[4,128,128]{2,1,0:T(8,128)(2,1)} %fusion.46), channel_id=1, source_target_pairs={{0,64},{16,80},{32,96},{48,112},{64,128},{80,144},{96,160},{112,17... | collective-permute-start | bytes 393224 | tf_op jit(solution)/shard_map/ppermute | solution.py:33
  34.9 6.0 %copy-start.11 = (f32[2,128,128]{2,1,0:T(8,128)S(1)}, f32[2,128,128]{2,1,0:T(8,128)}, u32[]{:S(2)}) copy-start(f32[2,128,128]{2,1,0:T(8,128)} %get-tuple-element.22) | copy-start | bytes 393220
  34.9 6.3 %copy-start.9 = (f32[2,128,128]{2,1,0:T(8,128)S(1)}, f32[2,128,128]{2,1,0:T(8,128)}, u32[]{:S(2)}) copy-start(f32[2,128,128]{2,1,0:T(8,128)} %get-tuple-element.28) | copy-start | bytes 393220
  35.0 6.6 %copy-start.10 = (f32[2,128,128]{2,1,0:T(8,128)S(1)}, f32[2,128,128]{2,1,0:T(8,128)}, u32[]{:S(2)}) copy-start(f32[2,128,128]{2,1,0:T(8,128)} %get-tuple-element.24) | copy-start | bytes 393220
  41.2 1.6 %copy-start.1 = (f32[2,512,512]{2,1,0:T(8,128)S(1)}, f32[2,512,512]{2,1,0:T(8,128)}, u32[]{:S(2)}) copy-start(f32[2,512,512]{2,1,0:T(8,128)} %fusion.65) | copy-start | bytes 6291460
  41.2 1.6 %copy-start.8 = (bf16[1024,128]{1,0:T(8,128)(2,1)S(1)}, bf16[1024,128]{1,0:T(8,128)(2,1)}, u32[]{:S(2)}) copy-start(bf16[1024,128]{1,0:T(8,128)(2,1)} %copy-done.7) | copy-start | bytes 786436
  41.9 1.8 %copy-start = (f32[2,512,512]{2,1,0:T(8,128)S(1)}, f32[2,512,512]{2,1,0:T(8,128)}, u32[]{:S(2)}) copy-start(f32[2,512,512]{2,1,0:T(8,128)} %fusion.67) | copy-start | bytes 6291460
  42.0 1.8 %copy-start.6 = (bf16[1024,128]{1,0:T(8,128)(2,1)S(1)}, bf16[1024,128]{1,0:T(8,128)(2,1)}, u32[]{:S(2)}) copy-start(bf16[1024,128]{1,0:T(8,128)(2,1)} %copy-done.5) | copy-start | bytes 786436
  43.7 1.0 copy-start.4
  44.5 1.6 %copy-start.2 = (f32[2,512,512]{2,1,0:T(8,128)S(1)}, f32[2,512,512]{2,1,0:T(8,128)}, u32[]{:S(2)}) copy-start(f32[2,512,512]{2,1,0:T(8,128)} %fusion.69) | copy-start | bytes 6291460
  47.0 1.2 copy-start.14
  47.0 1.2 copy-start.18
  47.4 2.9 %copy-start.19 = (bf16[512,6144]{1,0:T(8,128)(2,1)S(1)}, bf16[512,6144]{1,0:T(8,128)(2,1)}, u32[]{:S(2)}) copy-start(bf16[512,6144]{1,0:T(8,128)(2,1)} %param.13) | copy-start | bytes 18874372
Sparse Core Ops, SparseCore 0:
  60.0 79.5 reduce-scatter.1

commit v7 on v6

--- a/solution.py
+++ b/solution.py
@@ -52,22 +52,28 @@
     ]
     own_total = jnp.stack([jnp.sum(b, axis=0) for b in block_states])
     gated = norm_gain[None, :] * jax.nn.sigmoid(gate.astype(jnp.float32))
-    prior = exclusive_prefix(own_total)
     causal = jnp.arange(block)[:, None] >= jnp.arange(block)[None, :]
-    normed = []
+    early = []
     for h in range(heads):
         q_h = head(qa, h)
         k_h = head(ka, h)
         v_h = head(value, h)
-        states = jnp.cumsum(block_states[h], axis=0) - block_states[h] + (kv_start[h] + prior[h])[None]
+        states = jnp.cumsum(block_states[h], axis=0) - block_states[h] + kv_start[h][None]
         inter = jnp.einsum("ntd,nde->nte", q_h.astype(jnp.float32), states, precision=high)
         scores = jnp.einsum("ntd,nsd->nts", q_h, k_h, preferred_element_type=jnp.float32)
         scores = jnp.where(causal[None], scores, jnp.float32(0.0))
         intra = jnp.einsum("nts,nse->nte", scores, v_h.astype(jnp.float32), precision=high)
-        out_h = (inter + intra).reshape(rows, HD)
-        scale = lax.rsqrt(jnp.mean(out_h * out_h, axis=-1, keepdims=True) + 1e-05)
-        normed.append(out_h * scale)
-    attn = (jnp.concatenate(normed, axis=1) * gated).astype(jnp.bfloat16)
+        early.append((inter + intra).reshape(rows, HD))
+    prior = exclusive_prefix(own_total)
+    late = [
+        early[h] + jnp.dot(qa[:, h * HD:(h + 1) * HD].astype(jnp.float32), prior[h], precision=high)
+        for h in range(heads)
+    ]
+    out = jnp.concatenate(late, axis=1)
+    member = (jnp.arange(heads * HD)[:, None] // HD == jnp.arange(heads)[None, :]).astype(jnp.float32)
+    squares = jnp.dot(out * out, member, precision=high)
+    scale = lax.rsqrt(squares * (1.0 / HD) + 1e-05)
+    attn = (out * jnp.repeat(scale, HD, axis=1) * gated).astype(jnp.bfloat16)
     attn = lax.optimization_barrier(attn)
     return lax.psum_scatter(
         jnp.dot(attn, w_out, preferred_element_type=jnp.float32).astype(jnp.bfloat16),

time: 147 us -> 152 us (1.034)
  local copies, waits for them, and re-layouts: 3.9 us -> 14.5 us
  waiting for transfers between devices: 86.1 us -> 81 us
  matrix products: 22.8 us -> 25 us
  other arithmetic: 6.99 us -> 5.07 us
    reshape x0 -> x7, local copies, waits for them, and re-layouts: none -> 5.71 us  [the longest x4 4.24 us: per_device(): early.append((inter + intra).reshape(rows, HD))]
    ppermute x3, waiting for transfers between devices: 3.53 us -> 0.01 us  [exclusive_prefix(): lax.ppermute(row_total.astype(jnp.bfloat16), 'seq', perm)]
    dot_general x0 -> x5, matrix products: none -> 3.03 us  [the longest x4 2.46 us: per_device(): jnp.dot(qa[:, h * HD:(h + 1) * HD].astype(jnp.float32), prior[h], precisi...]
    dot_general x4, matrix products: 5.7 us -> 2.73 us  [per_device(): jnp.einsum('ntd,nsd->nts', q_h, k_h, preferred_element_type=jnp.float32)]
    unnamed x44 -> x65, local copies, waits for them, and re-layouts: 3.35 us -> 6.21 us
    ppermute x3, waiting for transfers between devices: 2.83 us -> 0.01 us  [exclusive_prefix(): got = lax.ppermute(sent, 'seq', perm).astype(jnp.float32)]
    dot_general x4, matrix products: 3.29 us -> 5.3 us  [per_device(): jnp.einsum('nts,nse->nte', scores, v_h.astype(jnp.float32), precision=high)]
  transfers between devices with their start and end apart: 7 -> 7, of which waited for: 4 -> 1; matrix products, arithmetic and copies ran while one was open for 4% -> 13% of each run, Pallas kernels for 0% -> 0%
where the time goes in v7:
time: 152 us
  waiting for transfers between devices  81 us (53%)
  matrix products  25 us (16%)
  local copies, waits for them, and re-layouts  14.5 us (10%)
  between operations  14 us (9%)
  starting transfers between devices  12 us (8%)
  other arithmetic  5.07 us (3%)
    reduce_scatter x1, waiting for transfers between devices, per_device(): lax.psum_scatter(jnp.dot(attn, w_out, preferred_element_type=jnp.float32)...  81 us
    dot_general x1, matrix products, per_device(): jnp.dot(attn, w_out, preferred_element_type=jnp.float32)  9.69 us
    ppermute x3, starting transfers between devices, exclusive_prefix(): lax.ppermute(row_total.astype(jnp.bfloat16), 'seq', perm)  7.43 us
    unnamed x65, local copies, waits for them, and re-layouts  6.21 us
    dot_general x4, matrix products, per_device(): jnp.einsum('nts,nse->nte', scores, v_h.astype(jnp.float32), precision=high)  5.3 us
    ppermute x3, starting transfers between devices, exclusive_prefix(): got = lax.ppermute(sent, 'seq', perm).astype(jnp.float32)  4.61 us
    reshape x4, local copies, waits for them, and re-layouts, per_device(): early.append((inter + intra).reshape(rows, HD))  4.24 us
    dot_general x4, matrix products, per_device(): jnp.einsum('ntd,nte->nde', head(ka, h), head(value, h), preferred_element...  3.06 us
  transfers between devices with their start and end apart: 7, of which 1 were waited for; matrix products, arithmetic and copies ran while one was open for 13% of the time, Pallas kernels for 0%

profile of v7, /device:TPU:2, one launch (start us, length us, event | category | flops | bytes accessed | tf_op | source)
XLA Modules:
  0.0 151.6 jit_solution(14422633778143179228)
XLA Ops:
  6.5 1.5 copy.21
  8.0 0.6 fusion.7
  10.4 0.9 fusion.78
  11.4 0.9 fusion.75
  12.3 0.9 fusion.76
  13.2 0.7 pad_maximum_fusion.2
  13.9 3.0 %collective-permute-start.2 = (bf16[4,128,128]{2,1,0:T(8,128)(2,1)}, bf16[4,128,128]{2,1,0:T(8,128)(2,1)}, u32[]{:S(2)}, u32[]{:S(2)}) collective-permute-start(bf16[4,128,128]{2,1,0:T(8,128)(2,1)} %pad_maximum_fusion.2), channel_id=1, source_target_pairs={{0,48},{16,0},{32,16},{48,32},{64,112},{80,64},{96,80},{112,96},{1... | collective-permute-start | bytes 393224 | tf_op jit(solution)/shard_map/ppermute | solution.py:28
  16.9 0.6 collective-permute-start.1
  17.6 1.0 collective-permute-start
  18.6 0.7 slice_bitcast_fusion.11
  19.3 1.5 copy.19
  20.8 0.6 fusion.3
  21.4 0.8 fusion.72
  22.8 1.1 copy.42
  23.9 1.4 fusion.86
  28.1 0.7 fusion.23
  28.8 1.5 %fusion.20 = f32[2,512,128]{2,1,0:T(8,128)} fusion(f32[2,512,128]{2,1,0:T(8,128)S(1)} %fusion.79, bf16[2,512,128]{2,1,0:T(8,128)(2,1)S(1)} %bitcast.93, f32[2,512,512]{2,1,0:T(8,128)S(1)} %fusion.80, pred[512,512]{1,0:T(8,128)(4,1)S(1)} %iota_compare_fusion), kind=kOutput, calls=%fused_computation.27 | convolution fusion | flops 403308544 | bytes 3670016 | tf_op jit(solution)/shard_map/nts,nse->nte/dot_general | solution.py:65
  30.4 1.5 %fusion.29 = f32[2,512,128]{2,1,0:T(8,128)} fusion(f32[2,512,128]{2,1,0:T(8,128)S(1)} %fusion.85, bf16[2,512,128]{2,1,0:T(8,128)(2,1)S(1)} %bitcast.91, f32[2,512,512]{2,1,0:T(8,128)S(1)} %fusion.86, pred[512,512]{1,0:T(8,128)(4,1)S(1)} %iota_compare_fusion), kind=kOutput, calls=%fused_computation.30 | convolution fusion | flops 403308544 | bytes 3670016 | tf_op jit(solution)/shard_map/nts,nse->nte/dot_general | solution.py:65
  32.2 1.1 fusion.58
  33.4 0.7 collective-permute-start.5
  34.0 4.7 %collective-permute-start.4 = (bf16[4,128,128]{2,1,0:T(8,128)(2,1)S(1)}, bf16[4,128,128]{2,1,0:T(8,128)(2,1)S(1)}, u32[]{:S(2)}, u32[]{:S(2)}) collective-permute-start(bf16[4,128,128]{2,1,0:T(8,128)(2,1)S(1)} %fusion.58), channel_id=1, source_target_pairs={{0,128},{16,144},{32,160},{48,176},{64,192},{80,208},{96,224},{112... | collective-permute-start | bytes 393224 | tf_op jit(solution)/shard_map/ppermute | solution.py:33
  38.7 2.1 %collective-permute-start.3 = (bf16[4,128,128]{2,1,0:T(8,128)(2,1)S(1)}, bf16[4,128,128]{2,1,0:T(8,128)(2,1)}, u32[]{:S(2)}, u32[]{:S(2)}) collective-permute-start(bf16[4,128,128]{2,1,0:T(8,128)(2,1)S(1)} %fusion.58), channel_id=1, source_target_pairs={{0,64},{16,80},{32,96},{48,112},{64,128},{80,144},{96,160},{112,17... | collective-permute-start | bytes 393224 | tf_op jit(solution)/shard_map/ppermute | solution.py:33
  40.8 1.5 %fusion.26 = f32[2,512,128]{2,1,0:T(8,128)} fusion(f32[2,512,128]{2,1,0:T(8,128)S(1)} %fusion.83, bf16[2,512,128]{2,1,0:T(8,128)(2,1)S(1)} %bitcast.89, f32[2,512,512]{2,1,0:T(8,128)S(1)} %fusion.84, pred[512,512]{1,0:T(8,128)(4,1)S(1)} %iota_compare_fusion), kind=kOutput, calls=%fused_computation.29 | convolution fusion | flops 403308544 | bytes 3670016 | tf_op jit(solution)/shard_map/nts,nse->nte/dot_general | solution.py:65
  42.3 1.5 %copy.37 = bf16[1024,512]{0,1:T(8,128)(2,1)S(1)} copy(bf16[1024,512]{1,0:T(8,128)(2,1)} %param.10) | data formatting | bytes 2097152 | tf_op args[3]
  43.9 1.0 copy.43
  44.9 1.0 copy.30
  45.9 2.0 %copy.47 = f32[1024,128]{0,1:T(8,128)} copy(f32[1024,128]{1,0:T(8,128)} %bitcast.114) | data formatting | bytes 1048576 | tf_op jit(solution)/shard_map/reshape | solution.py:66
  48.2 1.3 fusion.57
  49.5 1.4 convolution_add_fusion.2
  52.9 0.6 fusion.9
  54.0 9.7 %convolution_convert_fusion = bf16[1024,6144]{1,0:T(8,128)(2,1)} fusion(bf16[1024,512]{0,1:T(8,128)(2,1)S(1)} %fusion.9, bf16[512,6144]{1,0:T(8,128)(2,1)S(1)} %bitcast.125), kind=kOutput, calls=%fused_computation | convolution fusion | flops 6448742400 | bytes 19922944 | tf_op jit(solution)/shard_map/dot_general | solution.py:79
  63.7 81.0 %reduce-scatter.2.cloned.1.call-done = bf16[64,6144]{1,0:T(8,128)(2,1)} async-done(((bf16[1024,6144]{1,0:T(8,128)(2,1)}), bf16[64,6144]{1,0:T(8,128)(2,1)}) %reduce-scatter.2.cloned.1.call-update) | async-done | bytes 786448 | tf_op jit(solution)/shard_map/reduce_scatter | solution.py:78
  (99 shorter events, 7.9 us)
Async XLA Ops:
  6.5 138.2 %reduce-scatter.2.cloned.1.call-start = ((), (), s32[]{:S(2)}) async-start(), calls=%async_computation.1 | async-start | bytes 13369344 | tf_op jit(solution)/shard_map/reduce_scatter | solution.py:78
  8.6 1.3 copy-start.14
  8.9 1.5 %copy-start.4 = (bf16[1024,128]{1,0:T(8,128)(2,1)}, bf16[1024,128]{1,0:T(8,128)(2,1)S(1)}, u32[]{:S(2)}) copy-start(bf16[1024,128]{1,0:T(8,128)(2,1)S(1)} %copy.22) | copy-start | bytes 786436
  9.1 2.3 %copy-start.6 = (bf16[1024,128]{1,0:T(8,128)(2,1)}, bf16[1024,128]{1,0:T(8,128)(2,1)S(1)}, u32[]{:S(2)}) copy-start(bf16[1024,128]{1,0:T(8,128)(2,1)S(1)} %copy.28) | copy-start | bytes 786436
  9.3 3.0 %copy-start = (bf16[1024,128]{1,0:T(8,128)(2,1)}, bf16[1024,128]{1,0:T(8,128)(2,1)S(1)}, u32[]{:S(2)}) copy-start(bf16[1024,128]{1,0:T(8,128)(2,1)S(1)} %copy.26) | copy-start | bytes 786436
  9.9 3.3 %copy-start.2 = (bf16[1024,128]{1,0:T(8,128)(2,1)}, bf16[1024,128]{1,0:T(8,128)(2,1)S(1)}, u32[]{:S(2)}) copy-start(bf16[1024,128]{1,0:T(8,128)(2,1)S(1)} %copy.24) | copy-start | bytes 786436
  10.1 8.5 %copy-start.23 = (f32[4,128,128]{2,1,0:T(8,128)S(1)}, f32[4,128,128]{2,1,0:T(8,128)}, u32[]{:S(2)}) copy-start(f32[4,128,128]{2,1,0:T(8,128)} %param.11) | copy-start | bytes 786436
  10.4 7.1 %copy-start.15 = (bf16[128,128]{1,0:T(8,128)(2,1)}, bf16[128,128]{1,0:T(8,128)(2,1)S(1)}, u32[]{:S(2)}) copy-start(bf16[128,128]{1,0:T(8,128)(2,1)S(1)} %get-tuple-element.25) | copy-start | bytes 98308
  11.4 6.2 %copy-start.17 = (bf16[128,128]{1,0:T(8,128)(2,1)}, bf16[128,128]{1,0:T(8,128)(2,1)S(1)}, u32[]{:S(2)}) copy-start(bf16[128,128]{1,0:T(8,128)(2,1)S(1)} %get-tuple-element.27) | copy-start | bytes 98308
  12.3 7.0 %copy-start.19 = (bf16[128,128]{1,0:T(8,128)(2,1)}, bf16[128,128]{1,0:T(8,128)(2,1)S(1)}, u32[]{:S(2)}) copy-start(bf16[128,128]{1,0:T(8,128)(2,1)S(1)} %get-tuple-element.21) | copy-start | bytes 98308
  13.2 6.1 %copy-start.21 = (bf16[128,128]{1,0:T(8,128)(2,1)}, bf16[128,128]{1,0:T(8,128)(2,1)S(1)}, u32[]{:S(2)}) copy-start(bf16[128,128]{1,0:T(8,128)(2,1)S(1)} %get-tuple-element.23) | copy-start | bytes 98308
  13.9 18.3 %collective-permute-start.2 = (bf16[4,128,128]{2,1,0:T(8,128)(2,1)}, bf16[4,128,128]{2,1,0:T(8,128)(2,1)}, u32[]{:S(2)}, u32[]{:S(2)}) collective-permute-start(bf16[4,128,128]{2,1,0:T(8,128)(2,1)} %pad_maximum_fusion.2), channel_id=1, source_target_pairs={{0,48},{16,0},{32,16},{48,32},{64,112},{80,64},{96,80},{112,96},{1... | collective-permute-start | bytes 393224 | tf_op jit(solution)/shard_map/ppermute | solution.py:28
  16.9 15.3 %collective-permute-start.1 = (bf16[4,128,128]{2,1,0:T(8,128)(2,1)}, bf16[4,128,128]{2,1,0:T(8,128)(2,1)}, u32[]{:S(2)}, u32[]{:S(2)}) collective-permute-start(bf16[4,128,128]{2,1,0:T(8,128)(2,1)} %pad_maximum_fusion.2), channel_id=1, source_target_pairs={{0,32},{16,48},{32,0},{48,16},{64,96},{80,112},{96,64},{112,80},{1... | collective-permute-start | bytes 393224 | tf_op jit(solution)/shard_map/ppermute | solution.py:28
  17.6 14.6 %collective-permute-start = (bf16[4,128,128]{2,1,0:T(8,128)(2,1)}, bf16[4,128,128]{2,1,0:T(8,128)(2,1)}, u32[]{:S(2)}, u32[]{:S(2)}) collective-permute-start(bf16[4,128,128]{2,1,0:T(8,128)(2,1)} %pad_maximum_fusion.2), channel_id=1, source_target_pairs={{0,16},{16,32},{32,48},{48,0},{64,80},{80,96},{96,112},{112,64},{1... | collective-permute-start | bytes 393224 | tf_op jit(solution)/shard_map/ppermute | solution.py:28
  23.9 1.5 copy-start.13
  23.9 1.5 copy-start.27
  23.9 1.8 %copy-start.5 = (bf16[1024,128]{1,0:T(8,128)(2,1)S(1)}, bf16[1024,128]{1,0:T(8,128)(2,1)}, u32[]{:S(2)}) copy-start(bf16[1024,128]{1,0:T(8,128)(2,1)} %copy-done.4) | copy-start | bytes 786436
  26.2 1.0 copy-start.25
  26.6 1.0 copy-start.1
  30.3 1.9 %copy-start.16 = (bf16[128,128]{1,0:T(8,128)(2,1)S(1)}, bf16[128,128]{1,0:T(8,128)(2,1)}, u32[]{:S(2)}) copy-start(bf16[128,128]{1,0:T(8,128)(2,1)} %copy-done.15) | copy-start | bytes 98308
  30.3 1.9 %copy-start.18 = (bf16[128,128]{1,0:T(8,128)(2,1)S(1)}, bf16[128,128]{1,0:T(8,128)(2,1)}, u32[]{:S(2)}) copy-start(bf16[128,128]{1,0:T(8,128)(2,1)} %copy-done.17) | copy-start | bytes 98308
  30.3 1.9 %copy-start.20 = (bf16[128,128]{1,0:T(8,128)(2,1)S(1)}, bf16[128,128]{1,0:T(8,128)(2,1)}, u32[]{:S(2)}) copy-start(bf16[128,128]{1,0:T(8,128)(2,1)} %copy-done.19) | copy-start | bytes 98308
  30.3 1.9 %copy-start.22 = (bf16[128,128]{1,0:T(8,128)(2,1)S(1)}, bf16[128,128]{1,0:T(8,128)(2,1)}, u32[]{:S(2)}) copy-start(bf16[128,128]{1,0:T(8,128)(2,1)} %copy-done.21) | copy-start | bytes 98308
  33.4 14.8 %collective-permute-start.5 = (bf16[4,128,128]{2,1,0:T(8,128)(2,1)S(1)}, bf16[4,128,128]{2,1,0:T(8,128)(2,1)S(1)}, u32[]{:S(2)}, u32[]{:S(2)}) collective-permute-start(bf16[4,128,128]{2,1,0:T(8,128)(2,1)S(1)} %fusion.58), channel_id=1, source_target_pairs={{0,192},{16,208},{32,224},{48,240},{1,193},{17,209},{33,225},{49,2... | collective-permute-start | bytes 393224 | tf_op jit(solution)/shard_map/ppermute | solution.py:33
  34.0 14.2 %collective-permute-start.4 = (bf16[4,128,128]{2,1,0:T(8,128)(2,1)S(1)}, bf16[4,128,128]{2,1,0:T(8,128)(2,1)S(1)}, u32[]{:S(2)}, u32[]{:S(2)}) collective-permute-start(bf16[4,128,128]{2,1,0:T(8,128)(2,1)S(1)} %fusion.58), channel_id=1, source_target_pairs={{0,128},{16,144},{32,160},{48,176},{64,192},{80,208},{96,224},{112... | collective-permute-start | bytes 393224 | tf_op jit(solution)/shard_map/ppermute | solution.py:33
  38.7 9.5 %collective-permute-start.3 = (bf16[4,128,128]{2,1,0:T(8,128)(2,1)S(1)}, bf16[4,128,128]{2,1,0:T(8,128)(2,1)}, u32[]{:S(2)}, u32[]{:S(2)}) collective-permute-start(bf16[4,128,128]{2,1,0:T(8,128)(2,1)S(1)} %fusion.58), channel_id=1, source_target_pairs={{0,64},{16,80},{32,96},{48,112},{64,128},{80,144},{96,160},{112,17... | collective-permute-start | bytes 393224 | tf_op jit(solution)/shard_map/ppermute | solution.py:33
  42.3 2.6 %copy-start.7 = (f32[2,512,128]{2,1,0:T(8,128)S(1)}, f32[2,512,128]{2,1,0:T(8,128)}, u32[]{:S(2)}) copy-start(f32[2,512,128]{2,1,0:T(8,128)} %fusion.20) | copy-start | bytes 1572868
  44.9 3.0 %copy-start.8 = (f32[2,512,128]{2,1,0:T(8,128)S(1)}, f32[2,512,128]{2,1,0:T(8,128)}, u32[]{:S(2)}) copy-start(f32[2,512,128]{2,1,0:T(8,128)} %fusion.26) | copy-start | bytes 1572868
  48.1 2.8 %copy-start.9 = (f32[1024,128]{0,1:T(8,128)S(1)}, f32[1024,128]{0,1:T(8,128)}, u32[]{:S(2)}) copy-start(f32[1024,128]{0,1:T(8,128)} %copy.30) | copy-start | bytes 1572868
  48.2 3.1 %copy-start.10 = (f32[1024,128]{0,1:T(8,128)S(1)}, f32[1024,128]{0,1:T(8,128)}, u32[]{:S(2)}) copy-start(f32[1024,128]{0,1:T(8,128)} %copy.47) | copy-start | bytes 1572868
  50.9 2.6 %slice-start = ((s8[6291456]{0:T(1024)(128)(4,1)}), s8[4194304]{0:T(1024)(128)(4,1)S(1)}, s32[]{:S(2)}) async-start(s8[6291456]{0:T(1024)(128)(4,1)} %bitcast.124), calls=%async_computation.2 | async-start | bytes 8388608
  52.0 2.0 %slice-start.1 = ((s8[6291456]{0:T(1024)(128)(4,1)}), s8[2097152]{0:T(1024)(128)(4,1)S(1)}, s32[]{:S(2)}) async-start(s8[6291456]{0:T(1024)(128)(4,1)} %bitcast.124), calls=%async_computation.3 | async-start | bytes 4194304
  (6 other events, 5.5 us)
Sparse Core Ops, SparseCore 0:
  63.9 80.8 reduce-scatter.1

commit v8 on v6

--- a/solution.py
+++ b/solution.py
@@ -46,10 +46,13 @@
     def head(x, h):
         return x[:, h * HD:(h + 1) * HD].reshape(count, block, HD)
 
-    block_states = [
-        jnp.einsum("ntd,nte->nde", head(ka, h), head(value, h), preferred_element_type=jnp.float32)
-        for h in range(heads)
-    ]
+    full_states = jnp.einsum(
+        "ntd,nte->nde",
+        ka.reshape(count, block, heads * HD),
+        value.reshape(count, block, heads * HD),
+        preferred_element_type=jnp.float32,
+    )
+    block_states = [full_states[:, h * HD:(h + 1) * HD, h * HD:(h + 1) * HD] for h in range(heads)]
     own_total = jnp.stack([jnp.sum(b, axis=0) for b in block_states])
     gated = norm_gain[None, :] * jax.nn.sigmoid(gate.astype(jnp.float32))
     prior = exclusive_prefix(own_total)

time: 147 us -> 150 us (1.020)
  other arithmetic: 6.99 us -> 11.7 us
  local copies, waits for them, and re-layouts: 3.9 us -> 2.08 us
  matrix products: 22.8 us -> 24.4 us
    another operation x4, other arithmetic: 0.07 us -> 4.72 us  [per_device(): jnp.cumsum(block_states[h], axis=0) - block_states[h]]
    dot_general x1, matrix products: 9.59 us -> 12.5 us  [per_device(): jnp.dot(attn, w_out, preferred_element_type=jnp.float32)]
    unnamed x44 -> x42, local copies, waits for them, and re-layouts: 3.35 us -> 0.63 us
    dot_general x4 -> x1, matrix products: 3.08 us -> 0.76 us  [per_device(): jnp.einsum('ntd,nte->nde', ka.reshape(count, block, heads * HD), value.re...]
    ppermute x3, waiting for transfers between devices: 2.83 us -> 0.9 us  [exclusive_prefix(): got = lax.ppermute(sent, 'seq', perm).astype(jnp.float32)]
  transfers between devices with their start and end apart: 7 -> 7, of which waited for: 4 -> 3; matrix products, arithmetic and copies ran while one was open for 4% -> 5% of each run, Pallas kernels for 0% -> 0%
where the time goes in v8:
time: 150 us
  waiting for transfers between devices  84.9 us (57%)
  matrix products  24.4 us (16%)
  between operations  13.8 us (9%)
  starting transfers between devices  12.8 us (9%)
  other arithmetic  11.7 us (8%)
  local copies, waits for them, and re-layouts  2.08 us (1%)
    reduce_scatter x1, waiting for transfers between devices, per_device(): lax.psum_scatter(jnp.dot(attn, w_out, preferred_element_type=jnp.float32)...  79.8 us
    dot_general x1, matrix products, per_device(): jnp.dot(attn, w_out, preferred_element_type=jnp.float32)  12.5 us
    ppermute x3, starting transfers between devices, exclusive_prefix(): lax.ppermute(row_total.astype(jnp.bfloat16), 'seq', perm)  8.07 us
    dot_general x4, matrix products, per_device(): jnp.einsum('ntd,nsd->nts', q_h, k_h, preferred_element_type=jnp.float32)  5.7 us
    another operation x4, other arithmetic, per_device(): jnp.cumsum(block_states[h], axis=0) - block_states[h]  4.72 us
    ppermute x3, starting transfers between devices, exclusive_prefix(): got = lax.ppermute(sent, 'seq', perm).astype(jnp.float32)  4.69 us
    ppermute x3, waiting for transfers between devices, exclusive_prefix(): lax.ppermute(row_total.astype(jnp.bfloat16), 'seq', perm)  4.25 us
    dot_general x4, matrix products, per_device(): jnp.einsum('nts,nse->nte', scores, v_h.astype(jnp.float32), precision=high)  3.3 us
  transfers between devices with their start and end apart: 7, of which 3 were waited for; matrix products, arithmetic and copies ran while one was open for 5% of the time, Pallas kernels for 0%

profile of v8, /device:TPU:2, one launch (start us, length us, event | category | flops | bytes accessed | tf_op | source)
XLA Modules:
  0.0 149.7 jit_solution(15881401813417116499)
XLA Ops:
  6.5 1.9 %fusion.7 = bf16[1024,512]{1,0:T(8,128)(2,1)S(1)} fusion(bf16[1024,512]{1,0:T(8,128)(2,1)} %param.8), kind=kLoop, calls=%fused_computation.12 | loop fusion | flops 3145728 | bytes 2097152 | tf_op jit(solution)/shard_map/convert_element_type | solution.py:44
  8.5 0.8 fusion.62
  9.3 3.1 %collective-permute-start.2 = (bf16[4,128,128]{2,1,0:T(8,128)(2,1)S(1)}, bf16[4,128,128]{2,1,0:T(8,128)(2,1)S(1)}, u32[]{:S(2)}, u32[]{:S(2)}) collective-permute-start(bf16[4,128,128]{2,1,0:T(8,128)(2,1)S(1)} %pad_maximum_fusion), channel_id=1, source_target_pairs={{0,48},{16,0},{32,16},{48,32},{64,112},{80,64},{96,80},{112,96},{1... | collective-permute-start | bytes 393224 | tf_op jit(solution)/shard_map/ppermute | solution.py:28
  12.4 0.6 collective-permute-start.1
  13.0 1.0 collective-permute-start
  14.2 0.6 fusion.3
  15.0 1.8 %fusion.70 = f32[2,512,512]{2,1,0:T(8,128)} fusion(bf16[2,512,128]{2,1,0:T(8,128)(2,1)S(1)} %bitcast.84, bf16[2,512,128]{2,1,0:T(8,128)(2,1)S(1)} %bitcast.95), kind=kOutput, calls=%fused_computation.104 | convolution fusion | flops 134217728 | bytes 2621440 | tf_op jit(solution)/shard_map/ntd,nsd->nts/dot_general | solution.py:67
  16.8 1.8 %fusion.64 = f32[2,512,512]{2,1,0:T(8,128)} fusion(bf16[2,512,128]{2,1,0:T(8,128)(2,1)S(1)} %bitcast.86, bf16[2,512,128]{2,1,0:T(8,128)(2,1)S(1)} %bitcast.94), kind=kOutput, calls=%fused_computation.98 | convolution fusion | flops 134217728 | bytes 2621440 | tf_op jit(solution)/shard_map/ntd,nsd->nts/dot_general | solution.py:67
  18.6 1.7 %fusion.68 = f32[2,512,512]{2,1,0:T(8,128)} fusion(bf16[2,512,128]{2,1,0:T(8,128)(2,1)S(1)} %bitcast.80, bf16[2,512,128]{2,1,0:T(8,128)(2,1)S(1)} %bitcast.93), kind=kOutput, calls=%fused_computation.102 | convolution fusion | flops 134217728 | bytes 2621440 | tf_op jit(solution)/shard_map/ntd,nsd->nts/dot_general | solution.py:67
  20.3 0.4 fusion.66
  20.8 0.9 collective-permute-done
  21.7 0.7 fusion.46
  22.4 1.3 collective-permute-start.5
  23.7 4.7 %collective-permute-start.4 = (bf16[4,128,128]{2,1,0:T(8,128)(2,1)}, bf16[4,128,128]{2,1,0:T(8,128)(2,1)}, u32[]{:S(2)}, u32[]{:S(2)}) collective-permute-start(bf16[4,128,128]{2,1,0:T(8,128)(2,1)} %fusion.46), channel_id=1, source_target_pairs={{0,128},{16,144},{32,160},{48,176},{64,192},{80,208},{96,224},{112... | collective-permute-start | bytes 393224 | tf_op jit(solution)/shard_map/ppermute | solution.py:33
  28.4 2.1 %collective-permute-start.3 = (bf16[4,128,128]{2,1,0:T(8,128)(2,1)}, bf16[4,128,128]{2,1,0:T(8,128)(2,1)}, u32[]{:S(2)}, u32[]{:S(2)}) collective-permute-start(bf16[4,128,128]{2,1,0:T(8,128)(2,1)} %fusion.46), channel_id=1, source_target_pairs={{0,64},{16,80},{32,96},{48,112},{64,128},{80,144},{96,160},{112,17... | collective-permute-start | bytes 393224 | tf_op jit(solution)/shard_map/ppermute | solution.py:33
  30.5 1.1 fusion.60
  31.7 4.2 %collective-permute-done.3 = bf16[4,128,128]{2,1,0:T(8,128)(2,1)} collective-permute-done((bf16[4,128,128]{2,1,0:T(8,128)(2,1)}, bf16[4,128,128]{2,1,0:T(8,128)(2,1)}, u32[]{:S(2)}, u32[]{:S(2)}) %collective-permute-start.3) | collective-permute-done | bytes 131104 | tf_op jit(solution)/shard_map/ppermute | solution.py:33
  36.0 1.3 fusion.45
  37.3 1.0 fusion.54
  38.2 1.2 fusion.32
  39.4 1.2 fusion.63
  40.7 0.8 multiply_reduce_fusion.3
  41.6 1.2 fusion.29
  43.1 0.8 multiply_reduce_fusion
  44.0 1.2 fusion.30
  45.2 1.1 fusion.31
  47.0 0.8 multiply_reduce_fusion.1
  47.8 0.8 multiply_reduce_fusion.2
  49.4 0.5 copy-done.11
  49.9 0.6 fusion.8
  50.5 12.5 %convolution_convert_fusion = bf16[1024,6144]{1,0:T(8,128)(2,1)} fusion(bf16[1024,512]{1,0:T(8,128)(2,1)S(1)} %fusion.8, bf16[512,6144]{1,0:T(8,128)(2,1)} %param.13), kind=kOutput, calls=%fused_computation | convolution fusion | flops 6448742400 | bytes 19922944 | tf_op jit(solution)/shard_map/dot_general | solution.py:76
  63.0 79.8 %reduce-scatter.2.cloned.1.call-done = bf16[64,6144]{1,0:T(8,128)(2,1)} async-done(((bf16[1024,6144]{1,0:T(8,128)(2,1)}), bf16[64,6144]{1,0:T(8,128)(2,1)}) %reduce-scatter.2.cloned.1.call-update) | async-done | bytes 786448 | tf_op jit(solution)/shard_map/reduce_scatter | solution.py:75
  (61 shorter events, 2.2 us)
Async XLA Ops:
  6.5 1.9 %copy-start.4 = (bf16[1024,512]{1,0:T(8,128)(2,1)S(1)}, bf16[1024,512]{1,0:T(8,128)(2,1)}, u32[]{:S(2)}) copy-start(bf16[1024,512]{1,0:T(8,128)(2,1)} %param.9) | copy-start | bytes 3145732
  6.5 136.3 %reduce-scatter.2.cloned.1.call-start = ((), (), s32[]{:S(2)}) async-start(), calls=%async_computation.1 | async-start | bytes 13369344 | tf_op jit(solution)/shard_map/reduce_scatter | solution.py:75
  9.2 5.6 %copy-start.3 = (f32[2,512,512]{2,1,0:T(8,128)}, f32[2,512,512]{2,1,0:T(8,128)S(1)}, u32[]{:S(2)}) copy-start(f32[2,512,512]{2,1,0:T(8,128)S(1)} %fusion.62) | copy-start | bytes 6291460
  9.2 5.0 %copy-start.10 = (bf16[1024,512]{1,0:T(8,128)(2,1)S(1)}, bf16[1024,512]{1,0:T(8,128)(2,1)}, u32[]{:S(2)}) copy-start(bf16[1024,512]{1,0:T(8,128)(2,1)} %param.7) | copy-start | bytes 3145732
  9.3 11.4 %collective-permute-start.2 = (bf16[4,128,128]{2,1,0:T(8,128)(2,1)S(1)}, bf16[4,128,128]{2,1,0:T(8,128)(2,1)S(1)}, u32[]{:S(2)}, u32[]{:S(2)}) collective-permute-start(bf16[4,128,128]{2,1,0:T(8,128)(2,1)S(1)} %pad_maximum_fusion), channel_id=1, source_target_pairs={{0,48},{16,0},{32,16},{48,32},{64,112},{80,64},{96,80},{112,96},{1... | collective-permute-start | bytes 393224 | tf_op jit(solution)/shard_map/ppermute | solution.py:28
  12.4 8.4 %collective-permute-start.1 = (bf16[4,128,128]{2,1,0:T(8,128)(2,1)S(1)}, bf16[4,128,128]{2,1,0:T(8,128)(2,1)S(1)}, u32[]{:S(2)}, u32[]{:S(2)}) collective-permute-start(bf16[4,128,128]{2,1,0:T(8,128)(2,1)S(1)} %pad_maximum_fusion), channel_id=1, source_target_pairs={{0,32},{16,48},{32,0},{48,16},{64,96},{80,112},{96,64},{112,80},{1... | collective-permute-start | bytes 393224 | tf_op jit(solution)/shard_map/ppermute | solution.py:28
  13.0 8.6 %collective-permute-start = (bf16[4,128,128]{2,1,0:T(8,128)(2,1)S(1)}, bf16[4,128,128]{2,1,0:T(8,128)(2,1)S(1)}, u32[]{:S(2)}, u32[]{:S(2)}) collective-permute-start(bf16[4,128,128]{2,1,0:T(8,128)(2,1)S(1)} %pad_maximum_fusion), channel_id=1, source_target_pairs={{0,16},{16,32},{32,48},{48,0},{64,80},{80,96},{96,112},{112,64},{1... | collective-permute-start | bytes 393224 | tf_op jit(solution)/shard_map/ppermute | solution.py:28
  15.0 3.6 %copy-start.7 = (bf16[1024,128]{1,0:T(8,128)(2,1)}, bf16[1024,128]{1,0:T(8,128)(2,1)S(1)}, u32[]{:S(2)}) copy-start(bf16[1024,128]{1,0:T(8,128)(2,1)S(1)} %get-tuple-element.18) | copy-start | bytes 786436
  15.0 3.6 %copy-start.9 = (bf16[1024,128]{1,0:T(8,128)(2,1)}, bf16[1024,128]{1,0:T(8,128)(2,1)S(1)}, u32[]{:S(2)}) copy-start(bf16[1024,128]{1,0:T(8,128)(2,1)S(1)} %get-tuple-element.17) | copy-start | bytes 786436
  15.0 5.3 %copy-start.5 = (bf16[1024,128]{1,0:T(8,128)(2,1)}, bf16[1024,128]{1,0:T(8,128)(2,1)S(1)}, u32[]{:S(2)}) copy-start(bf16[1024,128]{1,0:T(8,128)(2,1)S(1)} %get-tuple-element.20) | copy-start | bytes 786436
  20.8 10.8 %copy-start.16 = (bf16[4,128,128]{2,1,0:T(8,128)(2,1)}, bf16[4,128,128]{2,1,0:T(8,128)(2,1)S(1)}, u32[]{:S(2)}) copy-start(bf16[4,128,128]{2,1,0:T(8,128)(2,1)S(1)} %collective-permute-done.1) | copy-start | bytes 393220
  21.7 9.9 %copy-start.17 = (bf16[4,128,128]{2,1,0:T(8,128)(2,1)}, bf16[4,128,128]{2,1,0:T(8,128)(2,1)S(1)}, u32[]{:S(2)}) copy-start(bf16[4,128,128]{2,1,0:T(8,128)(2,1)S(1)} %collective-permute-done) | copy-start | bytes 393220
  22.4 9.3 %collective-permute-start.5 = (bf16[4,128,128]{2,1,0:T(8,128)(2,1)}, bf16[4,128,128]{2,1,0:T(8,128)(2,1)}, u32[]{:S(2)}, u32[]{:S(2)}) collective-permute-start(bf16[4,128,128]{2,1,0:T(8,128)(2,1)} %fusion.46), channel_id=1, source_target_pairs={{0,192},{16,208},{32,224},{48,240},{1,193},{17,209},{33,225},{49,2... | collective-permute-start | bytes 393224 | tf_op jit(solution)/shard_map/ppermute | solution.py:33
  23.7 8.0 %collective-permute-start.4 = (bf16[4,128,128]{2,1,0:T(8,128)(2,1)}, bf16[4,128,128]{2,1,0:T(8,128)(2,1)}, u32[]{:S(2)}, u32[]{:S(2)}) collective-permute-start(bf16[4,128,128]{2,1,0:T(8,128)(2,1)} %fusion.46), channel_id=1, source_target_pairs={{0,128},{16,144},{32,160},{48,176},{64,192},{80,208},{96,224},{112... | collective-permute-start | bytes 393224 | tf_op jit(solution)/shard_map/ppermute | solution.py:33
  28.4 7.6 %collective-permute-start.3 = (bf16[4,128,128]{2,1,0:T(8,128)(2,1)}, bf16[4,128,128]{2,1,0:T(8,128)(2,1)}, u32[]{:S(2)}, u32[]{:S(2)}) collective-permute-start(bf16[4,128,128]{2,1,0:T(8,128)(2,1)} %fusion.46), channel_id=1, source_target_pairs={{0,64},{16,80},{32,96},{48,112},{64,128},{80,144},{96,160},{112,17... | collective-permute-start | bytes 393224 | tf_op jit(solution)/shard_map/ppermute | solution.py:33
  31.6 9.1 %copy-start.15 = (bf16[1024,128]{1,0:T(8,128)(2,1)S(1)}, bf16[1024,128]{1,0:T(8,128)(2,1)}, u32[]{:S(2)}) copy-start(bf16[1024,128]{1,0:T(8,128)(2,1)} %get-tuple-element.13) | copy-start | bytes 786436
  31.6 9.1 %copy-start.2 = (f32[2,512,512]{2,1,0:T(8,128)S(1)}, f32[2,512,512]{2,1,0:T(8,128)}, u32[]{:S(2)}) copy-start(f32[2,512,512]{2,1,0:T(8,128)} %fusion.64) | copy-start | bytes 6291460
  40.7 2.1 %copy-start.8 = (bf16[1024,128]{1,0:T(8,128)(2,1)S(1)}, bf16[1024,128]{1,0:T(8,128)(2,1)}, u32[]{:S(2)}) copy-start(bf16[1024,128]{1,0:T(8,128)(2,1)} %copy-done.7) | copy-start | bytes 786436
  40.7 2.4 %copy-start.1 = (f32[2,512,512]{2,1,0:T(8,128)S(1)}, f32[2,512,512]{2,1,0:T(8,128)}, u32[]{:S(2)}) copy-start(f32[2,512,512]{2,1,0:T(8,128)} %fusion.70) | copy-start | bytes 6291460
  40.7 2.4 %copy-start.14 = (bf16[1024,128]{1,0:T(8,128)(2,1)S(1)}, bf16[1024,128]{1,0:T(8,128)(2,1)}, u32[]{:S(2)}) copy-start(bf16[1024,128]{1,0:T(8,128)(2,1)} %get-tuple-element.15) | copy-start | bytes 786436
  43.1 3.2 %copy-start.6 = (bf16[1024,128]{1,0:T(8,128)(2,1)S(1)}, bf16[1024,128]{1,0:T(8,128)(2,1)}, u32[]{:S(2)}) copy-start(bf16[1024,128]{1,0:T(8,128)(2,1)} %copy-done.5) | copy-start | bytes 786436
  44.0 3.0 %copy-start = (f32[2,512,512]{2,1,0:T(8,128)S(1)}, f32[2,512,512]{2,1,0:T(8,128)}, u32[]{:S(2)}) copy-start(f32[2,512,512]{2,1,0:T(8,128)} %fusion.68) | copy-start | bytes 6291460
  44.0 3.0 %copy-start.13 = (bf16[1024,128]{1,0:T(8,128)(2,1)S(1)}, bf16[1024,128]{1,0:T(8,128)(2,1)}, u32[]{:S(2)}) copy-start(bf16[1024,128]{1,0:T(8,128)(2,1)} %get-tuple-element.16) | copy-start | bytes 786436
  46.6 1.2 copy-start.12
  48.7 1.2 copy-start.11
  48.7 1.2 copy-start.18
Sparse Core Ops, SparseCore 0:
  63.2 79.6 reduce-scatter.1

commit v9 on v6

--- a/solution.py
+++ b/solution.py
@@ -28,9 +28,11 @@
         got = lax.ppermute(sent, "seq", perm).astype(jnp.float32)
         row_total = row_total + got
         before = before + jnp.where(k <= along, got, jnp.float32(0.0))
+    row = index // r
     for k in range(1, rows):
-        perm = [(a * r + b, (a + k) * r + b) for a in range(rows - k) for b in range(r)]
-        before = before + lax.ppermute(row_total.astype(jnp.bfloat16), "seq", perm).astype(jnp.float32)
+        perm = [(a * r + b, ((a + k) % rows) * r + b) for a in range(rows) for b in range(r)]
+        got = lax.ppermute(row_total.astype(jnp.bfloat16), "seq", perm).astype(jnp.float32)
+        before = before + jnp.where(k <= row, got, jnp.float32(0.0))
     return before
 
 

time: 147 us -> 144 us (0.980)
  starting transfers between devices: 12.8 us -> 9.53 us
    ppermute x3, starting transfers between devices: 8.08 us -> 4.77 us  [exclusive_prefix(): lax.ppermute(row_total.astype(jnp.bfloat16), 'seq', perm)]
  transfers between devices with their start and end apart: 7 -> 7, of which waited for: 4 -> 5; matrix products, arithmetic and copies ran while one was open for 4% -> 5% of each run, Pallas kernels for 0% -> 0%
where the time goes in v9:
time: 144 us; the launch traced here: 143 us
  waiting for transfers between devices  86.2 us (60%)
  matrix products  22.8 us (16%)
  between operations  13.7 us (10%)
  starting transfers between devices  9.53 us (7%)
  other arithmetic  7.02 us (5%)
  local copies, waits for them, and re-layouts  3.9 us (3%)
    reduce_scatter x1, waiting for transfers between devices, per_device(): lax.psum_scatter(jnp.dot(attn, w_out, preferred_element_type=jnp.float32)...  79.8 us
    dot_general x1, matrix products, per_device(): jnp.dot(attn, w_out, preferred_element_type=jnp.float32)  9.59 us
    dot_general x4, matrix products, per_device(): jnp.einsum('ntd,nsd->nts', q_h, k_h, preferred_element_type=jnp.float32)  5.7 us
    ppermute x3, starting transfers between devices, exclusive_prefix(): lax.ppermute(row_total.astype(jnp.bfloat16), 'seq', perm)  4.77 us
    ppermute x3, starting transfers between devices, exclusive_prefix(): got = lax.ppermute(sent, 'seq', perm).astype(jnp.float32)  4.76 us
    ppermute x3, waiting for transfers between devices, exclusive_prefix(): lax.ppermute(row_total.astype(jnp.bfloat16), 'seq', perm)  3.54 us
    unnamed x44, local copies, waits for them, and re-layouts  3.35 us
    dot_general x4, matrix products, per_device(): jnp.einsum('nts,nse->nte', scores, v_h.astype(jnp.float32), precision=high)  3.29 us
  transfers between devices with their start and end apart: 7, of which 5 were waited for; matrix products, arithmetic and copies ran while one was open for 5% of the time, Pallas kernels for 0%

profile of v9, /device:TPU:2, one launch (start us, length us, event | category | flops | bytes accessed | tf_op | source)
XLA Modules:
  0.0 143.2 jit_solution(8712418236285875540)
XLA Ops:
  6.5 1.9 %fusion.7 = bf16[1024,512]{1,0:T(8,128)(2,1)S(1)} fusion(bf16[1024,512]{1,0:T(8,128)(2,1)} %param.8), kind=kLoop, calls=%fused_computation.12 | loop fusion | flops 3145728 | bytes 2097152 | tf_op jit(solution)/shard_map/convert_element_type | solution.py:46
  9.2 0.9 fusion.61
  10.1 0.9 fusion.58
  11.0 0.9 fusion.59
  12.0 3.1 %collective-permute-start.2 = (bf16[4,128,128]{2,1,0:T(8,128)(2,1)S(1)}, bf16[4,128,128]{2,1,0:T(8,128)(2,1)S(1)}, u32[]{:S(2)}, u32[]{:S(2)}) collective-permute-start(bf16[4,128,128]{2,1,0:T(8,128)(2,1)S(1)} %pad_maximum_fusion), channel_id=1, source_target_pairs={{0,48},{16,0},{32,16},{48,32},{64,112},{80,64},{96,80},{112,96},{1... | collective-permute-start | bytes 393224 | tf_op jit(solution)/shard_map/ppermute | solution.py:28
  15.1 0.6 collective-permute-start.1
  15.7 1.0 collective-permute-start
  16.8 0.6 fusion.3
  17.6 1.7 %fusion.65 = f32[2,512,512]{2,1,0:T(8,128)} fusion(bf16[2,512,128]{2,1,0:T(8,128)(2,1)S(1)} %bitcast.86, bf16[2,512,128]{2,1,0:T(8,128)(2,1)S(1)} %bitcast.109), kind=kOutput, calls=%fused_computation.95 | convolution fusion | flops 134217728 | bytes 2621440 | tf_op jit(solution)/shard_map/ntd,nsd->nts/dot_general | solution.py:66
  19.3 1.8 %fusion.67 = f32[2,512,512]{2,1,0:T(8,128)} fusion(bf16[2,512,128]{2,1,0:T(8,128)(2,1)S(1)} %bitcast.88, bf16[2,512,128]{2,1,0:T(8,128)(2,1)S(1)} %bitcast.107), kind=kOutput, calls=%fused_computation.97 | convolution fusion | flops 134217728 | bytes 2621440 | tf_op jit(solution)/shard_map/ntd,nsd->nts/dot_general | solution.py:66
  21.5 1.4 collective-permute-done.1
  22.9 1.4 collective-permute-done
  24.3 0.7 fusion.46
  25.1 0.5 collective-permute-start.5
  25.6 2.4 %collective-permute-start.4 = (bf16[4,128,128]{2,1,0:T(8,128)(2,1)}, bf16[4,128,128]{2,1,0:T(8,128)(2,1)}, u32[]{:S(2)}, u32[]{:S(2)}) collective-permute-start(bf16[4,128,128]{2,1,0:T(8,128)(2,1)} %fusion.46), channel_id=1, source_target_pairs={{0,128},{16,144},{32,160},{48,176},{64,192},{80,208},{96,224},{112... | collective-permute-start | bytes 393224 | tf_op jit(solution)/shard_map/ppermute | solution.py:34
  28.0 1.8 %collective-permute-start.3 = (bf16[4,128,128]{2,1,0:T(8,128)(2,1)}, bf16[4,128,128]{2,1,0:T(8,128)(2,1)}, u32[]{:S(2)}, u32[]{:S(2)}) collective-permute-start(bf16[4,128,128]{2,1,0:T(8,128)(2,1)} %fusion.46), channel_id=1, source_target_pairs={{0,64},{16,80},{32,96},{48,112},{64,128},{80,144},{96,160},{112,17... | collective-permute-start | bytes 393224 | tf_op jit(solution)/shard_map/ppermute | solution.py:34
  29.8 1.8 %fusion.69 = f32[2,512,512]{2,1,0:T(8,128)} fusion(bf16[2,512,128]{2,1,0:T(8,128)(2,1)S(1)} %bitcast.92, bf16[2,512,128]{2,1,0:T(8,128)(2,1)S(1)} %bitcast.103), kind=kOutput, calls=%fused_computation.99 | convolution fusion | flops 134217728 | bytes 2621440 | tf_op jit(solution)/shard_map/ntd,nsd->nts/dot_general | solution.py:66
  31.7 2.7 %collective-permute-done.4 = bf16[4,128,128]{2,1,0:T(8,128)(2,1)} collective-permute-done((bf16[4,128,128]{2,1,0:T(8,128)(2,1)}, bf16[4,128,128]{2,1,0:T(8,128)(2,1)}, u32[]{:S(2)}, u32[]{:S(2)}) %collective-permute-start.4) | collective-permute-done | bytes 131104 | tf_op jit(solution)/shard_map/ppermute | solution.py:34
  34.4 0.8 collective-permute-done.3
  35.3 1.4 fusion.45
  36.6 1.0 fusion.50
  39.0 0.6 copy-done.1
  39.5 0.8 multiply_reduce_fusion.2
  40.4 0.8 multiply_reduce_fusion.1
  41.3 0.8 multiply_reduce_fusion.3
  42.2 0.7 copy-done.2
  42.9 0.8 multiply_reduce_fusion
  44.4 0.5 copy-done.14
  45.0 0.6 fusion.8
  45.5 1.4 copy-done.19
  47.0 9.6 %convolution_convert_fusion = bf16[1024,6144]{1,0:T(8,128)(2,1)} fusion(bf16[1024,512]{1,0:T(8,128)(2,1)S(1)} %fusion.8, bf16[512,6144]{1,0:T(8,128)(2,1)S(1)} %copy-done.19), kind=kOutput, calls=%fused_computation | convolution fusion | flops 6448742400 | bytes 19922944 | tf_op jit(solution)/shard_map/dot_general | solution.py:75
  56.6 79.8 %reduce-scatter.2.cloned.1.call-done = bf16[64,6144]{1,0:T(8,128)(2,1)} async-done(((bf16[1024,6144]{1,0:T(8,128)(2,1)}), bf16[64,6144]{1,0:T(8,128)(2,1)}) %reduce-scatter.2.cloned.1.call-update) | async-done | bytes 786448 | tf_op jit(solution)/shard_map/reduce_scatter | solution.py:74
  (65 shorter events, 3.5 us)
Async XLA Ops:
  6.5 2.1 %copy-start.12 = (bf16[1024,512]{1,0:T(8,128)(2,1)S(1)}, bf16[1024,512]{1,0:T(8,128)(2,1)}, u32[]{:S(2)}) copy-start(bf16[1024,512]{1,0:T(8,128)(2,1)} %param.9) | copy-start | bytes 3145732
  6.5 129.8 %reduce-scatter.2.cloned.1.call-start = ((), (), s32[]{:S(2)}) async-start(), calls=%async_computation.1 | async-start | bytes 13369344 | tf_op jit(solution)/shard_map/reduce_scatter | solution.py:74
  8.6 8.1 %copy-start.13 = (bf16[1024,512]{1,0:T(8,128)(2,1)S(1)}, bf16[1024,512]{1,0:T(8,128)(2,1)}, u32[]{:S(2)}) copy-start(bf16[1024,512]{1,0:T(8,128)(2,1)} %param.7) | copy-start | bytes 3145732
  8.8 6.9 %copy-start.3 = (bf16[1024,128]{1,0:T(8,128)(2,1)}, bf16[1024,128]{1,0:T(8,128)(2,1)S(1)}, u32[]{:S(2)}) copy-start(bf16[1024,128]{1,0:T(8,128)(2,1)S(1)} %get-tuple-element.9) | copy-start | bytes 786436
  8.9 6.9 %copy-start.5 = (bf16[1024,128]{1,0:T(8,128)(2,1)}, bf16[1024,128]{1,0:T(8,128)(2,1)S(1)}, u32[]{:S(2)}) copy-start(bf16[1024,128]{1,0:T(8,128)(2,1)S(1)} %get-tuple-element.12) | copy-start | bytes 786436
  8.9 6.8 %copy-start.7 = (bf16[1024,128]{1,0:T(8,128)(2,1)}, bf16[1024,128]{1,0:T(8,128)(2,1)S(1)}, u32[]{:S(2)}) copy-start(bf16[1024,128]{1,0:T(8,128)(2,1)S(1)} %get-tuple-element.10) | copy-start | bytes 786436
  12.0 9.5 %collective-permute-start.2 = (bf16[4,128,128]{2,1,0:T(8,128)(2,1)S(1)}, bf16[4,128,128]{2,1,0:T(8,128)(2,1)S(1)}, u32[]{:S(2)}, u32[]{:S(2)}) collective-permute-start(bf16[4,128,128]{2,1,0:T(8,128)(2,1)S(1)} %pad_maximum_fusion), channel_id=1, source_target_pairs={{0,48},{16,0},{32,16},{48,32},{64,112},{80,64},{96,80},{112,96},{1... | collective-permute-start | bytes 393224 | tf_op jit(solution)/shard_map/ppermute | solution.py:28
  15.1 7.9 %collective-permute-start.1 = (bf16[4,128,128]{2,1,0:T(8,128)(2,1)S(1)}, bf16[4,128,128]{2,1,0:T(8,128)(2,1)S(1)}, u32[]{:S(2)}, u32[]{:S(2)}) collective-permute-start(bf16[4,128,128]{2,1,0:T(8,128)(2,1)S(1)} %pad_maximum_fusion), channel_id=1, source_target_pairs={{0,32},{16,48},{32,0},{48,16},{64,96},{80,112},{96,64},{112,80},{1... | collective-permute-start | bytes 393224 | tf_op jit(solution)/shard_map/ppermute | solution.py:28
  15.7 8.6 %collective-permute-start = (bf16[4,128,128]{2,1,0:T(8,128)(2,1)S(1)}, bf16[4,128,128]{2,1,0:T(8,128)(2,1)S(1)}, u32[]{:S(2)}, u32[]{:S(2)}) collective-permute-start(bf16[4,128,128]{2,1,0:T(8,128)(2,1)S(1)} %pad_maximum_fusion), channel_id=1, source_target_pairs={{0,16},{16,32},{32,48},{48,0},{64,80},{80,96},{96,112},{112,64},{1... | collective-permute-start | bytes 393224 | tf_op jit(solution)/shard_map/ppermute | solution.py:28
  21.5 10.1 %copy-start.15 = (bf16[4,128,128]{2,1,0:T(8,128)(2,1)}, bf16[4,128,128]{2,1,0:T(8,128)(2,1)S(1)}, u32[]{:S(2)}) copy-start(bf16[4,128,128]{2,1,0:T(8,128)(2,1)S(1)} %collective-permute-done.2) | copy-start | bytes 393220
  22.9 8.7 %copy-start.16 = (bf16[4,128,128]{2,1,0:T(8,128)(2,1)}, bf16[4,128,128]{2,1,0:T(8,128)(2,1)S(1)}, u32[]{:S(2)}) copy-start(bf16[4,128,128]{2,1,0:T(8,128)(2,1)S(1)} %collective-permute-done.1) | copy-start | bytes 393220
  24.3 7.3 %copy-start.17 = (bf16[4,128,128]{2,1,0:T(8,128)(2,1)}, bf16[4,128,128]{2,1,0:T(8,128)(2,1)S(1)}, u32[]{:S(2)}) copy-start(bf16[4,128,128]{2,1,0:T(8,128)(2,1)S(1)} %collective-permute-done) | copy-start | bytes 393220
  25.1 6.7 %collective-permute-start.5 = (bf16[4,128,128]{2,1,0:T(8,128)(2,1)}, bf16[4,128,128]{2,1,0:T(8,128)(2,1)}, u32[]{:S(2)}, u32[]{:S(2)}) collective-permute-start(bf16[4,128,128]{2,1,0:T(8,128)(2,1)} %fusion.46), channel_id=1, source_target_pairs={{0,192},{16,208},{32,224},{48,240},{64,0},{80,16},{96,32},{112,48}... | collective-permute-start | bytes 393224 | tf_op jit(solution)/shard_map/ppermute | solution.py:34
  25.6 8.8 %collective-permute-start.4 = (bf16[4,128,128]{2,1,0:T(8,128)(2,1)}, bf16[4,128,128]{2,1,0:T(8,128)(2,1)}, u32[]{:S(2)}, u32[]{:S(2)}) collective-permute-start(bf16[4,128,128]{2,1,0:T(8,128)(2,1)} %fusion.46), channel_id=1, source_target_pairs={{0,128},{16,144},{32,160},{48,176},{64,192},{80,208},{96,224},{112... | collective-permute-start | bytes 393224 | tf_op jit(solution)/shard_map/ppermute | solution.py:34
  28.0 7.2 %collective-permute-start.3 = (bf16[4,128,128]{2,1,0:T(8,128)(2,1)}, bf16[4,128,128]{2,1,0:T(8,128)(2,1)}, u32[]{:S(2)}, u32[]{:S(2)}) collective-permute-start(bf16[4,128,128]{2,1,0:T(8,128)(2,1)} %fusion.46), channel_id=1, source_target_pairs={{0,64},{16,80},{32,96},{48,112},{64,128},{80,144},{96,160},{112,17... | collective-permute-start | bytes 393224 | tf_op jit(solution)/shard_map/ppermute | solution.py:34
  31.6 6.0 %copy-start.11 = (f32[2,128,128]{2,1,0:T(8,128)S(1)}, f32[2,128,128]{2,1,0:T(8,128)}, u32[]{:S(2)}) copy-start(f32[2,128,128]{2,1,0:T(8,128)} %get-tuple-element.22) | copy-start | bytes 393220
  31.6 6.3 %copy-start.9 = (f32[2,128,128]{2,1,0:T(8,128)S(1)}, f32[2,128,128]{2,1,0:T(8,128)}, u32[]{:S(2)}) copy-start(f32[2,128,128]{2,1,0:T(8,128)} %get-tuple-element.28) | copy-start | bytes 393220
  31.7 6.6 %copy-start.10 = (f32[2,128,128]{2,1,0:T(8,128)S(1)}, f32[2,128,128]{2,1,0:T(8,128)}, u32[]{:S(2)}) copy-start(f32[2,128,128]{2,1,0:T(8,128)} %get-tuple-element.24) | copy-start | bytes 393220
  37.9 1.6 %copy-start.1 = (f32[2,512,512]{2,1,0:T(8,128)S(1)}, f32[2,512,512]{2,1,0:T(8,128)}, u32[]{:S(2)}) copy-start(f32[2,512,512]{2,1,0:T(8,128)} %fusion.65) | copy-start | bytes 6291460
  38.0 1.6 %copy-start.8 = (bf16[1024,128]{1,0:T(8,128)(2,1)S(1)}, bf16[1024,128]{1,0:T(8,128)(2,1)}, u32[]{:S(2)}) copy-start(bf16[1024,128]{1,0:T(8,128)(2,1)} %copy-done.7) | copy-start | bytes 786436
  38.7 1.8 %copy-start = (f32[2,512,512]{2,1,0:T(8,128)S(1)}, f32[2,512,512]{2,1,0:T(8,128)}, u32[]{:S(2)}) copy-start(f32[2,512,512]{2,1,0:T(8,128)} %fusion.67) | copy-start | bytes 6291460
  38.7 1.8 %copy-start.6 = (bf16[1024,128]{1,0:T(8,128)(2,1)S(1)}, bf16[1024,128]{1,0:T(8,128)(2,1)}, u32[]{:S(2)}) copy-start(bf16[1024,128]{1,0:T(8,128)(2,1)} %copy-done.5) | copy-start | bytes 786436
  40.4 1.0 copy-start.4
  41.3 1.6 %copy-start.2 = (f32[2,512,512]{2,1,0:T(8,128)S(1)}, f32[2,512,512]{2,1,0:T(8,128)}, u32[]{:S(2)}) copy-start(f32[2,512,512]{2,1,0:T(8,128)} %fusion.69) | copy-start | bytes 6291460
  43.7 1.2 copy-start.14
  43.7 1.2 copy-start.18
  44.1 2.9 %copy-start.19 = (bf16[512,6144]{1,0:T(8,128)(2,1)S(1)}, bf16[512,6144]{1,0:T(8,128)(2,1)}, u32[]{:S(2)}) copy-start(bf16[512,6144]{1,0:T(8,128)(2,1)} %param.13) | copy-start | bytes 18874372
Sparse Core Ops, SparseCore 0:
  56.7 79.6 reduce-scatter.1

commit v10 on v8

--- a/solution.py
+++ b/solution.py
@@ -28,9 +28,11 @@
         got = lax.ppermute(sent, "seq", perm).astype(jnp.float32)
         row_total = row_total + got
         before = before + jnp.where(k <= along, got, jnp.float32(0.0))
+    row = index // r
     for k in range(1, rows):
-        perm = [(a * r + b, (a + k) * r + b) for a in range(rows - k) for b in range(r)]
-        before = before + lax.ppermute(row_total.astype(jnp.bfloat16), "seq", perm).astype(jnp.float32)
+        perm = [(a * r + b, ((a + k) % rows) * r + b) for a in range(rows) for b in range(r)]
+        got = lax.ppermute(row_total.astype(jnp.bfloat16), "seq", perm).astype(jnp.float32)
+        before = before + jnp.where(k <= row, got, jnp.float32(0.0))
     return before
 
 

time: 150 us -> 147 us (0.980)
  starting transfers between devices: 12.8 us -> 9.45 us
    ppermute x3, starting transfers between devices: 8.07 us -> 4.76 us  [exclusive_prefix(): lax.ppermute(row_total.astype(jnp.bfloat16), 'seq', perm)]
  transfers between devices with their start and end apart: 7 -> 7, of which waited for: 3 -> 4; matrix products, arithmetic and copies ran while one was open for 5% -> 5% of each run, Pallas kernels for 0% -> 0%
where the time goes in v10:
time: 147 us; the launch traced here: 146 us
  waiting for transfers between devices  85 us (58%)
  matrix products  24.4 us (17%)
  between operations  13.8 us (9%)
  other arithmetic  11.7 us (8%)
  starting transfers between devices  9.45 us (6%)
  local copies, waits for them, and re-layouts  2.08 us (1%)
    reduce_scatter x1, waiting for transfers between devices, per_device(): lax.psum_scatter(jnp.dot(attn, w_out, preferred_element_type=jnp.float32)...  79.8 us
    dot_general x1, matrix products, per_device(): jnp.dot(attn, w_out, preferred_element_type=jnp.float32)  12.5 us
    dot_general x4, matrix products, per_device(): jnp.einsum('ntd,nsd->nts', q_h, k_h, preferred_element_type=jnp.float32)  5.7 us
    ppermute x3, starting transfers between devices, exclusive_prefix(): lax.ppermute(row_total.astype(jnp.bfloat16), 'seq', perm)  4.76 us
    another operation x4, other arithmetic, per_device(): jnp.cumsum(block_states[h], axis=0) - block_states[h]  4.72 us
    ppermute x3, starting transfers between devices, exclusive_prefix(): got = lax.ppermute(sent, 'seq', perm).astype(jnp.float32)  4.69 us
    ppermute x3, waiting for transfers between devices, exclusive_prefix(): lax.ppermute(row_total.astype(jnp.bfloat16), 'seq', perm)  4.25 us
    dot_general x4, matrix products, per_device(): jnp.einsum('nts,nse->nte', scores, v_h.astype(jnp.float32), precision=high)  3.3 us
  transfers between devices with their start and end apart: 7, of which 4 were waited for; matrix products, arithmetic and copies ran while one was open for 5% of the time, Pallas kernels for 0%

profile of v10, /device:TPU:2, one launch (start us, length us, event | category | flops | bytes accessed | tf_op | source)
XLA Modules:
  0.0 146.4 jit_solution(2928089613801514900)
XLA Ops:
  6.5 1.9 %fusion.7 = bf16[1024,512]{1,0:T(8,128)(2,1)S(1)} fusion(bf16[1024,512]{1,0:T(8,128)(2,1)} %param.8), kind=kLoop, calls=%fused_computation.12 | loop fusion | flops 3145728 | bytes 2097152 | tf_op jit(solution)/shard_map/convert_element_type | solution.py:46
  8.5 0.8 fusion.62
  9.3 3.1 %collective-permute-start.2 = (bf16[4,128,128]{2,1,0:T(8,128)(2,1)S(1)}, bf16[4,128,128]{2,1,0:T(8,128)(2,1)S(1)}, u32[]{:S(2)}, u32[]{:S(2)}) collective-permute-start(bf16[4,128,128]{2,1,0:T(8,128)(2,1)S(1)} %pad_maximum_fusion), channel_id=1, source_target_pairs={{0,48},{16,0},{32,16},{48,32},{64,112},{80,64},{96,80},{112,96},{1... | collective-permute-start | bytes 393224 | tf_op jit(solution)/shard_map/ppermute | solution.py:28
  12.4 0.6 collective-permute-start.1
  13.0 1.0 collective-permute-start
  14.2 0.6 fusion.3
  15.0 1.8 %fusion.70 = f32[2,512,512]{2,1,0:T(8,128)} fusion(bf16[2,512,128]{2,1,0:T(8,128)(2,1)S(1)} %bitcast.84, bf16[2,512,128]{2,1,0:T(8,128)(2,1)S(1)} %bitcast.95), kind=kOutput, calls=%fused_computation.104 | convolution fusion | flops 134217728 | bytes 2621440 | tf_op jit(solution)/shard_map/ntd,nsd->nts/dot_general | solution.py:69
  16.8 1.8 %fusion.64 = f32[2,512,512]{2,1,0:T(8,128)} fusion(bf16[2,512,128]{2,1,0:T(8,128)(2,1)S(1)} %bitcast.86, bf16[2,512,128]{2,1,0:T(8,128)(2,1)S(1)} %bitcast.94), kind=kOutput, calls=%fused_computation.98 | convolution fusion | flops 134217728 | bytes 2621440 | tf_op jit(solution)/shard_map/ntd,nsd->nts/dot_general | solution.py:69
  18.6 1.7 %fusion.68 = f32[2,512,512]{2,1,0:T(8,128)} fusion(bf16[2,512,128]{2,1,0:T(8,128)(2,1)S(1)} %bitcast.80, bf16[2,512,128]{2,1,0:T(8,128)(2,1)S(1)} %bitcast.93), kind=kOutput, calls=%fused_computation.102 | convolution fusion | flops 134217728 | bytes 2621440 | tf_op jit(solution)/shard_map/ntd,nsd->nts/dot_general | solution.py:69
  20.8 0.9 collective-permute-done
  21.7 0.7 fusion.46
  22.4 0.5 collective-permute-start.5
  22.9 2.4 %collective-permute-start.4 = (bf16[4,128,128]{2,1,0:T(8,128)(2,1)}, bf16[4,128,128]{2,1,0:T(8,128)(2,1)}, u32[]{:S(2)}, u32[]{:S(2)}) collective-permute-start(bf16[4,128,128]{2,1,0:T(8,128)(2,1)} %fusion.46), channel_id=1, source_target_pairs={{0,128},{16,144},{32,160},{48,176},{64,192},{80,208},{96,224},{112... | collective-permute-start | bytes 393224 | tf_op jit(solution)/shard_map/ppermute | solution.py:34
  25.4 1.8 %collective-permute-start.3 = (bf16[4,128,128]{2,1,0:T(8,128)(2,1)}, bf16[4,128,128]{2,1,0:T(8,128)(2,1)}, u32[]{:S(2)}, u32[]{:S(2)}) collective-permute-start(bf16[4,128,128]{2,1,0:T(8,128)(2,1)} %fusion.46), channel_id=1, source_target_pairs={{0,64},{16,80},{32,96},{48,112},{64,128},{80,144},{96,160},{112,17... | collective-permute-start | bytes 393224 | tf_op jit(solution)/shard_map/ppermute | solution.py:34
  27.2 1.1 fusion.60
  28.4 3.4 %collective-permute-done.4 = bf16[4,128,128]{2,1,0:T(8,128)(2,1)} collective-permute-done((bf16[4,128,128]{2,1,0:T(8,128)(2,1)}, bf16[4,128,128]{2,1,0:T(8,128)(2,1)}, u32[]{:S(2)}, u32[]{:S(2)}) %collective-permute-start.4) | collective-permute-done | bytes 131104 | tf_op jit(solution)/shard_map/ppermute | solution.py:34
  31.8 0.9 collective-permute-done.3
  32.7 1.3 fusion.45
  34.0 1.0 fusion.54
  35.0 1.2 fusion.32
  36.1 1.2 fusion.63
  37.4 0.8 multiply_reduce_fusion.3
  38.3 1.2 fusion.29
  39.9 0.8 multiply_reduce_fusion
  40.7 1.2 fusion.30
  41.9 1.1 fusion.31
  43.7 0.8 multiply_reduce_fusion.1
  44.5 0.8 multiply_reduce_fusion.2
  46.1 0.5 copy-done.11
  46.6 0.6 fusion.8
  47.2 12.5 %convolution_convert_fusion = bf16[1024,6144]{1,0:T(8,128)(2,1)} fusion(bf16[1024,512]{1,0:T(8,128)(2,1)S(1)} %fusion.8, bf16[512,6144]{1,0:T(8,128)(2,1)} %param.13), kind=kOutput, calls=%fused_computation | convolution fusion | flops 6448742400 | bytes 19922944 | tf_op jit(solution)/shard_map/dot_general | solution.py:78
  59.8 79.8 %reduce-scatter.2.cloned.1.call-done = bf16[64,6144]{1,0:T(8,128)(2,1)} async-done(((bf16[1024,6144]{1,0:T(8,128)(2,1)}), bf16[64,6144]{1,0:T(8,128)(2,1)}) %reduce-scatter.2.cloned.1.call-update) | async-done | bytes 786448 | tf_op jit(solution)/shard_map/reduce_scatter | solution.py:77
  (61 shorter events, 2.6 us)
Async XLA Ops:
  6.5 1.9 %copy-start.4 = (bf16[1024,512]{1,0:T(8,128)(2,1)S(1)}, bf16[1024,512]{1,0:T(8,128)(2,1)}, u32[]{:S(2)}) copy-start(bf16[1024,512]{1,0:T(8,128)(2,1)} %param.9) | copy-start | bytes 3145732
  6.5 133.0 %reduce-scatter.2.cloned.1.call-start = ((), (), s32[]{:S(2)}) async-start(), calls=%async_computation.1 | async-start | bytes 13369344 | tf_op jit(solution)/shard_map/reduce_scatter | solution.py:77
  9.2 5.6 %copy-start.3 = (f32[2,512,512]{2,1,0:T(8,128)}, f32[2,512,512]{2,1,0:T(8,128)S(1)}, u32[]{:S(2)}) copy-start(f32[2,512,512]{2,1,0:T(8,128)S(1)} %fusion.62) | copy-start | bytes 6291460
  9.2 5.0 %copy-start.10 = (bf16[1024,512]{1,0:T(8,128)(2,1)S(1)}, bf16[1024,512]{1,0:T(8,128)(2,1)}, u32[]{:S(2)}) copy-start(bf16[1024,512]{1,0:T(8,128)(2,1)} %param.7) | copy-start | bytes 3145732
  9.3 11.4 %collective-permute-start.2 = (bf16[4,128,128]{2,1,0:T(8,128)(2,1)S(1)}, bf16[4,128,128]{2,1,0:T(8,128)(2,1)S(1)}, u32[]{:S(2)}, u32[]{:S(2)}) collective-permute-start(bf16[4,128,128]{2,1,0:T(8,128)(2,1)S(1)} %pad_maximum_fusion), channel_id=1, source_target_pairs={{0,48},{16,0},{32,16},{48,32},{64,112},{80,64},{96,80},{112,96},{1... | collective-permute-start | bytes 393224 | tf_op jit(solution)/shard_map/ppermute | solution.py:28
  12.4 8.4 %collective-permute-start.1 = (bf16[4,128,128]{2,1,0:T(8,128)(2,1)S(1)}, bf16[4,128,128]{2,1,0:T(8,128)(2,1)S(1)}, u32[]{:S(2)}, u32[]{:S(2)}) collective-permute-start(bf16[4,128,128]{2,1,0:T(8,128)(2,1)S(1)} %pad_maximum_fusion), channel_id=1, source_target_pairs={{0,32},{16,48},{32,0},{48,16},{64,96},{80,112},{96,64},{112,80},{1... | collective-permute-start | bytes 393224 | tf_op jit(solution)/shard_map/ppermute | solution.py:28
  13.0 8.6 %collective-permute-start = (bf16[4,128,128]{2,1,0:T(8,128)(2,1)S(1)}, bf16[4,128,128]{2,1,0:T(8,128)(2,1)S(1)}, u32[]{:S(2)}, u32[]{:S(2)}) collective-permute-start(bf16[4,128,128]{2,1,0:T(8,128)(2,1)S(1)} %pad_maximum_fusion), channel_id=1, source_target_pairs={{0,16},{16,32},{32,48},{48,0},{64,80},{80,96},{96,112},{112,64},{1... | collective-permute-start | bytes 393224 | tf_op jit(solution)/shard_map/ppermute | solution.py:28
  15.0 3.6 %copy-start.7 = (bf16[1024,128]{1,0:T(8,128)(2,1)}, bf16[1024,128]{1,0:T(8,128)(2,1)S(1)}, u32[]{:S(2)}) copy-start(bf16[1024,128]{1,0:T(8,128)(2,1)S(1)} %get-tuple-element.18) | copy-start | bytes 786436
  15.0 3.6 %copy-start.9 = (bf16[1024,128]{1,0:T(8,128)(2,1)}, bf16[1024,128]{1,0:T(8,128)(2,1)S(1)}, u32[]{:S(2)}) copy-start(bf16[1024,128]{1,0:T(8,128)(2,1)S(1)} %get-tuple-element.17) | copy-start | bytes 786436
  15.0 5.3 %copy-start.5 = (bf16[1024,128]{1,0:T(8,128)(2,1)}, bf16[1024,128]{1,0:T(8,128)(2,1)S(1)}, u32[]{:S(2)}) copy-start(bf16[1024,128]{1,0:T(8,128)(2,1)S(1)} %get-tuple-element.20) | copy-start | bytes 786436
  20.8 7.5 %copy-start.16 = (bf16[4,128,128]{2,1,0:T(8,128)(2,1)}, bf16[4,128,128]{2,1,0:T(8,128)(2,1)S(1)}, u32[]{:S(2)}) copy-start(bf16[4,128,128]{2,1,0:T(8,128)(2,1)S(1)} %collective-permute-done.1) | copy-start | bytes 393220
  21.7 6.6 %copy-start.17 = (bf16[4,128,128]{2,1,0:T(8,128)(2,1)}, bf16[4,128,128]{2,1,0:T(8,128)(2,1)S(1)}, u32[]{:S(2)}) copy-start(bf16[4,128,128]{2,1,0:T(8,128)(2,1)S(1)} %collective-permute-done) | copy-start | bytes 393220
  22.4 6.0 %collective-permute-start.5 = (bf16[4,128,128]{2,1,0:T(8,128)(2,1)}, bf16[4,128,128]{2,1,0:T(8,128)(2,1)}, u32[]{:S(2)}, u32[]{:S(2)}) collective-permute-start(bf16[4,128,128]{2,1,0:T(8,128)(2,1)} %fusion.46), channel_id=1, source_target_pairs={{0,192},{16,208},{32,224},{48,240},{64,0},{80,16},{96,32},{112,48}... | collective-permute-start | bytes 393224 | tf_op jit(solution)/shard_map/ppermute | solution.py:34
  22.9 8.9 %collective-permute-start.4 = (bf16[4,128,128]{2,1,0:T(8,128)(2,1)}, bf16[4,128,128]{2,1,0:T(8,128)(2,1)}, u32[]{:S(2)}, u32[]{:S(2)}) collective-permute-start(bf16[4,128,128]{2,1,0:T(8,128)(2,1)} %fusion.46), channel_id=1, source_target_pairs={{0,128},{16,144},{32,160},{48,176},{64,192},{80,208},{96,224},{112... | collective-permute-start | bytes 393224 | tf_op jit(solution)/shard_map/ppermute | solution.py:34
  25.4 7.3 %collective-permute-start.3 = (bf16[4,128,128]{2,1,0:T(8,128)(2,1)}, bf16[4,128,128]{2,1,0:T(8,128)(2,1)}, u32[]{:S(2)}, u32[]{:S(2)}) collective-permute-start(bf16[4,128,128]{2,1,0:T(8,128)(2,1)} %fusion.46), channel_id=1, source_target_pairs={{0,64},{16,80},{32,96},{48,112},{64,128},{80,144},{96,160},{112,17... | collective-permute-start | bytes 393224 | tf_op jit(solution)/shard_map/ppermute | solution.py:34
  28.3 9.1 %copy-start.15 = (bf16[1024,128]{1,0:T(8,128)(2,1)S(1)}, bf16[1024,128]{1,0:T(8,128)(2,1)}, u32[]{:S(2)}) copy-start(bf16[1024,128]{1,0:T(8,128)(2,1)} %get-tuple-element.13) | copy-start | bytes 786436
  28.3 9.1 %copy-start.2 = (f32[2,512,512]{2,1,0:T(8,128)S(1)}, f32[2,512,512]{2,1,0:T(8,128)}, u32[]{:S(2)}) copy-start(f32[2,512,512]{2,1,0:T(8,128)} %fusion.64) | copy-start | bytes 6291460
  37.4 2.1 %copy-start.8 = (bf16[1024,128]{1,0:T(8,128)(2,1)S(1)}, bf16[1024,128]{1,0:T(8,128)(2,1)}, u32[]{:S(2)}) copy-start(bf16[1024,128]{1,0:T(8,128)(2,1)} %copy-done.7) | copy-start | bytes 786436
  37.4 2.4 %copy-start.1 = (f32[2,512,512]{2,1,0:T(8,128)S(1)}, f32[2,512,512]{2,1,0:T(8,128)}, u32[]{:S(2)}) copy-start(f32[2,512,512]{2,1,0:T(8,128)} %fusion.70) | copy-start | bytes 6291460
  37.4 2.4 %copy-start.14 = (bf16[1024,128]{1,0:T(8,128)(2,1)S(1)}, bf16[1024,128]{1,0:T(8,128)(2,1)}, u32[]{:S(2)}) copy-start(bf16[1024,128]{1,0:T(8,128)(2,1)} %get-tuple-element.15) | copy-start | bytes 786436
  39.8 3.2 %copy-start.6 = (bf16[1024,128]{1,0:T(8,128)(2,1)S(1)}, bf16[1024,128]{1,0:T(8,128)(2,1)}, u32[]{:S(2)}) copy-start(bf16[1024,128]{1,0:T(8,128)(2,1)} %copy-done.5) | copy-start | bytes 786436
  40.7 3.0 %copy-start = (f32[2,512,512]{2,1,0:T(8,128)S(1)}, f32[2,512,512]{2,1,0:T(8,128)}, u32[]{:S(2)}) copy-start(f32[2,512,512]{2,1,0:T(8,128)} %fusion.68) | copy-start | bytes 6291460
  40.7 3.0 %copy-start.13 = (bf16[1024,128]{1,0:T(8,128)(2,1)S(1)}, bf16[1024,128]{1,0:T(8,128)(2,1)}, u32[]{:S(2)}) copy-start(bf16[1024,128]{1,0:T(8,128)(2,1)} %get-tuple-element.16) | copy-start | bytes 786436
  43.3 1.2 copy-start.12
  45.4 1.2 copy-start.11
  45.4 1.2 copy-start.18
Sparse Core Ops, SparseCore 0:
  59.9 79.6 reduce-scatter.1

commit v11 on v9

--- a/solution.py
+++ b/solution.py
@@ -67,7 +67,8 @@
         scores = jnp.where(causal[None], scores, jnp.float32(0.0))
         intra = jnp.einsum("nts,nse->nte", scores, v_h.astype(jnp.float32), precision=high)
         out_h = (inter + intra).reshape(rows, HD)
-        scale = lax.rsqrt(jnp.mean(out_h * out_h, axis=-1, keepdims=True) + 1e-05)
+        squares = jnp.dot(out_h * out_h, jnp.ones((HD, 1), jnp.float32), precision=high)
+        scale = lax.rsqrt(squares * (1.0 / HD) + 1e-05)
         normed.append(out_h * scale)
     attn = (jnp.concatenate(normed, axis=1) * gated).astype(jnp.bfloat16)
     attn = lax.optimization_barrier(attn)

time: 144 us -> 145 us (level)
    unnamed x44 -> x40, local copies, waits for them, and re-layouts: 3.35 us -> 3.61 us
where the time goes in v11:
time: 145 us; the launch traced here: 144 us
  waiting for transfers between devices  86.2 us (59%)
  matrix products  23.9 us (16%)
  between operations  13.7 us (9%)
  starting transfers between devices  9.52 us (7%)
  other arithmetic  7.05 us (5%)
  local copies, waits for them, and re-layouts  4.16 us (3%)
    reduce_scatter x1, waiting for transfers between devices, per_device(): lax.psum_scatter(jnp.dot(attn, w_out, preferred_element_type=jnp.float32)...  79.8 us
    dot_general x1, matrix products, per_device(): jnp.dot(attn, w_out, preferred_element_type=jnp.float32)  9.58 us
    dot_general x4, matrix products, per_device(): jnp.einsum('ntd,nsd->nts', q_h, k_h, preferred_element_type=jnp.float32)  5.74 us
    ppermute x3, starting transfers between devices, exclusive_prefix(): lax.ppermute(row_total.astype(jnp.bfloat16), 'seq', perm)  4.77 us
    ppermute x3, starting transfers between devices, exclusive_prefix(): got = lax.ppermute(sent, 'seq', perm).astype(jnp.float32)  4.76 us
    unnamed x40, local copies, waits for them, and re-layouts  3.61 us
    ppermute x3, waiting for transfers between devices, exclusive_prefix(): lax.ppermute(row_total.astype(jnp.bfloat16), 'seq', perm)  3.51 us
    dot_general x4, matrix products, per_device(): jnp.einsum('ntd,nte->nde', head(ka, h), head(value, h), preferred_element...  3.11 us
  transfers between devices with their start and end apart: 7, of which 5 were waited for; matrix products, arithmetic and copies ran while one was open for 5% of the time, Pallas kernels for 0%

profile of v11, /device:TPU:2, one launch (start us, length us, event | category | flops | bytes accessed | tf_op | source)
XLA Modules:
  0.0 144.5 jit_solution(5191163223061925012)
XLA Ops:
  6.5 1.9 %fusion.7 = bf16[1024,512]{1,0:T(8,128)(2,1)S(1)} fusion(bf16[1024,512]{1,0:T(8,128)(2,1)} %param.8), kind=kLoop, calls=%fused_computation.12 | loop fusion | flops 3145728 | bytes 2097152 | tf_op jit(solution)/shard_map/convert_element_type | solution.py:46
  9.2 0.9 fusion.73
  10.1 0.9 fusion.70
  11.1 0.9 fusion.71
  12.0 3.1 %collective-permute-start.2 = (bf16[4,128,128]{2,1,0:T(8,128)(2,1)S(1)}, bf16[4,128,128]{2,1,0:T(8,128)(2,1)S(1)}, u32[]{:S(2)}, u32[]{:S(2)}) collective-permute-start(bf16[4,128,128]{2,1,0:T(8,128)(2,1)S(1)} %pad_maximum_fusion), channel_id=1, source_target_pairs={{0,48},{16,0},{32,16},{48,32},{64,112},{80,64},{96,80},{112,96},{1... | collective-permute-start | bytes 393224 | tf_op jit(solution)/shard_map/ppermute | solution.py:28
  15.1 0.6 collective-permute-start.1
  15.7 1.0 collective-permute-start
  16.8 0.6 fusion.3
  17.6 1.8 %fusion.81 = f32[2,512,512]{2,1,0:T(8,128)} fusion(bf16[2,512,128]{2,1,0:T(8,128)(2,1)S(1)} %bitcast.86, bf16[2,512,128]{2,1,0:T(8,128)(2,1)S(1)} %bitcast.109), kind=kOutput, calls=%fused_computation.107 | convolution fusion | flops 134217728 | bytes 2621440 | tf_op jit(solution)/shard_map/ntd,nsd->nts/dot_general | solution.py:66
  19.3 1.8 %fusion.83 = f32[2,512,512]{2,1,0:T(8,128)} fusion(bf16[2,512,128]{2,1,0:T(8,128)(2,1)S(1)} %bitcast.88, bf16[2,512,128]{2,1,0:T(8,128)(2,1)S(1)} %bitcast.107), kind=kOutput, calls=%fused_computation.109 | convolution fusion | flops 134217728 | bytes 2621440 | tf_op jit(solution)/shard_map/ntd,nsd->nts/dot_general | solution.py:66
  21.6 1.4 collective-permute-done.1
  23.0 1.4 collective-permute-done
  24.4 0.8 fusion.46
  25.1 0.5 collective-permute-start.5
  25.7 2.4 %collective-permute-start.4 = (bf16[4,128,128]{2,1,0:T(8,128)(2,1)}, bf16[4,128,128]{2,1,0:T(8,128)(2,1)}, u32[]{:S(2)}, u32[]{:S(2)}) collective-permute-start(bf16[4,128,128]{2,1,0:T(8,128)(2,1)} %fusion.46), channel_id=1, source_target_pairs={{0,128},{16,144},{32,160},{48,176},{64,192},{80,208},{96,224},{112... | collective-permute-start | bytes 393224 | tf_op jit(solution)/shard_map/ppermute | solution.py:34
  28.1 1.8 %collective-permute-start.3 = (bf16[4,128,128]{2,1,0:T(8,128)(2,1)}, bf16[4,128,128]{2,1,0:T(8,128)(2,1)}, u32[]{:S(2)}, u32[]{:S(2)}) collective-permute-start(bf16[4,128,128]{2,1,0:T(8,128)(2,1)} %fusion.46), channel_id=1, source_target_pairs={{0,64},{16,80},{32,96},{48,112},{64,128},{80,144},{96,160},{112,17... | collective-permute-start | bytes 393224 | tf_op jit(solution)/shard_map/ppermute | solution.py:34
  29.9 1.8 %fusion.85 = f32[2,512,512]{2,1,0:T(8,128)} fusion(bf16[2,512,128]{2,1,0:T(8,128)(2,1)S(1)} %bitcast.92, bf16[2,512,128]{2,1,0:T(8,128)(2,1)S(1)} %bitcast.103), kind=kOutput, calls=%fused_computation.111 | convolution fusion | flops 134217728 | bytes 2621440 | tf_op jit(solution)/shard_map/ntd,nsd->nts/dot_general | solution.py:66
  31.8 2.7 %collective-permute-done.4 = bf16[4,128,128]{2,1,0:T(8,128)(2,1)} collective-permute-done((bf16[4,128,128]{2,1,0:T(8,128)(2,1)}, bf16[4,128,128]{2,1,0:T(8,128)(2,1)}, u32[]{:S(2)}, u32[]{:S(2)}) %collective-permute-start.4) | collective-permute-done | bytes 131104 | tf_op jit(solution)/shard_map/ppermute | solution.py:34
  34.5 0.8 collective-permute-done.3
  35.3 1.4 fusion.45
  36.7 1.0 fusion.50
  39.0 0.6 copy-done.1
  39.6 0.7 fusion.76
  40.7 0.5 copy-done
  41.2 0.7 fusion.75
  42.3 0.8 fusion.77
  43.9 0.8 fusion.74
  45.7 0.5 copy-done.14
  46.2 0.6 fusion.8
  46.8 1.4 copy-done.19
  48.2 9.6 %convolution_convert_fusion = bf16[1024,6144]{1,0:T(8,128)(2,1)} fusion(bf16[1024,512]{1,0:T(8,128)(2,1)S(1)} %fusion.8, bf16[512,6144]{1,0:T(8,128)(2,1)S(1)} %copy-done.19), kind=kOutput, calls=%fused_computation | convolution fusion | flops 6448742400 | bytes 19922944 | tf_op jit(solution)/shard_map/dot_general | solution.py:76
  57.8 79.8 %reduce-scatter.2.cloned.1.call-done = bf16[64,6144]{1,0:T(8,128)(2,1)} async-done(((bf16[1024,6144]{1,0:T(8,128)(2,1)}), bf16[64,6144]{1,0:T(8,128)(2,1)}) %reduce-scatter.2.cloned.1.call-update) | async-done | bytes 786448 | tf_op jit(solution)/shard_map/reduce_scatter | solution.py:75
  (65 shorter events, 5.2 us)
Async XLA Ops:
  6.5 2.1 %copy-start.12 = (bf16[1024,512]{1,0:T(8,128)(2,1)S(1)}, bf16[1024,512]{1,0:T(8,128)(2,1)}, u32[]{:S(2)}) copy-start(bf16[1024,512]{1,0:T(8,128)(2,1)} %param.9) | copy-start | bytes 3145732
  6.5 131.1 %reduce-scatter.2.cloned.1.call-start = ((), (), s32[]{:S(2)}) async-start(), calls=%async_computation.1 | async-start | bytes 13369344 | tf_op jit(solution)/shard_map/reduce_scatter | solution.py:75
  8.6 8.1 %copy-start.13 = (bf16[1024,512]{1,0:T(8,128)(2,1)S(1)}, bf16[1024,512]{1,0:T(8,128)(2,1)}, u32[]{:S(2)}) copy-start(bf16[1024,512]{1,0:T(8,128)(2,1)} %param.7) | copy-start | bytes 3145732
  8.8 6.9 %copy-start.3 = (bf16[1024,128]{1,0:T(8,128)(2,1)}, bf16[1024,128]{1,0:T(8,128)(2,1)S(1)}, u32[]{:S(2)}) copy-start(bf16[1024,128]{1,0:T(8,128)(2,1)S(1)} %get-tuple-element.9) | copy-start | bytes 786436
  8.9 6.9 %copy-start.5 = (bf16[1024,128]{1,0:T(8,128)(2,1)}, bf16[1024,128]{1,0:T(8,128)(2,1)S(1)}, u32[]{:S(2)}) copy-start(bf16[1024,128]{1,0:T(8,128)(2,1)S(1)} %get-tuple-element.12) | copy-start | bytes 786436
  8.9 6.9 %copy-start.7 = (bf16[1024,128]{1,0:T(8,128)(2,1)}, bf16[1024,128]{1,0:T(8,128)(2,1)S(1)}, u32[]{:S(2)}) copy-start(bf16[1024,128]{1,0:T(8,128)(2,1)S(1)} %get-tuple-element.10) | copy-start | bytes 786436
  12.0 9.5 %collective-permute-start.2 = (bf16[4,128,128]{2,1,0:T(8,128)(2,1)S(1)}, bf16[4,128,128]{2,1,0:T(8,128)(2,1)S(1)}, u32[]{:S(2)}, u32[]{:S(2)}) collective-permute-start(bf16[4,128,128]{2,1,0:T(8,128)(2,1)S(1)} %pad_maximum_fusion), channel_id=1, source_target_pairs={{0,48},{16,0},{32,16},{48,32},{64,112},{80,64},{96,80},{112,96},{1... | collective-permute-start | bytes 393224 | tf_op jit(solution)/shard_map/ppermute | solution.py:28
  15.1 7.9 %collective-permute-start.1 = (bf16[4,128,128]{2,1,0:T(8,128)(2,1)S(1)}, bf16[4,128,128]{2,1,0:T(8,128)(2,1)S(1)}, u32[]{:S(2)}, u32[]{:S(2)}) collective-permute-start(bf16[4,128,128]{2,1,0:T(8,128)(2,1)S(1)} %pad_maximum_fusion), channel_id=1, source_target_pairs={{0,32},{16,48},{32,0},{48,16},{64,96},{80,112},{96,64},{112,80},{1... | collective-permute-start | bytes 393224 | tf_op jit(solution)/shard_map/ppermute | solution.py:28
  15.7 8.6 %collective-permute-start = (bf16[4,128,128]{2,1,0:T(8,128)(2,1)S(1)}, bf16[4,128,128]{2,1,0:T(8,128)(2,1)S(1)}, u32[]{:S(2)}, u32[]{:S(2)}) collective-permute-start(bf16[4,128,128]{2,1,0:T(8,128)(2,1)S(1)} %pad_maximum_fusion), channel_id=1, source_target_pairs={{0,16},{16,32},{32,48},{48,0},{64,80},{80,96},{96,112},{112,64},{1... | collective-permute-start | bytes 393224 | tf_op jit(solution)/shard_map/ppermute | solution.py:28
  21.5 10.2 %copy-start.15 = (bf16[4,128,128]{2,1,0:T(8,128)(2,1)}, bf16[4,128,128]{2,1,0:T(8,128)(2,1)S(1)}, u32[]{:S(2)}) copy-start(bf16[4,128,128]{2,1,0:T(8,128)(2,1)S(1)} %collective-permute-done.2) | copy-start | bytes 393220
  23.0 8.7 %copy-start.16 = (bf16[4,128,128]{2,1,0:T(8,128)(2,1)}, bf16[4,128,128]{2,1,0:T(8,128)(2,1)S(1)}, u32[]{:S(2)}) copy-start(bf16[4,128,128]{2,1,0:T(8,128)(2,1)S(1)} %collective-permute-done.1) | copy-start | bytes 393220
  24.4 7.3 %copy-start.17 = (bf16[4,128,128]{2,1,0:T(8,128)(2,1)}, bf16[4,128,128]{2,1,0:T(8,128)(2,1)S(1)}, u32[]{:S(2)}) copy-start(bf16[4,128,128]{2,1,0:T(8,128)(2,1)S(1)} %collective-permute-done) | copy-start | bytes 393220
  25.1 6.7 %collective-permute-start.5 = (bf16[4,128,128]{2,1,0:T(8,128)(2,1)}, bf16[4,128,128]{2,1,0:T(8,128)(2,1)}, u32[]{:S(2)}, u32[]{:S(2)}) collective-permute-start(bf16[4,128,128]{2,1,0:T(8,128)(2,1)} %fusion.46), channel_id=1, source_target_pairs={{0,192},{16,208},{32,224},{48,240},{64,0},{80,16},{96,32},{112,48}... | collective-permute-start | bytes 393224 | tf_op jit(solution)/shard_map/ppermute | solution.py:34
  25.7 8.8 %collective-permute-start.4 = (bf16[4,128,128]{2,1,0:T(8,128)(2,1)}, bf16[4,128,128]{2,1,0:T(8,128)(2,1)}, u32[]{:S(2)}, u32[]{:S(2)}) collective-permute-start(bf16[4,128,128]{2,1,0:T(8,128)(2,1)} %fusion.46), channel_id=1, source_target_pairs={{0,128},{16,144},{32,160},{48,176},{64,192},{80,208},{96,224},{112... | collective-permute-start | bytes 393224 | tf_op jit(solution)/shard_map/ppermute | solution.py:34
  28.1 7.2 %collective-permute-start.3 = (bf16[4,128,128]{2,1,0:T(8,128)(2,1)}, bf16[4,128,128]{2,1,0:T(8,128)(2,1)}, u32[]{:S(2)}, u32[]{:S(2)}) collective-permute-start(bf16[4,128,128]{2,1,0:T(8,128)(2,1)} %fusion.46), channel_id=1, source_target_pairs={{0,64},{16,80},{32,96},{48,112},{64,128},{80,144},{96,160},{112,17... | collective-permute-start | bytes 393224 | tf_op jit(solution)/shard_map/ppermute | solution.py:34
  31.7 6.0 %copy-start.11 = (f32[2,128,128]{2,1,0:T(8,128)S(1)}, f32[2,128,128]{2,1,0:T(8,128)}, u32[]{:S(2)}) copy-start(f32[2,128,128]{2,1,0:T(8,128)} %get-tuple-element.22) | copy-start | bytes 393220
  31.7 6.3 %copy-start.9 = (f32[2,128,128]{2,1,0:T(8,128)S(1)}, f32[2,128,128]{2,1,0:T(8,128)}, u32[]{:S(2)}) copy-start(f32[2,128,128]{2,1,0:T(8,128)} %get-tuple-element.28) | copy-start | bytes 393220
  31.8 6.6 %copy-start.10 = (f32[2,128,128]{2,1,0:T(8,128)S(1)}, f32[2,128,128]{2,1,0:T(8,128)}, u32[]{:S(2)}) copy-start(f32[2,128,128]{2,1,0:T(8,128)} %get-tuple-element.24) | copy-start | bytes 393220
  38.0 1.6 %copy-start.1 = (f32[2,512,512]{2,1,0:T(8,128)S(1)}, f32[2,512,512]{2,1,0:T(8,128)}, u32[]{:S(2)}) copy-start(f32[2,512,512]{2,1,0:T(8,128)} %fusion.81) | copy-start | bytes 6291460
  38.0 1.6 %copy-start.8 = (bf16[1024,128]{1,0:T(8,128)(2,1)S(1)}, bf16[1024,128]{1,0:T(8,128)(2,1)}, u32[]{:S(2)}) copy-start(bf16[1024,128]{1,0:T(8,128)(2,1)} %copy-done.7) | copy-start | bytes 786436
  39.6 1.6 %copy-start = (f32[2,512,512]{2,1,0:T(8,128)S(1)}, f32[2,512,512]{2,1,0:T(8,128)}, u32[]{:S(2)}) copy-start(f32[2,512,512]{2,1,0:T(8,128)} %fusion.83) | copy-start | bytes 6291460
  39.6 1.6 %copy-start.6 = (bf16[1024,128]{1,0:T(8,128)(2,1)S(1)}, bf16[1024,128]{1,0:T(8,128)(2,1)}, u32[]{:S(2)}) copy-start(bf16[1024,128]{1,0:T(8,128)(2,1)} %copy-done.5) | copy-start | bytes 786436
  41.2 1.1 copy-start.4
  42.3 1.6 %copy-start.2 = (f32[2,512,512]{2,1,0:T(8,128)S(1)}, f32[2,512,512]{2,1,0:T(8,128)}, u32[]{:S(2)}) copy-start(f32[2,512,512]{2,1,0:T(8,128)} %fusion.85) | copy-start | bytes 6291460
  45.0 1.2 copy-start.14
  45.0 1.2 copy-start.18
  45.3 2.9 %copy-start.19 = (bf16[512,6144]{1,0:T(8,128)(2,1)S(1)}, bf16[512,6144]{1,0:T(8,128)(2,1)}, u32[]{:S(2)}) copy-start(bf16[512,6144]{1,0:T(8,128)(2,1)} %param.13) | copy-start | bytes 18874372
Sparse Core Ops, SparseCore 0:
  57.9 79.6 reduce-scatter.1

commit v12 on v9

--- a/solution.py
+++ b/solution.py
@@ -14,7 +14,7 @@
     return best
 
 
-def exclusive_prefix(total):
+def exclusive_prefix(total, start):
     n = lax.axis_size("seq")
     r = row_length(n)
     rows = n // r
@@ -29,10 +29,11 @@
         row_total = row_total + got
         before = before + jnp.where(k <= along, got, jnp.float32(0.0))
     row = index // r
+    before = before + start
     for k in range(1, rows):
         perm = [(a * r + b, ((a + k) % rows) * r + b) for a in range(rows) for b in range(r)]
-        got = lax.ppermute(row_total.astype(jnp.bfloat16), "seq", perm).astype(jnp.float32)
-        before = before + jnp.where(k <= row, got, jnp.float32(0.0))
+        sent_total = jnp.where(row < rows - k, row_total, jnp.float32(0.0)).astype(jnp.bfloat16)
+        before = before + lax.ppermute(sent_total, "seq", perm).astype(jnp.float32)
     return before
 
 
@@ -54,14 +55,14 @@
     ]
     own_total = jnp.stack([jnp.sum(b, axis=0) for b in block_states])
     gated = norm_gain[None, :] * jax.nn.sigmoid(gate.astype(jnp.float32))
-    prior = exclusive_prefix(own_total)
+    prior = exclusive_prefix(own_total, kv_start)
     causal = jnp.arange(block)[:, None] >= jnp.arange(block)[None, :]
     normed = []
     for h in range(heads):
         q_h = head(qa, h)
         k_h = head(ka, h)
         v_h = head(value, h)
-        states = jnp.cumsum(block_states[h], axis=0) - block_states[h] + (kv_start[h] + prior[h])[None]
+        states = jnp.cumsum(block_states[h], axis=0) - block_states[h] + prior[h][None]
         inter = jnp.einsum("ntd,nde->nte", q_h.astype(jnp.float32), states, precision=high)
         scores = jnp.einsum("ntd,nsd->nts", q_h, k_h, preferred_element_type=jnp.float32)
         scores = jnp.where(causal[None], scores, jnp.float32(0.0))

time: 144 us -> 148 us (1.028)
  other arithmetic: 7.02 us -> 11.8 us
  matrix products: 22.8 us -> 25.4 us
  local copies, waits for them, and re-layouts: 3.9 us -> 2.04 us
    dot_general x1, matrix products: 9.59 us -> 12.5 us  [per_device(): jnp.dot(attn, w_out, preferred_element_type=jnp.float32)]
    ppermute x3, waiting for transfers between devices: 2.83 us -> 0.01 us  [exclusive_prefix(): got = lax.ppermute(sent, 'seq', perm).astype(jnp.float32)]
    another operation x4, other arithmetic: 0.07 us -> 2.75 us  [per_device(): jnp.cumsum(block_states[h], axis=0) - block_states[h] + prior[h][None]]
    unnamed x44 -> x56, local copies, waits for them, and re-layouts: 3.35 us -> 1.47 us
    reduce_scatter x1, waiting for transfers between devices: 79.8 us -> 81.4 us  [per_device(): lax.psum_scatter(jnp.dot(attn, w_out, preferred_element_type=jnp.float32)...]
  transfers between devices with their start and end apart: 7 -> 7, of which waited for: 5 -> 4; matrix products, arithmetic and copies ran while one was open for 5% -> 7% of each run, Pallas kernels for 0% -> 0%
where the time goes in v12:
time: 148 us
  waiting for transfers between devices  85.5 us (58%)
  matrix products  25.4 us (17%)
  between operations  13.8 us (9%)
  other arithmetic  11.8 us (8%)
  starting transfers between devices  9.37 us (6%)
  local copies, waits for them, and re-layouts  2.04 us (1%)
    reduce_scatter x1, waiting for transfers between devices, per_device(): lax.psum_scatter(jnp.dot(attn, w_out, preferred_element_type=jnp.float32)...  81.4 us
    dot_general x1, matrix products, per_device(): jnp.dot(attn, w_out, preferred_element_type=jnp.float32)  12.5 us
    dot_general x4, matrix products, per_device(): jnp.einsum('ntd,nsd->nts', q_h, k_h, preferred_element_type=jnp.float32)  5.71 us
    ppermute x3, starting transfers between devices, exclusive_prefix(): before = before + lax.ppermute(sent_total, 'seq', perm).astype(jnp.float32)  4.76 us
    ppermute x3, starting transfers between devices, exclusive_prefix(): got = lax.ppermute(sent, 'seq', perm).astype(jnp.float32)  4.61 us
    ppermute x3, waiting for transfers between devices, exclusive_prefix(): before = before + lax.ppermute(sent_total, 'seq', perm).astype(jnp.float32)  4.06 us
    dot_general x4, matrix products, per_device(): jnp.einsum('nts,nse->nte', scores, v_h.astype(jnp.float32), precision=high)  3.29 us
  transfers between devices with their start and end apart: 7, of which 4 were waited for; matrix products, arithmetic and copies ran while one was open for 7% of the time, Pallas kernels for 0%

profile of v12, /device:TPU:2, one launch (start us, length us, event | category | flops | bytes accessed | tf_op | source)
XLA Modules:
  0.0 147.9 jit_solution(13571829580803081854)
XLA Ops:
  6.5 1.9 %fusion.7 = bf16[1024,512]{1,0:T(8,128)(2,1)S(1)} fusion(bf16[1024,512]{1,0:T(8,128)(2,1)} %param.8), kind=kLoop, calls=%fused_computation.12 | loop fusion | flops 3145728 | bytes 2097152 | tf_op jit(solution)/shard_map/convert_element_type | solution.py:47
  9.4 0.9 fusion.62
  10.6 0.7 pad_maximum_fusion
  11.3 3.0 %collective-permute-start.2 = (bf16[4,128,128]{2,1,0:T(8,128)(2,1)}, bf16[4,128,128]{2,1,0:T(8,128)(2,1)}, u32[]{:S(2)}, u32[]{:S(2)}) collective-permute-start(bf16[4,128,128]{2,1,0:T(8,128)(2,1)} %pad_maximum_fusion), channel_id=1, source_target_pairs={{0,48},{16,0},{32,16},{48,32},{64,112},{80,64},{96,80},{112,96},{1... | collective-permute-start | bytes 393224 | tf_op jit(solution)/shard_map/ppermute | solution.py:28
  14.3 0.6 collective-permute-start.1
  15.0 1.0 collective-permute-start
  15.9 1.8 %fusion.3 = bf16[1024,512]{1,0:T(8,128)(2,1)S(1)} fusion(bf16[1024,512]{1,0:T(8,128)(2,1)} %param.7), kind=kLoop, calls=%fused_computation.8 | loop fusion | flops 3145728 | bytes 2097152 | tf_op jit(solution)/shard_map/convert_element_type | solution.py:46
  18.0 0.8 reduce-window_subtract_fusion.2
  18.8 0.7 reduce-window_subtract_fusion.3
  19.5 1.8 %fusion.67 = f32[2,512,512]{2,1,0:T(8,128)} fusion(bf16[2,512,128]{2,1,0:T(8,128)(2,1)S(1)} %bitcast.104, bf16[2,512,128]{2,1,0:T(8,128)(2,1)S(1)} %bitcast.97), kind=kOutput, calls=%fused_computation.100 | convolution fusion | flops 134217728 | bytes 2621440 | tf_op jit(solution)/shard_map/ntd,nsd->nts/dot_general | solution.py:67
  21.2 1.8 %fusion.68 = f32[2,512,512]{2,1,0:T(8,128)} fusion(bf16[2,512,128]{2,1,0:T(8,128)(2,1)S(1)} %bitcast.102, bf16[2,512,128]{2,1,0:T(8,128)(2,1)S(1)} %bitcast.95), kind=kOutput, calls=%fused_computation.101 | convolution fusion | flops 134217728 | bytes 2621440 | tf_op jit(solution)/shard_map/ntd,nsd->nts/dot_general | solution.py:67
  23.0 1.8 %fusion.69 = f32[2,512,512]{2,1,0:T(8,128)} fusion(bf16[2,512,128]{2,1,0:T(8,128)(2,1)S(1)} %bitcast.100, bf16[2,512,128]{2,1,0:T(8,128)(2,1)S(1)} %bitcast.93), kind=kOutput, calls=%fused_computation.102 | convolution fusion | flops 134217728 | bytes 2621440 | tf_op jit(solution)/shard_map/ntd,nsd->nts/dot_general | solution.py:67
  24.8 0.4 fusion.66
  25.2 0.7 reduce-window_subtract_fusion
  25.9 1.9 %select_convert_fusion.2 = (bf16[4,128,128]{2,1,0:T(8,128)(2,1)}, bf16[4,128,128]{2,1,0:T(8,128)(2,1)}, bf16[4,128,128]{2,1,0:T(8,128)(2,1)}) fusion(pred[]{:T(512)S(6)} %lt.16, bf16[4,128,128]{2,1,0:T(8,128)(2,1)} %collective-permute-done.2, bf16[4,128,128]{2,1,0:T(8,128)(2,1)} %collective-permute-done.1, bf16[4,128,128]{2,1,0:T(8,128)(2,1)} %collective-permute-done, ...), kind=kLoop, calls=%fused_computation.62 | loop fusion | flops 1048576 | bytes 917507 | tf_op jit(solution)/shard_map/convert_element_type | solution.py:35
  27.8 1.5 %collective-permute-start.3 = (bf16[4,128,128]{2,1,0:T(8,128)(2,1)}, bf16[4,128,128]{2,1,0:T(8,128)(2,1)}, u32[]{:S(2)}, u32[]{:S(2)}) collective-permute-start(bf16[4,128,128]{2,1,0:T(8,128)(2,1)} %get-tuple-element.17), channel_id=1, source_target_pairs={{0,64},{16,80},{32,96},{48,112},{64,128},{80,144},{96,160},{112,17... | collective-permute-start | bytes 393224 | tf_op jit(solution)/shard_map/ppermute | solution.py:36
  29.3 1.1 collective-permute-start.4
  30.4 2.2 %collective-permute-start.5 = (bf16[4,128,128]{2,1,0:T(8,128)(2,1)}, bf16[4,128,128]{2,1,0:T(8,128)(2,1)}, u32[]{:S(2)}, u32[]{:S(2)}) collective-permute-start(bf16[4,128,128]{2,1,0:T(8,128)(2,1)} %get-tuple-element.19), channel_id=1, source_target_pairs={{0,192},{16,208},{32,224},{48,240},{64,0},{80,16},{96,32},{112,48}... | collective-permute-start | bytes 393224 | tf_op jit(solution)/shard_map/ppermute | solution.py:36
  32.6 0.7 reduce-window_subtract_fusion.1
  33.3 0.7 collective-permute-done.3
  34.0 2.8 %collective-permute-done.4 = bf16[4,128,128]{2,1,0:T(8,128)(2,1)} collective-permute-done((bf16[4,128,128]{2,1,0:T(8,128)(2,1)}, bf16[4,128,128]{2,1,0:T(8,128)(2,1)}, u32[]{:S(2)}, u32[]{:S(2)}) %collective-permute-start.4) | collective-permute-done | bytes 131104 | tf_op jit(solution)/shard_map/ppermute | solution.py:36
  36.8 0.6 collective-permute-done.5
  37.4 1.4 fusion.42
  38.8 1.2 fusion.47
  40.1 0.8 multiply_reduce_fusion.2
  41.7 0.8 multiply_reduce_fusion.1
  43.3 0.8 multiply_reduce_fusion
  44.5 0.8 multiply_reduce_fusion.3
  46.0 0.5 copy-done.13
  46.5 0.6 fusion.8
  47.1 12.5 %convolution_convert_fusion = bf16[1024,6144]{1,0:T(8,128)(2,1)} fusion(bf16[1024,512]{1,0:T(8,128)(2,1)S(1)} %fusion.8, bf16[512,6144]{1,0:T(8,128)(2,1)} %param.13), kind=kOutput, calls=%fused_computation | convolution fusion | flops 6448742400 | bytes 19922944 | tf_op jit(solution)/shard_map/dot_general | solution.py:76
  59.7 81.4 %reduce-scatter.2.cloned.1.call-done = bf16[64,6144]{1,0:T(8,128)(2,1)} async-done(((bf16[1024,6144]{1,0:T(8,128)(2,1)}), bf16[64,6144]{1,0:T(8,128)(2,1)}) %reduce-scatter.2.cloned.1.call-update) | async-done | bytes 786448 | tf_op jit(solution)/shard_map/reduce_scatter | solution.py:75
  (77 shorter events, 4.1 us)
Async XLA Ops:
  6.5 2.1 %copy-start.12 = (bf16[1024,512]{1,0:T(8,128)(2,1)S(1)}, bf16[1024,512]{1,0:T(8,128)(2,1)}, u32[]{:S(2)}) copy-start(bf16[1024,512]{1,0:T(8,128)(2,1)} %param.9) | copy-start | bytes 3145732
  6.5 134.5 %reduce-scatter.2.cloned.1.call-start = ((), (), s32[]{:S(2)}) async-start(), calls=%async_computation.1 | async-start | bytes 13369344 | tf_op jit(solution)/shard_map/reduce_scatter | solution.py:75
  9.1 8.6 %copy-start.17 = (bf16[128,128]{1,0:T(8,128)(2,1)}, bf16[128,128]{1,0:T(8,128)(2,1)S(1)}, u32[]{:S(2)}) copy-start(bf16[128,128]{1,0:T(8,128)(2,1)S(1)} %get-tuple-element.28) | copy-start | bytes 98308
  9.4 8.5 %copy-start.19 = (bf16[128,128]{1,0:T(8,128)(2,1)}, bf16[128,128]{1,0:T(8,128)(2,1)S(1)}, u32[]{:S(2)}) copy-start(bf16[128,128]{1,0:T(8,128)(2,1)S(1)} %get-tuple-element.30) | copy-start | bytes 98308
  10.4 7.6 %copy-start.21 = (bf16[128,128]{1,0:T(8,128)(2,1)}, bf16[128,128]{1,0:T(8,128)(2,1)S(1)}, u32[]{:S(2)}) copy-start(bf16[128,128]{1,0:T(8,128)(2,1)S(1)} %get-tuple-element.24) | copy-start | bytes 98308
  10.6 7.3 %copy-start.23 = (bf16[128,128]{1,0:T(8,128)(2,1)}, bf16[128,128]{1,0:T(8,128)(2,1)S(1)}, u32[]{:S(2)}) copy-start(bf16[128,128]{1,0:T(8,128)(2,1)S(1)} %get-tuple-element.26) | copy-start | bytes 98308
  11.3 14.6 %collective-permute-start.2 = (bf16[4,128,128]{2,1,0:T(8,128)(2,1)}, bf16[4,128,128]{2,1,0:T(8,128)(2,1)}, u32[]{:S(2)}, u32[]{:S(2)}) collective-permute-start(bf16[4,128,128]{2,1,0:T(8,128)(2,1)} %pad_maximum_fusion), channel_id=1, source_target_pairs={{0,48},{16,0},{32,16},{48,32},{64,112},{80,64},{96,80},{112,96},{1... | collective-permute-start | bytes 393224 | tf_op jit(solution)/shard_map/ppermute | solution.py:28
  14.3 11.6 %collective-permute-start.1 = (bf16[4,128,128]{2,1,0:T(8,128)(2,1)}, bf16[4,128,128]{2,1,0:T(8,128)(2,1)}, u32[]{:S(2)}, u32[]{:S(2)}) collective-permute-start(bf16[4,128,128]{2,1,0:T(8,128)(2,1)} %pad_maximum_fusion), channel_id=1, source_target_pairs={{0,32},{16,48},{32,0},{48,16},{64,96},{80,112},{96,64},{112,80},{1... | collective-permute-start | bytes 393224 | tf_op jit(solution)/shard_map/ppermute | solution.py:28
  15.0 10.9 %collective-permute-start = (bf16[4,128,128]{2,1,0:T(8,128)(2,1)}, bf16[4,128,128]{2,1,0:T(8,128)(2,1)}, u32[]{:S(2)}, u32[]{:S(2)}) collective-permute-start(bf16[4,128,128]{2,1,0:T(8,128)(2,1)} %pad_maximum_fusion), channel_id=1, source_target_pairs={{0,16},{16,32},{32,48},{48,0},{64,80},{80,96},{96,112},{112,64},{1... | collective-permute-start | bytes 393224 | tf_op jit(solution)/shard_map/ppermute | solution.py:28
  18.0 5.0 %copy-start.7 = (bf16[1024,128]{1,0:T(8,128)(2,1)}, bf16[1024,128]{1,0:T(8,128)(2,1)S(1)}, u32[]{:S(2)}) copy-start(bf16[1024,128]{1,0:T(8,128)(2,1)S(1)} %get-tuple-element.7) | copy-start | bytes 786436
  18.0 5.0 %copy-start.9 = (bf16[1024,128]{1,0:T(8,128)(2,1)}, bf16[1024,128]{1,0:T(8,128)(2,1)S(1)}, u32[]{:S(2)}) copy-start(bf16[1024,128]{1,0:T(8,128)(2,1)S(1)} %get-tuple-element.8) | copy-start | bytes 786436
  18.0 5.0 %copy-start.5 = (bf16[1024,128]{1,0:T(8,128)(2,1)}, bf16[1024,128]{1,0:T(8,128)(2,1)S(1)}, u32[]{:S(2)}) copy-start(bf16[1024,128]{1,0:T(8,128)(2,1)S(1)} %get-tuple-element.6) | copy-start | bytes 786436
  18.0 6.7 %copy-start.3 = (bf16[1024,128]{1,0:T(8,128)(2,1)}, bf16[1024,128]{1,0:T(8,128)(2,1)S(1)}, u32[]{:S(2)}) copy-start(bf16[1024,128]{1,0:T(8,128)(2,1)S(1)} %get-tuple-element.5) | copy-start | bytes 786436
  23.0 2.2 %copy-start.11 = (f32[2,128,128]{2,1,0:T(8,128)S(1)}, f32[2,128,128]{2,1,0:T(8,128)}, u32[]{:S(2)}) copy-start(f32[2,128,128]{2,1,0:T(8,128)} %get-tuple-element.25) | copy-start | bytes 393220
  24.7 1.2 copy-start.20
  24.7 1.2 copy-start.22
  24.7 1.2 copy-start.24
  25.2 13.6 %copy-start.10 = (bf16[1024,128]{1,0:T(8,128)(2,1)S(1)}, bf16[1024,128]{1,0:T(8,128)(2,1)}, u32[]{:S(2)}) copy-start(bf16[1024,128]{1,0:T(8,128)(2,1)} %copy-done.9) | copy-start | bytes 786436
  27.8 6.2 %collective-permute-start.3 = (bf16[4,128,128]{2,1,0:T(8,128)(2,1)}, bf16[4,128,128]{2,1,0:T(8,128)(2,1)}, u32[]{:S(2)}, u32[]{:S(2)}) collective-permute-start(bf16[4,128,128]{2,1,0:T(8,128)(2,1)} %get-tuple-element.17), channel_id=1, source_target_pairs={{0,64},{16,80},{32,96},{48,112},{64,128},{80,144},{96,160},{112,17... | collective-permute-start | bytes 393224 | tf_op jit(solution)/shard_map/ppermute | solution.py:36
  29.3 7.5 %collective-permute-start.4 = (bf16[4,128,128]{2,1,0:T(8,128)(2,1)}, bf16[4,128,128]{2,1,0:T(8,128)(2,1)}, u32[]{:S(2)}, u32[]{:S(2)}) collective-permute-start(bf16[4,128,128]{2,1,0:T(8,128)(2,1)} %get-tuple-element.18), channel_id=1, source_target_pairs={{0,128},{16,144},{32,160},{48,176},{64,192},{80,208},{96,224},{112... | collective-permute-start | bytes 393224 | tf_op jit(solution)/shard_map/ppermute | solution.py:36
  30.4 7.0 %collective-permute-start.5 = (bf16[4,128,128]{2,1,0:T(8,128)(2,1)}, bf16[4,128,128]{2,1,0:T(8,128)(2,1)}, u32[]{:S(2)}, u32[]{:S(2)}) collective-permute-start(bf16[4,128,128]{2,1,0:T(8,128)(2,1)} %get-tuple-element.19), channel_id=1, source_target_pairs={{0,192},{16,208},{32,224},{48,240},{64,0},{80,16},{96,32},{112,48}... | collective-permute-start | bytes 393224 | tf_op jit(solution)/shard_map/ppermute | solution.py:36
  33.2 6.9 %copy-start.2 = (f32[2,512,512]{2,1,0:T(8,128)S(1)}, f32[2,512,512]{2,1,0:T(8,128)}, u32[]{:S(2)}) copy-start(f32[2,512,512]{2,1,0:T(8,128)} %fusion.67) | copy-start | bytes 6291460
  38.8 2.1 %copy-start.8 = (bf16[1024,128]{1,0:T(8,128)(2,1)S(1)}, bf16[1024,128]{1,0:T(8,128)(2,1)}, u32[]{:S(2)}) copy-start(bf16[1024,128]{1,0:T(8,128)(2,1)} %copy-done.7) | copy-start | bytes 786436
  38.8 2.1 %copy-start.16 = (f32[2,128,128]{2,1,0:T(8,128)S(1)}, f32[2,128,128]{2,1,0:T(8,128)}, u32[]{:S(2)}) copy-start(f32[2,128,128]{2,1,0:T(8,128)} %reduce-window_subtract_fusion.1) | copy-start | bytes 393220
  40.1 1.6 %copy-start.1 = (f32[2,512,512]{2,1,0:T(8,128)S(1)}, f32[2,512,512]{2,1,0:T(8,128)}, u32[]{:S(2)}) copy-start(f32[2,512,512]{2,1,0:T(8,128)} %fusion.68) | copy-start | bytes 6291460
  41.0 1.6 %copy-start.6 = (bf16[1024,128]{1,0:T(8,128)(2,1)S(1)}, bf16[1024,128]{1,0:T(8,128)(2,1)}, u32[]{:S(2)}) copy-start(bf16[1024,128]{1,0:T(8,128)(2,1)} %copy-done.5) | copy-start | bytes 786436
  41.0 1.6 %copy-start.15 = (f32[2,128,128]{2,1,0:T(8,128)S(1)}, f32[2,128,128]{2,1,0:T(8,128)}, u32[]{:S(2)}) copy-start(f32[2,128,128]{2,1,0:T(8,128)} %reduce-window_subtract_fusion) | copy-start | bytes 393220
  41.7 1.6 %copy-start = (f32[2,512,512]{2,1,0:T(8,128)S(1)}, f32[2,512,512]{2,1,0:T(8,128)}, u32[]{:S(2)}) copy-start(f32[2,512,512]{2,1,0:T(8,128)} %fusion.69) | copy-start | bytes 6291460
  42.6 1.6 %copy-start.4 = (bf16[1024,128]{1,0:T(8,128)(2,1)S(1)}, bf16[1024,128]{1,0:T(8,128)(2,1)}, u32[]{:S(2)}) copy-start(bf16[1024,128]{1,0:T(8,128)(2,1)} %copy-done.3) | copy-start | bytes 786436
  42.6 1.6 %copy-start.14 = (f32[2,128,128]{2,1,0:T(8,128)S(1)}, f32[2,128,128]{2,1,0:T(8,128)}, u32[]{:S(2)}) copy-start(f32[2,128,128]{2,1,0:T(8,128)} %reduce-window_subtract_fusion.3) | copy-start | bytes 393220
  45.3 1.2 copy-start.13
  45.3 1.2 copy-start.25
  (1 other events, 1.1 us)
Sparse Core Ops, SparseCore 0:
  59.8 81.2 reduce-scatter.1

commit v13 on v9

--- a/solution.py
+++ b/solution.py
@@ -7,11 +7,7 @@
 
 
 def row_length(n):
-    best = 1
-    for r in range(1, n + 1):
-        if n % r == 0 and r * r <= n:
-            best = r
-    return best
+    return n // 2 if n % 2 == 0 else n
 
 
 def exclusive_prefix(total):

time: 144 us -> 150 us (1.042)
  starting transfers between devices: 9.53 us -> 13.3 us
  waiting for transfers between devices: 86.2 us -> 88.4 us
    ppermute x3 -> x7, starting transfers between devices: 4.76 us -> 11.2 us  [exclusive_prefix(): got = lax.ppermute(sent, 'seq', perm).astype(jnp.float32)]
    ppermute x3 -> x7, waiting for transfers between devices: 2.83 us -> 5.7 us  [exclusive_prefix(): got = lax.ppermute(sent, 'seq', perm).astype(jnp.float32)]
    ppermute x3 -> x1, starting transfers between devices: 4.77 us -> 2.13 us  [exclusive_prefix(): lax.ppermute(row_total.astype(jnp.bfloat16), 'seq', perm)]
    ppermute x3 -> x1, waiting for transfers between devices: 3.54 us -> 2.71 us  [exclusive_prefix(): lax.ppermute(row_total.astype(jnp.bfloat16), 'seq', perm)]
    unnamed x44 -> x52, local copies, waits for them, and re-layouts: 3.35 us -> 3.51 us
  transfers between devices with their start and end apart: 7 -> 9, of which waited for: 5 -> 6; matrix products, arithmetic and copies ran while one was open for 5% -> 4% of each run, Pallas kernels for 0% -> 0%
where the time goes in v13:
time: 150 us
  waiting for transfers between devices  88.4 us (59%)
  matrix products  22.8 us (15%)
  between operations  13.8 us (9%)
  starting transfers between devices  13.3 us (9%)
  other arithmetic  7.27 us (5%)
  local copies, waits for them, and re-layouts  4.06 us (3%)
    reduce_scatter x1, waiting for transfers between devices, per_device(): lax.psum_scatter(jnp.dot(attn, w_out, preferred_element_type=jnp.float32)...  80 us
    ppermute x7, starting transfers between devices, exclusive_prefix(): got = lax.ppermute(sent, 'seq', perm).astype(jnp.float32)  11.2 us
    dot_general x1, matrix products, per_device(): jnp.dot(attn, w_out, preferred_element_type=jnp.float32)  9.57 us
    dot_general x4, matrix products, per_device(): jnp.einsum('ntd,nsd->nts', q_h, k_h, preferred_element_type=jnp.float32)  5.71 us
    ppermute x7, waiting for transfers between devices, exclusive_prefix(): got = lax.ppermute(sent, 'seq', perm).astype(jnp.float32)  5.7 us
    unnamed x52, local copies, waits for them, and re-layouts  3.51 us
    dot_general x4, matrix products, per_device(): jnp.einsum('nts,nse->nte', scores, v_h.astype(jnp.float32), precision=high)  3.29 us
    dot_general x4, matrix products, per_device(): jnp.einsum('ntd,nte->nde', head(ka, h), head(value, h), preferred_element...  3.08 us
  transfers between devices with their start and end apart: 9, of which 6 were waited for; matrix products, arithmetic and copies ran while one was open for 4% of the time, Pallas kernels for 0%

profile of v13, /device:TPU:2, one launch (start us, length us, event | category | flops | bytes accessed | tf_op | source)
XLA Modules:
  0.0 149.7 jit_solution(15570730763128621869)
XLA Ops:
  6.5 1.9 %fusion.7 = bf16[1024,512]{1,0:T(8,128)(2,1)S(1)} fusion(bf16[1024,512]{1,0:T(8,128)(2,1)} %param.8), kind=kLoop, calls=%fused_computation.12 | loop fusion | flops 3145728 | bytes 2097152 | tf_op jit(solution)/shard_map/convert_element_type | solution.py:42
  9.2 0.9 fusion.63
  10.1 0.9 fusion.60
  11.0 0.9 fusion.61
  12.0 3.1 %collective-permute-start.6 = (bf16[4,128,128]{2,1,0:T(8,128)(2,1)S(1)}, bf16[4,128,128]{2,1,0:T(8,128)(2,1)S(1)}, u32[]{:S(2)}, u32[]{:S(2)}) collective-permute-start(bf16[4,128,128]{2,1,0:T(8,128)(2,1)S(1)} %pad_maximum_fusion), channel_id=1, source_target_pairs={{0,112},{16,0},{32,16},{48,32},{64,48},{80,64},{96,80},{112,96},{1... | collective-permute-start | bytes 393224 | tf_op jit(solution)/shard_map/ppermute | solution.py:24
  15.0 0.6 collective-permute-start.5
  15.7 1.9 %collective-permute-start.4 = (bf16[4,128,128]{2,1,0:T(8,128)(2,1)S(1)}, bf16[4,128,128]{2,1,0:T(8,128)(2,1)S(1)}, u32[]{:S(2)}, u32[]{:S(2)}) collective-permute-start(bf16[4,128,128]{2,1,0:T(8,128)(2,1)S(1)} %pad_maximum_fusion), channel_id=1, source_target_pairs={{0,80},{16,96},{32,112},{48,0},{64,16},{80,32},{96,48},{112,64},{1... | collective-permute-start | bytes 393224 | tf_op jit(solution)/shard_map/ppermute | solution.py:24
  17.6 0.5 collective-permute-start.3
  18.1 2.4 %collective-permute-start.2 = (bf16[4,128,128]{2,1,0:T(8,128)(2,1)S(1)}, bf16[4,128,128]{2,1,0:T(8,128)(2,1)S(1)}, u32[]{:S(2)}, u32[]{:S(2)}) collective-permute-start(bf16[4,128,128]{2,1,0:T(8,128)(2,1)S(1)} %pad_maximum_fusion), channel_id=1, source_target_pairs={{0,48},{16,64},{32,80},{48,96},{64,112},{80,0},{96,16},{112,32},{1... | collective-permute-start | bytes 393224 | tf_op jit(solution)/shard_map/ppermute | solution.py:24
  20.5 0.6 fusion.3
  21.3 1.8 %fusion.67 = f32[2,512,512]{2,1,0:T(8,128)} fusion(bf16[2,512,128]{2,1,0:T(8,128)(2,1)S(1)} %bitcast.86, bf16[2,512,128]{2,1,0:T(8,128)(2,1)S(1)} %bitcast.109), kind=kOutput, calls=%fused_computation.105 | convolution fusion | flops 134217728 | bytes 2621440 | tf_op jit(solution)/shard_map/ntd,nsd->nts/dot_general | solution.py:62
  23.5 2.7 %collective-permute-start.1 = (bf16[4,128,128]{2,1,0:T(8,128)(2,1)S(1)}, bf16[4,128,128]{2,1,0:T(8,128)(2,1)S(1)}, u32[]{:S(2)}, u32[]{:S(2)}) collective-permute-start(bf16[4,128,128]{2,1,0:T(8,128)(2,1)S(1)} %pad_maximum_fusion), channel_id=1, source_target_pairs={{0,32},{16,48},{32,64},{48,80},{64,96},{80,112},{96,0},{112,16},{1... | collective-permute-start | bytes 393224 | tf_op jit(solution)/shard_map/ppermute | solution.py:24
  26.2 1.8 %fusion.65 = f32[2,512,512]{2,1,0:T(8,128)} fusion(bf16[2,512,128]{2,1,0:T(8,128)(2,1)S(1)} %bitcast.90, bf16[2,512,128]{2,1,0:T(8,128)(2,1)S(1)} %bitcast.105), kind=kOutput, calls=%fused_computation.103 | convolution fusion | flops 134217728 | bytes 2621440 | tf_op jit(solution)/shard_map/ntd,nsd->nts/dot_general | solution.py:62
  28.2 0.8 collective-permute-done.2
  29.0 3.1 %collective-permute-done.1 = bf16[4,128,128]{2,1,0:T(8,128)(2,1)S(1)} collective-permute-done((bf16[4,128,128]{2,1,0:T(8,128)(2,1)S(1)}, bf16[4,128,128]{2,1,0:T(8,128)(2,1)S(1)}, u32[]{:S(2)}, u32[]{:S(2)}) %collective-permute-start.1) | collective-permute-done | bytes 131104 | tf_op jit(solution)/shard_map/ppermute | solution.py:24
  32.1 1.6 %collective-permute-done = bf16[4,128,128]{2,1,0:T(8,128)(2,1)S(1)} collective-permute-done((bf16[4,128,128]{2,1,0:T(8,128)(2,1)S(1)}, bf16[4,128,128]{2,1,0:T(8,128)(2,1)S(1)}, u32[]{:S(2)}, u32[]{:S(2)}) %collective-permute-start) | collective-permute-done | bytes 131104 | tf_op jit(solution)/shard_map/ppermute | solution.py:24
  33.6 0.8 fusion.48
  34.5 2.1 %collective-permute-start.7 = (bf16[4,128,128]{2,1,0:T(8,128)(2,1)}, bf16[4,128,128]{2,1,0:T(8,128)(2,1)}, u32[]{:S(2)}, u32[]{:S(2)}) collective-permute-start(bf16[4,128,128]{2,1,0:T(8,128)(2,1)} %fusion.48), channel_id=1, source_target_pairs={{0,128},{16,144},{32,160},{48,176},{64,192},{80,208},{96,224},{112... | collective-permute-start | bytes 393224 | tf_op jit(solution)/shard_map/ppermute | solution.py:30
  36.6 1.8 %fusion.71 = f32[2,512,512]{2,1,0:T(8,128)} fusion(bf16[2,512,128]{2,1,0:T(8,128)(2,1)S(1)} %bitcast.92, bf16[2,512,128]{2,1,0:T(8,128)(2,1)S(1)} %bitcast.103), kind=kOutput, calls=%fused_computation.109 | convolution fusion | flops 134217728 | bytes 2621440 | tf_op jit(solution)/shard_map/ntd,nsd->nts/dot_general | solution.py:62
  38.5 2.7 %collective-permute-done.7 = bf16[4,128,128]{2,1,0:T(8,128)(2,1)} collective-permute-done((bf16[4,128,128]{2,1,0:T(8,128)(2,1)}, bf16[4,128,128]{2,1,0:T(8,128)(2,1)}, u32[]{:S(2)}, u32[]{:S(2)}) %collective-permute-start.7) | collective-permute-done | bytes 131104 | tf_op jit(solution)/shard_map/ppermute | solution.py:30
  41.2 1.5 fusion.47
  42.7 1.0 fusion.52
  45.1 0.6 copy-done.1
  45.7 0.8 multiply_reduce_fusion.2
  46.5 0.8 multiply_reduce_fusion.1
  47.4 0.7 copy-done
  48.1 0.8 multiply_reduce_fusion.3
  49.2 0.8 multiply_reduce_fusion
  51.2 0.6 fusion.8
  51.8 1.4 copy-done.23
  53.2 9.6 %convolution_convert_fusion = bf16[1024,6144]{1,0:T(8,128)(2,1)} fusion(bf16[1024,512]{1,0:T(8,128)(2,1)S(1)} %fusion.8, bf16[512,6144]{1,0:T(8,128)(2,1)S(1)} %copy-done.23), kind=kOutput, calls=%fused_computation | convolution fusion | flops 6448742400 | bytes 19922944 | tf_op jit(solution)/shard_map/dot_general | solution.py:71
  62.8 80.0 %reduce-scatter.2.cloned.1.call-done = bf16[64,6144]{1,0:T(8,128)(2,1)} async-done(((bf16[1024,6144]{1,0:T(8,128)(2,1)}), bf16[64,6144]{1,0:T(8,128)(2,1)}) %reduce-scatter.2.cloned.1.call-update) | async-done | bytes 786448 | tf_op jit(solution)/shard_map/reduce_scatter | solution.py:70
  (77 shorter events, 4.4 us)
Async XLA Ops:
  6.5 2.1 %copy-start.12 = (bf16[1024,512]{1,0:T(8,128)(2,1)S(1)}, bf16[1024,512]{1,0:T(8,128)(2,1)}, u32[]{:S(2)}) copy-start(bf16[1024,512]{1,0:T(8,128)(2,1)} %param.9) | copy-start | bytes 3145732
  6.5 136.3 %reduce-scatter.2.cloned.1.call-start = ((), (), s32[]{:S(2)}) async-start(), calls=%async_computation.1 | async-start | bytes 13369344 | tf_op jit(solution)/shard_map/reduce_scatter | solution.py:70
  8.6 11.9 %copy-start.13 = (bf16[1024,512]{1,0:T(8,128)(2,1)S(1)}, bf16[1024,512]{1,0:T(8,128)(2,1)}, u32[]{:S(2)}) copy-start(bf16[1024,512]{1,0:T(8,128)(2,1)} %param.7) | copy-start | bytes 3145732
  8.8 9.3 %copy-start.3 = (bf16[1024,128]{1,0:T(8,128)(2,1)}, bf16[1024,128]{1,0:T(8,128)(2,1)S(1)}, u32[]{:S(2)}) copy-start(bf16[1024,128]{1,0:T(8,128)(2,1)S(1)} %get-tuple-element.9) | copy-start | bytes 786436
  8.9 9.3 %copy-start.5 = (bf16[1024,128]{1,0:T(8,128)(2,1)}, bf16[1024,128]{1,0:T(8,128)(2,1)S(1)}, u32[]{:S(2)}) copy-start(bf16[1024,128]{1,0:T(8,128)(2,1)S(1)} %get-tuple-element.12) | copy-start | bytes 786436
  8.9 9.2 %copy-start.7 = (bf16[1024,128]{1,0:T(8,128)(2,1)}, bf16[1024,128]{1,0:T(8,128)(2,1)S(1)}, u32[]{:S(2)}) copy-start(bf16[1024,128]{1,0:T(8,128)(2,1)S(1)} %get-tuple-element.10) | copy-start | bytes 786436
  12.0 11.5 %collective-permute-start.6 = (bf16[4,128,128]{2,1,0:T(8,128)(2,1)S(1)}, bf16[4,128,128]{2,1,0:T(8,128)(2,1)S(1)}, u32[]{:S(2)}, u32[]{:S(2)}) collective-permute-start(bf16[4,128,128]{2,1,0:T(8,128)(2,1)S(1)} %pad_maximum_fusion), channel_id=1, source_target_pairs={{0,112},{16,0},{32,16},{48,32},{64,48},{80,64},{96,80},{112,96},{1... | collective-permute-start | bytes 393224 | tf_op jit(solution)/shard_map/ppermute | solution.py:24
  15.0 11.1 %collective-permute-start.5 = (bf16[4,128,128]{2,1,0:T(8,128)(2,1)S(1)}, bf16[4,128,128]{2,1,0:T(8,128)(2,1)S(1)}, u32[]{:S(2)}, u32[]{:S(2)}) collective-permute-start(bf16[4,128,128]{2,1,0:T(8,128)(2,1)S(1)} %pad_maximum_fusion), channel_id=1, source_target_pairs={{0,96},{16,112},{32,0},{48,16},{64,32},{80,48},{96,64},{112,80},{1... | collective-permute-start | bytes 393224 | tf_op jit(solution)/shard_map/ppermute | solution.py:24
  15.7 12.3 %collective-permute-start.4 = (bf16[4,128,128]{2,1,0:T(8,128)(2,1)S(1)}, bf16[4,128,128]{2,1,0:T(8,128)(2,1)S(1)}, u32[]{:S(2)}, u32[]{:S(2)}) collective-permute-start(bf16[4,128,128]{2,1,0:T(8,128)(2,1)S(1)} %pad_maximum_fusion), channel_id=1, source_target_pairs={{0,80},{16,96},{32,112},{48,0},{64,16},{80,32},{96,48},{112,64},{1... | collective-permute-start | bytes 393224 | tf_op jit(solution)/shard_map/ppermute | solution.py:24
  17.6 10.6 %collective-permute-start.3 = (bf16[4,128,128]{2,1,0:T(8,128)(2,1)S(1)}, bf16[4,128,128]{2,1,0:T(8,128)(2,1)S(1)}, u32[]{:S(2)}, u32[]{:S(2)}) collective-permute-start(bf16[4,128,128]{2,1,0:T(8,128)(2,1)S(1)} %pad_maximum_fusion), channel_id=1, source_target_pairs={{0,64},{16,80},{32,96},{48,112},{64,0},{80,16},{96,32},{112,48},{1... | collective-permute-start | bytes 393224 | tf_op jit(solution)/shard_map/ppermute | solution.py:24
  18.1 10.8 %collective-permute-start.2 = (bf16[4,128,128]{2,1,0:T(8,128)(2,1)S(1)}, bf16[4,128,128]{2,1,0:T(8,128)(2,1)S(1)}, u32[]{:S(2)}, u32[]{:S(2)}) collective-permute-start(bf16[4,128,128]{2,1,0:T(8,128)(2,1)S(1)} %pad_maximum_fusion), channel_id=1, source_target_pairs={{0,48},{16,64},{32,80},{48,96},{64,112},{80,0},{96,16},{112,32},{1... | collective-permute-start | bytes 393224 | tf_op jit(solution)/shard_map/ppermute | solution.py:24
  23.5 14.8 %copy-start.15 = (bf16[4,128,128]{2,1,0:T(8,128)(2,1)}, bf16[4,128,128]{2,1,0:T(8,128)(2,1)S(1)}, u32[]{:S(2)}) copy-start(bf16[4,128,128]{2,1,0:T(8,128)(2,1)S(1)} %collective-permute-done.6) | copy-start | bytes 393220
  23.5 8.6 %collective-permute-start.1 = (bf16[4,128,128]{2,1,0:T(8,128)(2,1)S(1)}, bf16[4,128,128]{2,1,0:T(8,128)(2,1)S(1)}, u32[]{:S(2)}, u32[]{:S(2)}) collective-permute-start(bf16[4,128,128]{2,1,0:T(8,128)(2,1)S(1)} %pad_maximum_fusion), channel_id=1, source_target_pairs={{0,32},{16,48},{32,64},{48,80},{64,96},{80,112},{96,0},{112,16},{1... | collective-permute-start | bytes 393224 | tf_op jit(solution)/shard_map/ppermute | solution.py:24
  26.2 12.2 %copy-start.16 = (bf16[4,128,128]{2,1,0:T(8,128)(2,1)}, bf16[4,128,128]{2,1,0:T(8,128)(2,1)S(1)}, u32[]{:S(2)}) copy-start(bf16[4,128,128]{2,1,0:T(8,128)(2,1)S(1)} %collective-permute-done.5) | copy-start | bytes 393220
  26.2 7.5 %collective-permute-start = (bf16[4,128,128]{2,1,0:T(8,128)(2,1)S(1)}, bf16[4,128,128]{2,1,0:T(8,128)(2,1)S(1)}, u32[]{:S(2)}, u32[]{:S(2)}) collective-permute-start(bf16[4,128,128]{2,1,0:T(8,128)(2,1)S(1)} %pad_maximum_fusion), channel_id=1, source_target_pairs={{0,16},{16,32},{32,48},{48,64},{64,80},{80,96},{96,112},{112,0},{1... | collective-permute-start | bytes 393224 | tf_op jit(solution)/shard_map/ppermute | solution.py:24
  27.9 10.4 %copy-start.17 = (bf16[4,128,128]{2,1,0:T(8,128)(2,1)}, bf16[4,128,128]{2,1,0:T(8,128)(2,1)S(1)}, u32[]{:S(2)}) copy-start(bf16[4,128,128]{2,1,0:T(8,128)(2,1)S(1)} %collective-permute-done.4) | copy-start | bytes 393220
  28.2 10.2 %copy-start.18 = (bf16[4,128,128]{2,1,0:T(8,128)(2,1)}, bf16[4,128,128]{2,1,0:T(8,128)(2,1)S(1)}, u32[]{:S(2)}) copy-start(bf16[4,128,128]{2,1,0:T(8,128)(2,1)S(1)} %collective-permute-done.3) | copy-start | bytes 393220
  28.9 9.4 %copy-start.19 = (bf16[4,128,128]{2,1,0:T(8,128)(2,1)}, bf16[4,128,128]{2,1,0:T(8,128)(2,1)S(1)}, u32[]{:S(2)}) copy-start(bf16[4,128,128]{2,1,0:T(8,128)(2,1)S(1)} %collective-permute-done.2) | copy-start | bytes 393220
  32.1 6.3 %copy-start.20 = (bf16[4,128,128]{2,1,0:T(8,128)(2,1)}, bf16[4,128,128]{2,1,0:T(8,128)(2,1)S(1)}, u32[]{:S(2)}) copy-start(bf16[4,128,128]{2,1,0:T(8,128)(2,1)S(1)} %collective-permute-done.1) | copy-start | bytes 393220
  33.6 4.7 %copy-start.21 = (bf16[4,128,128]{2,1,0:T(8,128)(2,1)}, bf16[4,128,128]{2,1,0:T(8,128)(2,1)S(1)}, u32[]{:S(2)}) copy-start(bf16[4,128,128]{2,1,0:T(8,128)(2,1)S(1)} %collective-permute-done) | copy-start | bytes 393220
  34.5 6.8 %collective-permute-start.7 = (bf16[4,128,128]{2,1,0:T(8,128)(2,1)}, bf16[4,128,128]{2,1,0:T(8,128)(2,1)}, u32[]{:S(2)}, u32[]{:S(2)}) collective-permute-start(bf16[4,128,128]{2,1,0:T(8,128)(2,1)} %fusion.48), channel_id=1, source_target_pairs={{0,128},{16,144},{32,160},{48,176},{64,192},{80,208},{96,224},{112... | collective-permute-start | bytes 393224 | tf_op jit(solution)/shard_map/ppermute | solution.py:30
  38.4 5.3 %copy-start.11 = (f32[2,128,128]{2,1,0:T(8,128)S(1)}, f32[2,128,128]{2,1,0:T(8,128)}, u32[]{:S(2)}) copy-start(f32[2,128,128]{2,1,0:T(8,128)} %get-tuple-element.22) | copy-start | bytes 393220
  38.4 5.7 %copy-start.9 = (f32[2,128,128]{2,1,0:T(8,128)S(1)}, f32[2,128,128]{2,1,0:T(8,128)}, u32[]{:S(2)}) copy-start(f32[2,128,128]{2,1,0:T(8,128)} %get-tuple-element.28) | copy-start | bytes 393220
  42.7 1.7 %copy-start.10 = (f32[2,128,128]{2,1,0:T(8,128)S(1)}, f32[2,128,128]{2,1,0:T(8,128)}, u32[]{:S(2)}) copy-start(f32[2,128,128]{2,1,0:T(8,128)} %get-tuple-element.24) | copy-start | bytes 393220
  44.1 1.6 %copy-start.1 = (f32[2,512,512]{2,1,0:T(8,128)S(1)}, f32[2,512,512]{2,1,0:T(8,128)}, u32[]{:S(2)}) copy-start(f32[2,512,512]{2,1,0:T(8,128)} %fusion.67) | copy-start | bytes 6291460
  44.1 1.6 %copy-start.8 = (bf16[1024,128]{1,0:T(8,128)(2,1)S(1)}, bf16[1024,128]{1,0:T(8,128)(2,1)}, u32[]{:S(2)}) copy-start(bf16[1024,128]{1,0:T(8,128)(2,1)} %copy-done.7) | copy-start | bytes 786436
  44.8 1.7 %copy-start.6 = (bf16[1024,128]{1,0:T(8,128)(2,1)S(1)}, bf16[1024,128]{1,0:T(8,128)(2,1)}, u32[]{:S(2)}) copy-start(bf16[1024,128]{1,0:T(8,128)(2,1)} %copy-done.5) | copy-start | bytes 786436
  46.5 1.6 %copy-start = (f32[2,512,512]{2,1,0:T(8,128)S(1)}, f32[2,512,512]{2,1,0:T(8,128)}, u32[]{:S(2)}) copy-start(f32[2,512,512]{2,1,0:T(8,128)} %fusion.65) | copy-start | bytes 6291460
  46.5 1.6 %copy-start.4 = (bf16[1024,128]{1,0:T(8,128)(2,1)S(1)}, bf16[1024,128]{1,0:T(8,128)(2,1)}, u32[]{:S(2)}) copy-start(bf16[1024,128]{1,0:T(8,128)(2,1)} %copy-done.3) | copy-start | bytes 786436
  47.4 1.8 %copy-start.2 = (f32[2,512,512]{2,1,0:T(8,128)S(1)}, f32[2,512,512]{2,1,0:T(8,128)}, u32[]{:S(2)}) copy-start(f32[2,512,512]{2,1,0:T(8,128)} %fusion.71) | copy-start | bytes 6291460
  50.0 1.2 copy-start.14
  50.4 2.9 %copy-start.23 = (bf16[512,6144]{1,0:T(8,128)(2,1)S(1)}, bf16[512,6144]{1,0:T(8,128)(2,1)}, u32[]{:S(2)}) copy-start(bf16[512,6144]{1,0:T(8,128)(2,1)} %param.13) | copy-start | bytes 18874372
  (1 other events, 1.2 us)
Sparse Core Ops, SparseCore 0:
  62.9 79.8 reduce-scatter.1

commit v14 on v9

--- a/solution.py
+++ b/solution.py
@@ -70,7 +70,6 @@
         scale = lax.rsqrt(jnp.mean(out_h * out_h, axis=-1, keepdims=True) + 1e-05)
         normed.append(out_h * scale)
     attn = (jnp.concatenate(normed, axis=1) * gated).astype(jnp.bfloat16)
-    attn = lax.optimization_barrier(attn)
     return lax.psum_scatter(
         jnp.dot(attn, w_out, preferred_element_type=jnp.float32).astype(jnp.bfloat16),
         "tp",

time: 144 us -> 143 us (level)
  no operation moved by 1% of the time
where the time goes in v14:
time: 143 us; the launch traced here: 142 us
  waiting for transfers between devices  86.2 us (60%)
  matrix products  22.9 us (16%)
  between operations  13.7 us (10%)
  starting transfers between devices  9.53 us (7%)
  other arithmetic  6.44 us (5%)
  local copies, waits for them, and re-layouts  3.66 us (3%)
    reduce_scatter x1, waiting for transfers between devices, per_device(): lax.psum_scatter(jnp.dot(attn, w_out, preferred_element_type=jnp.float32)...  79.8 us
    dot_general x1, matrix products, per_device(): jnp.dot(attn, w_out, preferred_element_type=jnp.float32)  9.66 us
    dot_general x4, matrix products, per_device(): jnp.einsum('ntd,nsd->nts', q_h, k_h, preferred_element_type=jnp.float32)  5.7 us
    ppermute x3, starting transfers between devices, exclusive_prefix(): lax.ppermute(row_total.astype(jnp.bfloat16), 'seq', perm)  4.77 us
    ppermute x3, starting transfers between devices, exclusive_prefix(): got = lax.ppermute(sent, 'seq', perm).astype(jnp.float32)  4.76 us
    ppermute x3, waiting for transfers between devices, exclusive_prefix(): lax.ppermute(row_total.astype(jnp.bfloat16), 'seq', perm)  3.54 us
    dot_general x4, matrix products, per_device(): jnp.einsum('nts,nse->nte', scores, v_h.astype(jnp.float32), precision=high)  3.28 us
    unnamed x44, local copies, waits for them, and re-layouts  3.11 us
  transfers between devices with their start and end apart: 7, of which 5 were waited for; matrix products, arithmetic and copies ran while one was open for 5% of the time, Pallas kernels for 0%

profile of v14, /device:TPU:2, one launch (start us, length us, event | category | flops | bytes accessed | tf_op | source)
XLA Modules:
  0.0 142.5 jit_solution(16291202906422324992)
XLA Ops:
  6.5 1.9 %fusion.7 = bf16[1024,512]{1,0:T(8,128)(2,1)S(1)} fusion(bf16[1024,512]{1,0:T(8,128)(2,1)} %param.8), kind=kLoop, calls=%fused_computation.12 | loop fusion | flops 3145728 | bytes 2097152 | tf_op jit(solution)/shard_map/convert_element_type | solution.py:46
  9.2 0.9 fusion.66
  10.1 0.9 fusion.63
  11.0 0.9 fusion.64
  12.0 3.1 %collective-permute-start.2 = (bf16[4,128,128]{2,1,0:T(8,128)(2,1)S(1)}, bf16[4,128,128]{2,1,0:T(8,128)(2,1)S(1)}, u32[]{:S(2)}, u32[]{:S(2)}) collective-permute-start(bf16[4,128,128]{2,1,0:T(8,128)(2,1)S(1)} %pad_maximum_fusion), channel_id=1, source_target_pairs={{0,48},{16,0},{32,16},{48,32},{64,112},{80,64},{96,80},{112,96},{1... | collective-permute-start | bytes 393224 | tf_op jit(solution)/shard_map/ppermute | solution.py:28
  15.1 0.6 collective-permute-start.1
  15.7 1.0 collective-permute-start
  16.8 0.6 fusion.3
  17.6 1.7 %fusion.70 = f32[2,512,512]{2,1,0:T(8,128)} fusion(bf16[2,512,128]{2,1,0:T(8,128)(2,1)S(1)} %bitcast.85, bf16[2,512,128]{2,1,0:T(8,128)(2,1)S(1)} %bitcast.108), kind=kOutput, calls=%fused_computation.99 | convolution fusion | flops 134217728 | bytes 2621440 | tf_op jit(solution)/shard_map/ntd,nsd->nts/dot_general | solution.py:66
  19.3 1.8 %fusion.72 = f32[2,512,512]{2,1,0:T(8,128)} fusion(bf16[2,512,128]{2,1,0:T(8,128)(2,1)S(1)} %bitcast.87, bf16[2,512,128]{2,1,0:T(8,128)(2,1)S(1)} %bitcast.106), kind=kOutput, calls=%fused_computation.101 | convolution fusion | flops 134217728 | bytes 2621440 | tf_op jit(solution)/shard_map/ntd,nsd->nts/dot_general | solution.py:66
  21.1 0.4 fusion.68
  21.5 1.4 %collective-permute-done.1 = bf16[4,128,128]{2,1,0:T(8,128)(2,1)S(1)} collective-permute-done((bf16[4,128,128]{2,1,0:T(8,128)(2,1)S(1)}, bf16[4,128,128]{2,1,0:T(8,128)(2,1)S(1)}, u32[]{:S(2)}, u32[]{:S(2)}) %collective-permute-start.1) | collective-permute-done | bytes 131104 | tf_op jit(solution)/shard_map/ppermute | solution.py:28
  22.9 1.4 collective-permute-done
  24.3 0.7 fusion.49
  25.1 0.5 collective-permute-start.5
  25.6 2.4 %collective-permute-start.4 = (bf16[4,128,128]{2,1,0:T(8,128)(2,1)}, bf16[4,128,128]{2,1,0:T(8,128)(2,1)}, u32[]{:S(2)}, u32[]{:S(2)}) collective-permute-start(bf16[4,128,128]{2,1,0:T(8,128)(2,1)} %fusion.49), channel_id=1, source_target_pairs={{0,128},{16,144},{32,160},{48,176},{64,192},{80,208},{96,224},{112... | collective-permute-start | bytes 393224 | tf_op jit(solution)/shard_map/ppermute | solution.py:34
  28.0 1.8 %collective-permute-start.3 = (bf16[4,128,128]{2,1,0:T(8,128)(2,1)}, bf16[4,128,128]{2,1,0:T(8,128)(2,1)}, u32[]{:S(2)}, u32[]{:S(2)}) collective-permute-start(bf16[4,128,128]{2,1,0:T(8,128)(2,1)} %fusion.49), channel_id=1, source_target_pairs={{0,64},{16,80},{32,96},{48,112},{64,128},{80,144},{96,160},{112,17... | collective-permute-start | bytes 393224 | tf_op jit(solution)/shard_map/ppermute | solution.py:34
  29.8 1.8 %fusion.74 = f32[2,512,512]{2,1,0:T(8,128)} fusion(bf16[2,512,128]{2,1,0:T(8,128)(2,1)S(1)} %bitcast.91, bf16[2,512,128]{2,1,0:T(8,128)(2,1)S(1)} %bitcast.102), kind=kOutput, calls=%fused_computation.103 | convolution fusion | flops 134217728 | bytes 2621440 | tf_op jit(solution)/shard_map/ntd,nsd->nts/dot_general | solution.py:66
  31.7 2.7 %collective-permute-done.4 = bf16[4,128,128]{2,1,0:T(8,128)(2,1)} collective-permute-done((bf16[4,128,128]{2,1,0:T(8,128)(2,1)}, bf16[4,128,128]{2,1,0:T(8,128)(2,1)}, u32[]{:S(2)}, u32[]{:S(2)}) %collective-permute-start.4) | collective-permute-done | bytes 131104 | tf_op jit(solution)/shard_map/ppermute | solution.py:34
  34.4 0.8 collective-permute-done.3
  35.3 1.4 fusion.48
  36.6 1.0 fusion.53
  39.0 0.6 copy-done.1
  39.5 0.8 multiply_reduce_fusion.2
  40.4 0.8 multiply_reduce_fusion.1
  41.3 0.8 multiply_reduce_fusion.3
  42.2 0.7 copy-done.2
  42.9 0.8 multiply_reduce_fusion
  44.4 1.2 copy-done.17
  45.7 0.5 copy-done.18
  46.1 9.7 %convolution_convert_fusion = bf16[1024,6144]{1,0:T(8,128)(2,1)} fusion(bf16[512,6144]{1,0:T(8,128)(2,1)S(1)} %copy-done.17, f32[1024,128]{1,0:T(8,128)S(1)} %get-tuple-element.37, f32[1024,128]{1,0:T(8,128)S(1)} %get-tuple-element.38, f32[1024,128]{1,0:T(8,128)S(1)} %get-tuple-element.39, f32[1024,128]{1,0:T(8,128)S(1)} %get-tuple-element.40, ...), kind=kOutput, calls=%fused_computation | convolution fusion | flops 6453985280 | bytes 22022144 | tf_op jit(solution)/shard_map/dot_general | solution.py:74
  55.8 79.8 %reduce-scatter.2.cloned.1.call-done = bf16[64,6144]{1,0:T(8,128)(2,1)} async-done(((bf16[1024,6144]{1,0:T(8,128)(2,1)}), bf16[64,6144]{1,0:T(8,128)(2,1)}) %reduce-scatter.2.cloned.1.call-update) | async-done | bytes 786448 | tf_op jit(solution)/shard_map/reduce_scatter | solution.py:73
  (64 shorter events, 3.1 us)
Async XLA Ops:
  6.5 2.1 %copy-start.12 = (bf16[1024,512]{1,0:T(8,128)(2,1)S(1)}, bf16[1024,512]{1,0:T(8,128)(2,1)}, u32[]{:S(2)}) copy-start(bf16[1024,512]{1,0:T(8,128)(2,1)} %param.9) | copy-start | bytes 3145732
  6.5 129.1 %reduce-scatter.2.cloned.1.call-start = ((), (), s32[]{:S(2)}) async-start(), calls=%async_computation.1 | async-start | bytes 13369344 | tf_op jit(solution)/shard_map/reduce_scatter | solution.py:73
  8.6 8.1 %copy-start.13 = (bf16[1024,512]{1,0:T(8,128)(2,1)S(1)}, bf16[1024,512]{1,0:T(8,128)(2,1)}, u32[]{:S(2)}) copy-start(bf16[1024,512]{1,0:T(8,128)(2,1)} %param.7) | copy-start | bytes 3145732
  8.8 6.9 %copy-start.3 = (bf16[1024,128]{1,0:T(8,128)(2,1)}, bf16[1024,128]{1,0:T(8,128)(2,1)S(1)}, u32[]{:S(2)}) copy-start(bf16[1024,128]{1,0:T(8,128)(2,1)S(1)} %get-tuple-element.9) | copy-start | bytes 786436
  8.9 6.9 %copy-start.5 = (bf16[1024,128]{1,0:T(8,128)(2,1)}, bf16[1024,128]{1,0:T(8,128)(2,1)S(1)}, u32[]{:S(2)}) copy-start(bf16[1024,128]{1,0:T(8,128)(2,1)S(1)} %get-tuple-element.12) | copy-start | bytes 786436
  8.9 6.8 %copy-start.7 = (bf16[1024,128]{1,0:T(8,128)(2,1)}, bf16[1024,128]{1,0:T(8,128)(2,1)S(1)}, u32[]{:S(2)}) copy-start(bf16[1024,128]{1,0:T(8,128)(2,1)S(1)} %get-tuple-element.10) | copy-start | bytes 786436
  12.0 9.5 %collective-permute-start.2 = (bf16[4,128,128]{2,1,0:T(8,128)(2,1)S(1)}, bf16[4,128,128]{2,1,0:T(8,128)(2,1)S(1)}, u32[]{:S(2)}, u32[]{:S(2)}) collective-permute-start(bf16[4,128,128]{2,1,0:T(8,128)(2,1)S(1)} %pad_maximum_fusion), channel_id=1, source_target_pairs={{0,48},{16,0},{32,16},{48,32},{64,112},{80,64},{96,80},{112,96},{1... | collective-permute-start | bytes 393224 | tf_op jit(solution)/shard_map/ppermute | solution.py:28
  15.1 7.9 %collective-permute-start.1 = (bf16[4,128,128]{2,1,0:T(8,128)(2,1)S(1)}, bf16[4,128,128]{2,1,0:T(8,128)(2,1)S(1)}, u32[]{:S(2)}, u32[]{:S(2)}) collective-permute-start(bf16[4,128,128]{2,1,0:T(8,128)(2,1)S(1)} %pad_maximum_fusion), channel_id=1, source_target_pairs={{0,32},{16,48},{32,0},{48,16},{64,96},{80,112},{96,64},{112,80},{1... | collective-permute-start | bytes 393224 | tf_op jit(solution)/shard_map/ppermute | solution.py:28
  15.7 8.6 %collective-permute-start = (bf16[4,128,128]{2,1,0:T(8,128)(2,1)S(1)}, bf16[4,128,128]{2,1,0:T(8,128)(2,1)S(1)}, u32[]{:S(2)}, u32[]{:S(2)}) collective-permute-start(bf16[4,128,128]{2,1,0:T(8,128)(2,1)S(1)} %pad_maximum_fusion), channel_id=1, source_target_pairs={{0,16},{16,32},{32,48},{48,0},{64,80},{80,96},{96,112},{112,64},{1... | collective-permute-start | bytes 393224 | tf_op jit(solution)/shard_map/ppermute | solution.py:28
  21.5 10.1 %copy-start.14 = (bf16[4,128,128]{2,1,0:T(8,128)(2,1)}, bf16[4,128,128]{2,1,0:T(8,128)(2,1)S(1)}, u32[]{:S(2)}) copy-start(bf16[4,128,128]{2,1,0:T(8,128)(2,1)S(1)} %collective-permute-done.2) | copy-start | bytes 393220
  22.9 8.7 %copy-start.15 = (bf16[4,128,128]{2,1,0:T(8,128)(2,1)}, bf16[4,128,128]{2,1,0:T(8,128)(2,1)S(1)}, u32[]{:S(2)}) copy-start(bf16[4,128,128]{2,1,0:T(8,128)(2,1)S(1)} %collective-permute-done.1) | copy-start | bytes 393220
  24.3 7.3 %copy-start.16 = (bf16[4,128,128]{2,1,0:T(8,128)(2,1)}, bf16[4,128,128]{2,1,0:T(8,128)(2,1)S(1)}, u32[]{:S(2)}) copy-start(bf16[4,128,128]{2,1,0:T(8,128)(2,1)S(1)} %collective-permute-done) | copy-start | bytes 393220
  25.1 6.7 %collective-permute-start.5 = (bf16[4,128,128]{2,1,0:T(8,128)(2,1)}, bf16[4,128,128]{2,1,0:T(8,128)(2,1)}, u32[]{:S(2)}, u32[]{:S(2)}) collective-permute-start(bf16[4,128,128]{2,1,0:T(8,128)(2,1)} %fusion.49), channel_id=1, source_target_pairs={{0,192},{16,208},{32,224},{48,240},{64,0},{80,16},{96,32},{112,48}... | collective-permute-start | bytes 393224 | tf_op jit(solution)/shard_map/ppermute | solution.py:34
  25.6 8.8 %collective-permute-start.4 = (bf16[4,128,128]{2,1,0:T(8,128)(2,1)}, bf16[4,128,128]{2,1,0:T(8,128)(2,1)}, u32[]{:S(2)}, u32[]{:S(2)}) collective-permute-start(bf16[4,128,128]{2,1,0:T(8,128)(2,1)} %fusion.49), channel_id=1, source_target_pairs={{0,128},{16,144},{32,160},{48,176},{64,192},{80,208},{96,224},{112... | collective-permute-start | bytes 393224 | tf_op jit(solution)/shard_map/ppermute | solution.py:34
  28.0 7.2 %collective-permute-start.3 = (bf16[4,128,128]{2,1,0:T(8,128)(2,1)}, bf16[4,128,128]{2,1,0:T(8,128)(2,1)}, u32[]{:S(2)}, u32[]{:S(2)}) collective-permute-start(bf16[4,128,128]{2,1,0:T(8,128)(2,1)} %fusion.49), channel_id=1, source_target_pairs={{0,64},{16,80},{32,96},{48,112},{64,128},{80,144},{96,160},{112,17... | collective-permute-start | bytes 393224 | tf_op jit(solution)/shard_map/ppermute | solution.py:34
  31.6 6.0 %copy-start.11 = (f32[2,128,128]{2,1,0:T(8,128)S(1)}, f32[2,128,128]{2,1,0:T(8,128)}, u32[]{:S(2)}) copy-start(f32[2,128,128]{2,1,0:T(8,128)} %get-tuple-element.22) | copy-start | bytes 393220
  31.6 6.3 %copy-start.9 = (f32[2,128,128]{2,1,0:T(8,128)S(1)}, f32[2,128,128]{2,1,0:T(8,128)}, u32[]{:S(2)}) copy-start(f32[2,128,128]{2,1,0:T(8,128)} %get-tuple-element.28) | copy-start | bytes 393220
  31.7 6.6 %copy-start.10 = (f32[2,128,128]{2,1,0:T(8,128)S(1)}, f32[2,128,128]{2,1,0:T(8,128)}, u32[]{:S(2)}) copy-start(f32[2,128,128]{2,1,0:T(8,128)} %get-tuple-element.24) | copy-start | bytes 393220
  37.9 1.6 %copy-start.1 = (f32[2,512,512]{2,1,0:T(8,128)S(1)}, f32[2,512,512]{2,1,0:T(8,128)}, u32[]{:S(2)}) copy-start(f32[2,512,512]{2,1,0:T(8,128)} %fusion.70) | copy-start | bytes 6291460
  38.0 1.6 %copy-start.8 = (bf16[1024,128]{1,0:T(8,128)(2,1)S(1)}, bf16[1024,128]{1,0:T(8,128)(2,1)}, u32[]{:S(2)}) copy-start(bf16[1024,128]{1,0:T(8,128)(2,1)} %copy-done.7) | copy-start | bytes 786436
  38.7 1.8 %copy-start = (f32[2,512,512]{2,1,0:T(8,128)S(1)}, f32[2,512,512]{2,1,0:T(8,128)}, u32[]{:S(2)}) copy-start(f32[2,512,512]{2,1,0:T(8,128)} %fusion.72) | copy-start | bytes 6291460
  38.7 1.8 %copy-start.6 = (bf16[1024,128]{1,0:T(8,128)(2,1)S(1)}, bf16[1024,128]{1,0:T(8,128)(2,1)}, u32[]{:S(2)}) copy-start(bf16[1024,128]{1,0:T(8,128)(2,1)} %copy-done.5) | copy-start | bytes 786436
  40.4 1.0 copy-start.4
  41.3 1.6 %copy-start.2 = (f32[2,512,512]{2,1,0:T(8,128)S(1)}, f32[2,512,512]{2,1,0:T(8,128)}, u32[]{:S(2)}) copy-start(f32[2,512,512]{2,1,0:T(8,128)} %fusion.74) | copy-start | bytes 6291460
  42.9 2.8 %copy-start.17 = (bf16[512,6144]{1,0:T(8,128)(2,1)S(1)}, bf16[512,6144]{1,0:T(8,128)(2,1)}, u32[]{:S(2)}) copy-start(bf16[512,6144]{1,0:T(8,128)(2,1)} %param.13) | copy-start | bytes 18874372
  43.7 2.4 %copy-start.18 = (bf16[1024,512]{1,0:T(8,128)(2,1)S(1)}, bf16[1024,512]{1,0:T(8,128)(2,1)}, u32[]{:S(2)}) copy-start(bf16[1024,512]{1,0:T(8,128)(2,1)} %param.10) | copy-start | bytes 3145732
  43.7 2.4 %copy-start.19 = (f32[512]{0:T(512)S(1)}, f32[512]{0:T(512)}, u32[]{:S(2)}) copy-start(f32[512]{0:T(512)} %param.12) | copy-start | bytes 6148
Sparse Core Ops, SparseCore 0:
  55.9 79.6 reduce-scatter.1

commit v15 on v10

--- a/solution.py
+++ b/solution.py
@@ -73,7 +73,6 @@
         scale = lax.rsqrt(jnp.mean(out_h * out_h, axis=-1, keepdims=True) + 1e-05)
         normed.append(out_h * scale)
     attn = (jnp.concatenate(normed, axis=1) * gated).astype(jnp.bfloat16)
-    attn = lax.optimization_barrier(attn)
     return lax.psum_scatter(
         jnp.dot(attn, w_out, preferred_element_type=jnp.float32).astype(jnp.bfloat16),
         "tp",

time: 147 us -> 143 us (0.973)
  matrix products: 24.4 us -> 21.6 us
    dot_general x1, matrix products: 12.5 us -> 9.69 us  [per_device(): jnp.dot(attn, w_out, preferred_element_type=jnp.float32)]
where the time goes in v15:
time: 143 us
  waiting for transfers between devices  85 us (59%)
  matrix products  21.6 us (15%)
  between operations  13.8 us (10%)
  other arithmetic  10.9 us (8%)
  starting transfers between devices  9.45 us (7%)
  local copies, waits for them, and re-layouts  2.37 us (2%)
    reduce_scatter x1, waiting for transfers between devices, per_device(): lax.psum_scatter(jnp.dot(attn, w_out, preferred_element_type=jnp.float32)...  79.8 us
    dot_general x1, matrix products, per_device(): jnp.dot(attn, w_out, preferred_element_type=jnp.float32)  9.69 us
    dot_general x4, matrix products, per_device(): jnp.einsum('ntd,nsd->nts', q_h, k_h, preferred_element_type=jnp.float32)  5.7 us
    ppermute x3, starting transfers between devices, exclusive_prefix(): lax.ppermute(row_total.astype(jnp.bfloat16), 'seq', perm)  4.76 us
    ppermute x3, starting transfers between devices, exclusive_prefix(): got = lax.ppermute(sent, 'seq', perm).astype(jnp.float32)  4.69 us
    another operation x4, other arithmetic, per_device(): jnp.cumsum(block_states[h], axis=0) - block_states[h]  4.53 us
    ppermute x3, waiting for transfers between devices, exclusive_prefix(): lax.ppermute(row_total.astype(jnp.bfloat16), 'seq', perm)  4.26 us
    dot_general x4, matrix products, per_device(): jnp.einsum('nts,nse->nte', scores, v_h.astype(jnp.float32), precision=high)  3.3 us
  transfers between devices with their start and end apart: 7, of which 4 were waited for; matrix products, arithmetic and copies ran while one was open for 5% of the time, Pallas kernels for 0%

profile of v15, /device:TPU:2, one launch (start us, length us, event | category | flops | bytes accessed | tf_op | source)
XLA Modules:
  0.0 143.1 jit_solution(2847404846788188894)
XLA Ops:
  6.5 1.9 %fusion.7 = bf16[1024,512]{1,0:T(8,128)(2,1)S(1)} fusion(bf16[1024,512]{1,0:T(8,128)(2,1)} %param.8), kind=kLoop, calls=%fused_computation.12 | loop fusion | flops 3145728 | bytes 2097152 | tf_op jit(solution)/shard_map/convert_element_type | solution.py:46
  8.5 0.8 fusion.67
  9.3 3.1 %collective-permute-start.2 = (bf16[4,128,128]{2,1,0:T(8,128)(2,1)S(1)}, bf16[4,128,128]{2,1,0:T(8,128)(2,1)S(1)}, u32[]{:S(2)}, u32[]{:S(2)}) collective-permute-start(bf16[4,128,128]{2,1,0:T(8,128)(2,1)S(1)} %pad_maximum_fusion), channel_id=1, source_target_pairs={{0,48},{16,0},{32,16},{48,32},{64,112},{80,64},{96,80},{112,96},{1... | collective-permute-start | bytes 393224 | tf_op jit(solution)/shard_map/ppermute | solution.py:28
  12.4 0.6 collective-permute-start.1
  13.0 1.0 collective-permute-start
  14.2 0.6 fusion.3
  15.0 1.8 %fusion.75 = f32[2,512,512]{2,1,0:T(8,128)} fusion(bf16[2,512,128]{2,1,0:T(8,128)(2,1)S(1)} %bitcast.83, bf16[2,512,128]{2,1,0:T(8,128)(2,1)S(1)} %bitcast.94), kind=kOutput, calls=%fused_computation.108 | convolution fusion | flops 134217728 | bytes 2621440 | tf_op jit(solution)/shard_map/ntd,nsd->nts/dot_general | solution.py:69
  16.8 1.8 %fusion.69 = f32[2,512,512]{2,1,0:T(8,128)} fusion(bf16[2,512,128]{2,1,0:T(8,128)(2,1)S(1)} %bitcast.85, bf16[2,512,128]{2,1,0:T(8,128)(2,1)S(1)} %bitcast.93), kind=kOutput, calls=%fused_computation.102 | convolution fusion | flops 134217728 | bytes 2621440 | tf_op jit(solution)/shard_map/ntd,nsd->nts/dot_general | solution.py:69
  18.6 1.7 %fusion.73 = f32[2,512,512]{2,1,0:T(8,128)} fusion(bf16[2,512,128]{2,1,0:T(8,128)(2,1)S(1)} %bitcast.79, bf16[2,512,128]{2,1,0:T(8,128)(2,1)S(1)} %bitcast.92), kind=kOutput, calls=%fused_computation.106 | convolution fusion | flops 134217728 | bytes 2621440 | tf_op jit(solution)/shard_map/ntd,nsd->nts/dot_general | solution.py:69
  20.3 0.4 fusion.71
  20.8 0.9 collective-permute-done
  21.7 0.7 fusion.49
  22.4 0.5 collective-permute-start.5
  22.9 2.4 %collective-permute-start.4 = (bf16[4,128,128]{2,1,0:T(8,128)(2,1)}, bf16[4,128,128]{2,1,0:T(8,128)(2,1)}, u32[]{:S(2)}, u32[]{:S(2)}) collective-permute-start(bf16[4,128,128]{2,1,0:T(8,128)(2,1)} %fusion.49), channel_id=1, source_target_pairs={{0,128},{16,144},{32,160},{48,176},{64,192},{80,208},{96,224},{112... | collective-permute-start | bytes 393224 | tf_op jit(solution)/shard_map/ppermute | solution.py:34
  25.4 1.8 %collective-permute-start.3 = (bf16[4,128,128]{2,1,0:T(8,128)(2,1)}, bf16[4,128,128]{2,1,0:T(8,128)(2,1)}, u32[]{:S(2)}, u32[]{:S(2)}) collective-permute-start(bf16[4,128,128]{2,1,0:T(8,128)(2,1)} %fusion.49), channel_id=1, source_target_pairs={{0,64},{16,80},{32,96},{48,112},{64,128},{80,144},{96,160},{112,17... | collective-permute-start | bytes 393224 | tf_op jit(solution)/shard_map/ppermute | solution.py:34
  27.2 1.1 fusion.65
  28.4 3.4 %collective-permute-done.4 = bf16[4,128,128]{2,1,0:T(8,128)(2,1)} collective-permute-done((bf16[4,128,128]{2,1,0:T(8,128)(2,1)}, bf16[4,128,128]{2,1,0:T(8,128)(2,1)}, u32[]{:S(2)}, u32[]{:S(2)}) %collective-permute-start.4) | collective-permute-done | bytes 131104 | tf_op jit(solution)/shard_map/ppermute | solution.py:34
  31.8 0.9 collective-permute-done.3
  32.7 1.3 fusion.48
  34.0 1.0 fusion.57
  35.0 1.1 fusion.32
  36.1 1.2 fusion.68
  37.4 0.8 multiply_reduce_fusion.3
  38.2 1.1 fusion.29
  39.7 0.8 multiply_reduce_fusion
  40.5 1.2 fusion.30
  41.8 1.1 fusion.31
  43.5 0.8 multiply_reduce_fusion.1
  44.4 0.8 multiply_reduce_fusion.2
  45.9 0.6 slice-done.1
  46.7 9.7 %convolution_convert_fusion = bf16[1024,6144]{1,0:T(8,128)(2,1)} fusion(bf16[512,6144]{1,0:T(8,128)(2,1)S(1)} %bitcast.108, f32[1024,128]{1,0:T(8,128)S(1)} %get-tuple-element.33, f32[1024,128]{1,0:T(8,128)S(1)} %get-tuple-element.34, f32[1024,128]{1,0:T(8,128)S(1)} %get-tuple-element.35, f32[1024,128]{1,0:T(8,128)S(1)} %get-tuple-element.36, ...), kind=kOutput, calls=%fused_computation | convolution fusion | flops 6453985280 | bytes 22022144 | tf_op jit(solution)/shard_map/dot_general | solution.py:77
  56.5 79.8 %reduce-scatter.2.cloned.1.call-done = bf16[64,6144]{1,0:T(8,128)(2,1)} async-done(((bf16[1024,6144]{1,0:T(8,128)(2,1)}), bf16[64,6144]{1,0:T(8,128)(2,1)}) %reduce-scatter.2.cloned.1.call-update) | async-done | bytes 786448 | tf_op jit(solution)/shard_map/reduce_scatter | solution.py:76
  (65 shorter events, 2.4 us)
Async XLA Ops:
  6.5 1.9 %copy-start.4 = (bf16[1024,512]{1,0:T(8,128)(2,1)S(1)}, bf16[1024,512]{1,0:T(8,128)(2,1)}, u32[]{:S(2)}) copy-start(bf16[1024,512]{1,0:T(8,128)(2,1)} %param.9) | copy-start | bytes 3145732
  6.5 129.7 %reduce-scatter.2.cloned.1.call-start = ((), (), s32[]{:S(2)}) async-start(), calls=%async_computation.1 | async-start | bytes 13369344 | tf_op jit(solution)/shard_map/reduce_scatter | solution.py:76
  9.2 5.6 %copy-start.3 = (f32[2,512,512]{2,1,0:T(8,128)}, f32[2,512,512]{2,1,0:T(8,128)S(1)}, u32[]{:S(2)}) copy-start(f32[2,512,512]{2,1,0:T(8,128)S(1)} %fusion.67) | copy-start | bytes 6291460
  9.2 5.0 %copy-start.10 = (bf16[1024,512]{1,0:T(8,128)(2,1)S(1)}, bf16[1024,512]{1,0:T(8,128)(2,1)}, u32[]{:S(2)}) copy-start(bf16[1024,512]{1,0:T(8,128)(2,1)} %param.7) | copy-start | bytes 3145732
  9.3 11.4 %collective-permute-start.2 = (bf16[4,128,128]{2,1,0:T(8,128)(2,1)S(1)}, bf16[4,128,128]{2,1,0:T(8,128)(2,1)S(1)}, u32[]{:S(2)}, u32[]{:S(2)}) collective-permute-start(bf16[4,128,128]{2,1,0:T(8,128)(2,1)S(1)} %pad_maximum_fusion), channel_id=1, source_target_pairs={{0,48},{16,0},{32,16},{48,32},{64,112},{80,64},{96,80},{112,96},{1... | collective-permute-start | bytes 393224 | tf_op jit(solution)/shard_map/ppermute | solution.py:28
  12.4 8.4 %collective-permute-start.1 = (bf16[4,128,128]{2,1,0:T(8,128)(2,1)S(1)}, bf16[4,128,128]{2,1,0:T(8,128)(2,1)S(1)}, u32[]{:S(2)}, u32[]{:S(2)}) collective-permute-start(bf16[4,128,128]{2,1,0:T(8,128)(2,1)S(1)} %pad_maximum_fusion), channel_id=1, source_target_pairs={{0,32},{16,48},{32,0},{48,16},{64,96},{80,112},{96,64},{112,80},{1... | collective-permute-start | bytes 393224 | tf_op jit(solution)/shard_map/ppermute | solution.py:28
  13.0 8.6 %collective-permute-start = (bf16[4,128,128]{2,1,0:T(8,128)(2,1)S(1)}, bf16[4,128,128]{2,1,0:T(8,128)(2,1)S(1)}, u32[]{:S(2)}, u32[]{:S(2)}) collective-permute-start(bf16[4,128,128]{2,1,0:T(8,128)(2,1)S(1)} %pad_maximum_fusion), channel_id=1, source_target_pairs={{0,16},{16,32},{32,48},{48,0},{64,80},{80,96},{96,112},{112,64},{1... | collective-permute-start | bytes 393224 | tf_op jit(solution)/shard_map/ppermute | solution.py:28
  15.0 3.6 %copy-start.7 = (bf16[1024,128]{1,0:T(8,128)(2,1)}, bf16[1024,128]{1,0:T(8,128)(2,1)S(1)}, u32[]{:S(2)}) copy-start(bf16[1024,128]{1,0:T(8,128)(2,1)S(1)} %get-tuple-element.18) | copy-start | bytes 786436
  15.0 3.6 %copy-start.9 = (bf16[1024,128]{1,0:T(8,128)(2,1)}, bf16[1024,128]{1,0:T(8,128)(2,1)S(1)}, u32[]{:S(2)}) copy-start(bf16[1024,128]{1,0:T(8,128)(2,1)S(1)} %get-tuple-element.17) | copy-start | bytes 786436
  15.0 5.3 %copy-start.5 = (bf16[1024,128]{1,0:T(8,128)(2,1)}, bf16[1024,128]{1,0:T(8,128)(2,1)S(1)}, u32[]{:S(2)}) copy-start(bf16[1024,128]{1,0:T(8,128)(2,1)S(1)} %get-tuple-element.20) | copy-start | bytes 786436
  20.8 7.5 %copy-start.15 = (bf16[4,128,128]{2,1,0:T(8,128)(2,1)}, bf16[4,128,128]{2,1,0:T(8,128)(2,1)S(1)}, u32[]{:S(2)}) copy-start(bf16[4,128,128]{2,1,0:T(8,128)(2,1)S(1)} %collective-permute-done.1) | copy-start | bytes 393220
  21.7 6.6 %copy-start.16 = (bf16[4,128,128]{2,1,0:T(8,128)(2,1)}, bf16[4,128,128]{2,1,0:T(8,128)(2,1)S(1)}, u32[]{:S(2)}) copy-start(bf16[4,128,128]{2,1,0:T(8,128)(2,1)S(1)} %collective-permute-done) | copy-start | bytes 393220
  22.4 6.0 %collective-permute-start.5 = (bf16[4,128,128]{2,1,0:T(8,128)(2,1)}, bf16[4,128,128]{2,1,0:T(8,128)(2,1)}, u32[]{:S(2)}, u32[]{:S(2)}) collective-permute-start(bf16[4,128,128]{2,1,0:T(8,128)(2,1)} %fusion.49), channel_id=1, source_target_pairs={{0,192},{16,208},{32,224},{48,240},{64,0},{80,16},{96,32},{112,48}... | collective-permute-start | bytes 393224 | tf_op jit(solution)/shard_map/ppermute | solution.py:34
  22.9 8.9 %collective-permute-start.4 = (bf16[4,128,128]{2,1,0:T(8,128)(2,1)}, bf16[4,128,128]{2,1,0:T(8,128)(2,1)}, u32[]{:S(2)}, u32[]{:S(2)}) collective-permute-start(bf16[4,128,128]{2,1,0:T(8,128)(2,1)} %fusion.49), channel_id=1, source_target_pairs={{0,128},{16,144},{32,160},{48,176},{64,192},{80,208},{96,224},{112... | collective-permute-start | bytes 393224 | tf_op jit(solution)/shard_map/ppermute | solution.py:34
  25.4 7.3 %collective-permute-start.3 = (bf16[4,128,128]{2,1,0:T(8,128)(2,1)}, bf16[4,128,128]{2,1,0:T(8,128)(2,1)}, u32[]{:S(2)}, u32[]{:S(2)}) collective-permute-start(bf16[4,128,128]{2,1,0:T(8,128)(2,1)} %fusion.49), channel_id=1, source_target_pairs={{0,64},{16,80},{32,96},{48,112},{64,128},{80,144},{96,160},{112,17... | collective-permute-start | bytes 393224 | tf_op jit(solution)/shard_map/ppermute | solution.py:34
  28.3 9.1 %copy-start.14 = (bf16[1024,128]{1,0:T(8,128)(2,1)S(1)}, bf16[1024,128]{1,0:T(8,128)(2,1)}, u32[]{:S(2)}) copy-start(bf16[1024,128]{1,0:T(8,128)(2,1)} %get-tuple-element.13) | copy-start | bytes 786436
  28.3 9.0 %copy-start.2 = (f32[2,512,512]{2,1,0:T(8,128)S(1)}, f32[2,512,512]{2,1,0:T(8,128)}, u32[]{:S(2)}) copy-start(f32[2,512,512]{2,1,0:T(8,128)} %fusion.69) | copy-start | bytes 6291460
  37.3 2.0 %copy-start.8 = (bf16[1024,128]{1,0:T(8,128)(2,1)S(1)}, bf16[1024,128]{1,0:T(8,128)(2,1)}, u32[]{:S(2)}) copy-start(bf16[1024,128]{1,0:T(8,128)(2,1)} %copy-done.7) | copy-start | bytes 786436
  37.3 2.3 %copy-start.1 = (f32[2,512,512]{2,1,0:T(8,128)S(1)}, f32[2,512,512]{2,1,0:T(8,128)}, u32[]{:S(2)}) copy-start(f32[2,512,512]{2,1,0:T(8,128)} %fusion.75) | copy-start | bytes 6291460
  37.3 2.3 %copy-start.13 = (bf16[1024,128]{1,0:T(8,128)(2,1)S(1)}, bf16[1024,128]{1,0:T(8,128)(2,1)}, u32[]{:S(2)}) copy-start(bf16[1024,128]{1,0:T(8,128)(2,1)} %get-tuple-element.15) | copy-start | bytes 786436
  39.7 3.2 %copy-start.6 = (bf16[1024,128]{1,0:T(8,128)(2,1)S(1)}, bf16[1024,128]{1,0:T(8,128)(2,1)}, u32[]{:S(2)}) copy-start(bf16[1024,128]{1,0:T(8,128)(2,1)} %copy-done.5) | copy-start | bytes 786436
  40.5 3.0 %copy-start = (f32[2,512,512]{2,1,0:T(8,128)S(1)}, f32[2,512,512]{2,1,0:T(8,128)}, u32[]{:S(2)}) copy-start(f32[2,512,512]{2,1,0:T(8,128)} %fusion.73) | copy-start | bytes 6291460
  40.5 3.0 %copy-start.12 = (bf16[1024,128]{1,0:T(8,128)(2,1)S(1)}, bf16[1024,128]{1,0:T(8,128)(2,1)}, u32[]{:S(2)}) copy-start(bf16[1024,128]{1,0:T(8,128)(2,1)} %get-tuple-element.16) | copy-start | bytes 786436
  43.2 1.2 copy-start.11
  43.5 2.4 %slice-start = ((s8[6291456]{0:T(1024)(128)(4,1)}), s8[4194304]{0:T(1024)(128)(4,1)S(1)}, s32[]{:S(2)}) async-start(s8[6291456]{0:T(1024)(128)(4,1)} %bitcast.107), calls=%async_computation.2 | async-start | bytes 8388608
  44.4 2.2 %slice-start.1 = ((s8[6291456]{0:T(1024)(128)(4,1)}), s8[2097152]{0:T(1024)(128)(4,1)S(1)}, s32[]{:S(2)}) async-start(s8[6291456]{0:T(1024)(128)(4,1)} %bitcast.107), calls=%async_computation.3 | async-start | bytes 4194304
  45.2 1.5 %copy-start.17 = (bf16[1024,512]{1,0:T(8,128)(2,1)S(1)}, bf16[1024,512]{1,0:T(8,128)(2,1)}, u32[]{:S(2)}) copy-start(bf16[1024,512]{1,0:T(8,128)(2,1)} %param.10) | copy-start | bytes 3145732
  45.2 1.5 %copy-start.18 = (f32[512]{0:T(512)S(1)}, f32[512]{0:T(512)}, u32[]{:S(2)}) copy-start(f32[512]{0:T(512)} %param.12) | copy-start | bytes 6148
Sparse Core Ops, SparseCore 0:
  56.6 79.6 reduce-scatter.1
